TPU v7x, 32 devices: a whole 2x2x4 slice. The times are simulated.
32 devices in a mesh: gx: 8 (over z, y), gy: 4 (over x, core).
Axes of the slice: x: 2, y: 2, z: 4, core: 2. Of those that a mesh axis runs over, the one named last changes fastest.
Arguments:
- start_panel: float32 [16, 64, 128, 128], P(None, 'gx', 'gy'), may hold values from -6 to 6
- ocean_mask: int32 [64, 128, 128], P('gx', 'gy'), may hold values from 0 to 1, as said below
- conduct_x: float32 [64, 128, 128], P('gx', 'gy'), may hold values from 0.3 to 3
- conduct_y: float32 [64, 128, 128], P('gx', 'gy'), may hold values from 0.3 to 3
- conduct_z: float32 [64, 128, 128], P('gx', 'gy'), may hold values from 0.3 to 3
- diag_shift: float32 [64, 128, 128], P('gx', 'gy'), may hold values from 0.5 to 2
Outputs:
- basis_out: float32 [16, 64, 128, 128], P(None, 'gx', 'gy')
- ritz_residual: float32 [16, 64, 128, 128], P(None, 'gx', 'gy')
Inputs may be any that keep to these rules, and one draw needn't show every extreme that they name: `ocean_mask`: 1 marks an ocean cell; the share of ocean cells falls along the first dimension from about 0.9 to about 0.2.
All inputs are finite; a program needn't handle non-finite values.
Results may differ from a plain program's by a relative error of at most 0.0003.
Values sent between devices are 32-bit elements; how exact they have to be, the bound alone decides.
No kernel may reach another device: no remote copies, remote signals or barrier semaphores. Data moves between devices by JAX's collectives and lax.ppermute only.
A program may use at most 64 MiB of HBM per device.

v0:
```python
import jax
import jax.numpy as jnp
from jax import lax
from jax.sharding import PartitionSpec as P

FILTER_STEPS = 2


FILTER_CENTRE = 22.0
FILTER_HALF = 18.0
FILTER_NORM = 2.0 * (22.0 / 18.0) * (22.0 / 18.0) - 1.0


def halo_pair(block, axis, dim):
    count = lax.axis_size(axis)
    forward = [(i, i + 1) for i in range(count - 1)]
    backward = [(target, source) for source, target in forward]
    low = lax.ppermute(lax.slice_in_dim(block, block.shape[dim] - 1, None, axis=dim), axis, forward)
    high = lax.ppermute(lax.slice_in_dim(block, 0, 1, axis=dim), axis, backward)
    return low, high


def padded_2(block, sides, width):
    (axis_a, dim_a), (axis_b, dim_b) = sides
    low_a, high_a = halo_pair(block, axis_a, dim_a)
    low_b, high_b = halo_pair(block, axis_b, dim_b)
    block = jnp.concatenate([low_a, block, high_a], axis=dim_a)
    edge = [(0, 0)] * block.ndim
    edge[dim_a] = (1, 1)
    low_b = jnp.pad(low_b, edge)
    high_b = jnp.pad(high_b, edge)
    return jnp.concatenate([low_b, block, high_b], axis=dim_b)


def stencil(values, fields):
    wet_mask = fields[0]
    along_x = fields[1]
    along_y = fields[2]
    along_z = fields[3]
    diag_term = fields[4]
    inner_wet = wet_mask[1:-1, 1:-1]
    face_x = along_x[:-1, 1:-1] * wet_mask[:-1, 1:-1] * wet_mask[1:, 1:-1]
    flow_x = face_x * (values[..., 1:, 1:-1, :] - values[..., :-1, 1:-1, :])
    face_y = along_y[1:-1, :-1] * wet_mask[1:-1, :-1] * wet_mask[1:-1, 1:]
    flow_y = face_y * (values[..., 1:-1, 1:, :] - values[..., 1:-1, :-1, :])
    centre = values[..., 1:-1, 1:-1, :]
    face_z = along_z[1:-1, 1:-1, :-1] * inner_wet[:, :, :-1] * inner_wet[:, :, 1:]
    flow_z = face_z * (centre[..., 1:] - centre[..., :-1])
    edges = [(0, 0)] * (centre.ndim - 1)
    net_z = jnp.pad(flow_z, edges + [(1, 0)]) - jnp.pad(flow_z, edges + [(0, 1)])
    net_x = flow_x[..., :-1, :, :] - flow_x[..., 1:, :, :]
    net_y = flow_y[..., :-1, :] - flow_y[..., 1:, :]
    return inner_wet * (diag_term[1:-1, 1:-1] * centre + net_x + net_y + net_z)


def operate(block, fields_one):
    padded = padded_2(block, (("gx", 1), ("gy", 2)), 1)
    return stencil(padded, fields_one)


def reduce_all(value):
    for axis in ("gy", "gx"):
        count = lax.axis_size(axis)
        assert count & (count - 1) == 0
        step = 1
        while step < count:
            pairs = [(i, i ^ step) for i in range(count)]
            value = value + lax.ppermute(value, axis, pairs)
            step *= 2
    return value


def inner_products(left, right):
    return jnp.einsum("kc,lc->kl", left, right, precision=lax.Precision.HIGHEST)


def combine(matrix, rows):
    return jnp.einsum("kl,lc->kc", matrix, rows, precision=lax.Precision.HIGHEST)


def triangle_inverse(gram_sum, vectors):
    factor = jnp.linalg.cholesky(gram_sum)
    return lax.linalg.triangular_solve(
        factor, jnp.eye(vectors, dtype=jnp.float32), left_side=True, lower=True
    )


def on_device(start_panel, ocean_mask, conduct_x, conduct_y, conduct_z, diag_shift):
    ocean_cells = ocean_mask.astype(jnp.float32)
    vectors = start_panel.shape[0]
    cell_total = (
        start_panel.shape[1]
        * start_panel.shape[2]
        * start_panel.shape[3]
        * lax.axis_size("gx")
        * lax.axis_size("gy")
    )
    field = start_panel * ocean_cells[None]
    fields = jnp.stack([ocean_cells, conduct_x, conduct_y, conduct_z, diag_shift])
    rows, cols = field.shape[1], field.shape[2]
    edges = [
        jnp.concatenate([part[:, a:b] for part in (field, fields)])
        for a, b in ((rows - 1, rows), (0, 1))
    ] + [
        jnp.concatenate([part[:, :, a:b] for part in (field, fields)])
        for a, b in ((cols - 1, cols), (0, 1))
    ]
    halos = []
    for axis, (to_high, to_low) in (("gx", edges[0:2]), ("gy", edges[2:4])):
        count = lax.axis_size(axis)
        forward = [(i, i + 1) for i in range(count - 1)]
        backward = [(target, source) for source, target in forward]
        halos += [lax.ppermute(to_high, axis, forward), lax.ppermute(to_low, axis, backward)]

    def assemble(block, part):
        low_x, high_x, low_y, high_y = (halo[part] for halo in halos)
        block = jnp.concatenate([low_x, block, high_x], axis=1)
        edge = ((0, 0), (1, 1), (0, 0), (0, 0))
        return jnp.concatenate([jnp.pad(low_y, edge), block, jnp.pad(high_y, edge)], axis=2)

    fields_one = assemble(fields, slice(vectors, None))
    together = assemble(field, slice(0, vectors))
    first = True
    for repeat in range(FILTER_STEPS):
        if first:
            applied = stencil(together, fields_one)
            first = False
        else:
            applied = operate(field, fields_one)
        middle = (applied - FILTER_CENTRE * field) / FILTER_HALF
        field = (
            2.0 * (operate(middle, fields_one) - FILTER_CENTRE * middle) / FILTER_HALF - field
        ) / FILTER_NORM
    flattened = field.reshape(vectors, -1)
    gram_sum = reduce_all(inner_products(flattened, flattened)) / cell_total
    inverse = triangle_inverse(gram_sum, vectors)
    basis_rows = combine(inverse, flattened)
    raw_images = operate(field, fields_one).reshape(vectors, -1)
    mixed_sum = reduce_all(inner_products(flattened, raw_images)) / cell_total
    projected = jnp.einsum(
        "ka,ab,lb->kl", inverse, mixed_sum, inverse, precision=lax.Precision.HIGHEST
    )
    residual = combine(inverse, raw_images) - combine(projected, basis_rows)
    return (basis_rows.reshape(field.shape), residual.reshape(field.shape))


def solution(mesh):
    placed = (
        P(None, "gx", "gy", None),
        P("gx", "gy", None),
        P("gx", "gy", None),
        P("gx", "gy", None),
        P("gx", "gy", None),
        P("gx", "gy", None),
    )
    return jax.shard_map(
        on_device,
        mesh=mesh,
        in_specs=placed,
        out_specs=(P(None, "gx", "gy", None), P(None, "gx", "gy", None)),
        check_vma=False,
    )
```

profile of v0, /device:TPU:0, one launch (start us, length us, event | category | flops | bytes accessed | tf_op | source)
XLA Modules:
  0.0 152.9 jit_solution(4217526851562052232)
XLA Ops:
  4.7 4.9 %collective-permute-start.1 = (f32[21,1,32,128]{3,2,1,0:T(8,128)S(1)}, f32[21,1,32,128]{3,2,1,0:T(8,128)S(1)}, u32[]{:S(2)}, u32[]{:S(2)}) collective-permute-start(f32[21,1,32,128]{3,2,1,0:T(8,128)S(1)} %pad_maximum_fusion.20), channel_id=1, source_target_pairs={{0,4},{4,8},{8,12},{12,16},{16,20},{20,24},{24,28},{1,5},{5,9},{9,... | collective-permute-start | bytes 1032200 | tf_op jit(solution)/shard_map/ppermute | solution.py:113
  12.5 3.0 %collective-permute-start = (f32[21,8,1,128]{3,2,1,0:T(1,128)S(1)}, f32[21,8,1,128]{3,2,1,0:T(1,128)S(1)}, u32[]{:S(2)}, u32[]{:S(2)}) collective-permute-start(f32[21,8,1,128]{3,2,1,0:T(1,128)S(1)} %pad_maximum_fusion.22), channel_id=1, source_target_pairs={{0,1},{1,2},{2,3},{4,5},{5,6},{6,7},{8,9},{9,10},{10,11},{12,13},{... | collective-permute-start | bytes 258056 | tf_op jit(solution)/shard_map/ppermute | solution.py:113
  16.5 7.8 %collective-permute-done.1 = f32[21,1,32,128]{3,2,1,0:T(8,128)S(1)} collective-permute-done((f32[21,1,32,128]{3,2,1,0:T(8,128)S(1)}, f32[21,1,32,128]{3,2,1,0:T(8,128)S(1)}, u32[]{:S(2)}, u32[]{:S(2)}) %collective-permute-start.1) | collective-permute-done | bytes 344096 | tf_op jit(solution)/shard_map/ppermute | solution.py:113
  30.8 5.0 %collective-permute-start.5 = (f32[16,1,32,128]{3,2,1,0:T(8,128)S(1)}, f32[16,1,32,128]{3,2,1,0:T(8,128)S(1)}, u32[]{:S(2)}, u32[]{:S(2)}) collective-permute-start(f32[16,1,32,128]{3,2,1,0:T(8,128)S(1)} %get-tuple-element.24), channel_id=1, source_target_pairs={{0,4},{4,8},{8,12},{12,16},{16,20},{20,24},{24,28},{1,5},{5,9},{9,... | collective-permute-start | bytes 786440 | tf_op jit(solution)/shard_map/ppermute | solution.py:18
  37.1 3.0 %collective-permute-start.7 = (f32[16,8,1,128]{3,2,1,0:T(1,128)S(1)}, f32[16,8,1,128]{3,2,1,0:T(1,128)S(1)}, u32[]{:S(2)}, u32[]{:S(2)}) collective-permute-start(f32[16,8,1,128]{3,2,1,0:T(1,128)S(1)} %get-tuple-element.23), channel_id=1, source_target_pairs={{0,1},{1,2},{2,3},{4,5},{5,6},{6,7},{8,9},{9,10},{10,11},{12,13},{... | collective-permute-start | bytes 196616 | tf_op jit(solution)/shard_map/ppermute | solution.py:18
  40.8 5.1 %collective-permute-done.5 = f32[16,1,32,128]{3,2,1,0:T(8,128)S(1)} collective-permute-done((f32[16,1,32,128]{3,2,1,0:T(8,128)S(1)}, f32[16,1,32,128]{3,2,1,0:T(8,128)S(1)}, u32[]{:S(2)}, u32[]{:S(2)}) %collective-permute-start.5) | collective-permute-done | bytes 262176 | tf_op jit(solution)/shard_map/ppermute | solution.py:18
  50.4 5.0 %collective-permute-start.9 = (f32[16,1,32,128]{3,2,1,0:T(8,128)S(1)}, f32[16,1,32,128]{3,2,1,0:T(8,128)S(1)}, u32[]{:S(2)}, u32[]{:S(2)}) collective-permute-start(f32[16,1,32,128]{3,2,1,0:T(8,128)S(1)} %get-tuple-element.20), channel_id=1, source_target_pairs={{0,4},{4,8},{8,12},{12,16},{16,20},{20,24},{24,28},{1,5},{5,9},{9,... | collective-permute-start | bytes 786440 | tf_op jit(solution)/shard_map/ppermute | solution.py:18
  56.7 3.0 %collective-permute-start.11 = (f32[16,8,1,128]{3,2,1,0:T(1,128)S(1)}, f32[16,8,1,128]{3,2,1,0:T(1,128)S(1)}, u32[]{:S(2)}, u32[]{:S(2)}) collective-permute-start(f32[16,8,1,128]{3,2,1,0:T(1,128)S(1)} %get-tuple-element.19), channel_id=1, source_target_pairs={{0,1},{1,2},{2,3},{4,5},{5,6},{6,7},{8,9},{9,10},{10,11},{12,13},{... | collective-permute-start | bytes 196616 | tf_op jit(solution)/shard_map/ppermute | solution.py:18
  60.4 5.3 %collective-permute-done.9 = f32[16,1,32,128]{3,2,1,0:T(8,128)S(1)} collective-permute-done((f32[16,1,32,128]{3,2,1,0:T(8,128)S(1)}, f32[16,1,32,128]{3,2,1,0:T(8,128)S(1)}, u32[]{:S(2)}, u32[]{:S(2)}) %collective-permute-start.9) | collective-permute-done | bytes 262176 | tf_op jit(solution)/shard_map/ppermute | solution.py:18
  69.8 5.0 %collective-permute-start.13 = (f32[16,1,32,128]{3,2,1,0:T(8,128)S(1)}, f32[16,1,32,128]{3,2,1,0:T(8,128)S(1)}, u32[]{:S(2)}, u32[]{:S(2)}) collective-permute-start(f32[16,1,32,128]{3,2,1,0:T(8,128)S(1)} %get-tuple-element.16), channel_id=1, source_target_pairs={{0,4},{4,8},{8,12},{12,16},{16,20},{20,24},{24,28},{1,5},{5,9},{9,... | collective-permute-start | bytes 786440 | tf_op jit(solution)/shard_map/ppermute | solution.py:18
  76.1 3.2 %collective-permute-start.15 = (f32[16,8,1,128]{3,2,1,0:T(1,128)S(1)}, f32[16,8,1,128]{3,2,1,0:T(1,128)S(1)}, u32[]{:S(2)}, u32[]{:S(2)}) collective-permute-start(f32[16,8,1,128]{3,2,1,0:T(1,128)S(1)} %get-tuple-element.15), channel_id=1, source_target_pairs={{0,1},{1,2},{2,3},{4,5},{5,6},{6,7},{8,9},{9,10},{10,11},{12,13},{... | collective-permute-start | bytes 196616 | tf_op jit(solution)/shard_map/ppermute | solution.py:18
  80.0 5.2 %collective-permute-done.13 = f32[16,1,32,128]{3,2,1,0:T(8,128)S(1)} collective-permute-done((f32[16,1,32,128]{3,2,1,0:T(8,128)S(1)}, f32[16,1,32,128]{3,2,1,0:T(8,128)S(1)}, u32[]{:S(2)}, u32[]{:S(2)}) %collective-permute-start.13) | collective-permute-done | bytes 262176 | tf_op jit(solution)/shard_map/ppermute | solution.py:18
  86.4 2.7 %broadcast_multiply_fusion = (f32[16,8,32,128]{3,2,1,0:T(8,128)S(1)}, f32[16,8,32,128]{3,2,1,0:T(8,128)}) fusion(f32[16,8,32,128]{3,2,1,0:T(8,128)S(1)} %get-tuple-element.7, f32[16,8,32,128]{3,2,1,0:T(8,128)S(1)} %get-tuple-element.5, f32[16,8,32,127]{3,2,1,0:T(8,128)S(1)} %fusion.36, f32[16,8,33,128]{3,2,1,0:T(8,128)S(1)} %fusion.6, ...), kind=kLoop, calls=%fused_computation.125 | loop fusion | flops 7340032 | bytes 19120128 | tf_op jit(solution)/shard_map/div | solution.py:131
  89.2 3.6 %fusion.70 = f32[16,16]{0,1:T(8,128)S(1)} fusion(f32[16,8,32,128]{3,2,1,0:T(8,128)S(1)} %get-tuple-element.2), kind=kOutput, calls=%fused_computation.123 | convolution fusion | flops 100663296 | bytes 2098176 | tf_op jit(solution)/shard_map/kc,lc->kl/dot_general | solution.py:74
  95.4 2.2 %collective-permute-done.17 = f32[16,16]{0,1:T(8,128)S(1)} collective-permute-done((f32[16,16]{0,1:T(8,128)S(1)}, f32[16,16]{0,1:T(8,128)S(1)}, u32[]{:S(2)}, u32[]{:S(2)}) %collective-permute-start.17) | collective-permute-done | bytes 1056 | tf_op jit(solution)/shard_map/ppermute | solution.py:68
  97.6 2.5 %collective-permute-start.18 = (f32[16,16]{0,1:T(8,128)S(1)}, f32[16,16]{0,1:T(8,128)S(1)}, u32[]{:S(2)}, u32[]{:S(2)}) collective-permute-start(f32[16,16]{0,1:T(8,128)S(1)} %add.143), channel_id=1, source_target_pairs={{0,4},{4,0},{8,12},{12,8},{16,20},{20,16},{24,28},{28,24},{1,5},{5... | collective-permute-start | bytes 3080 | tf_op jit(solution)/shard_map/ppermute | solution.py:68
  105.7 2.6 %collective-permute-start.20 = (f32[16,16]{0,1:T(8,128)S(1)}, f32[16,16]{0,1:T(8,128)S(1)}, u32[]{:S(2)}, u32[]{:S(2)}) collective-permute-start(f32[16,16]{0,1:T(8,128)S(1)} %add.145), channel_id=1, source_target_pairs={{0,16},{4,20},{8,24},{12,28},{16,0},{20,4},{24,8},{28,12},{1,17},{... | collective-permute-start | bytes 3080 | tf_op jit(solution)/shard_map/ppermute | solution.py:68
  109.7 4.6 %collective-permute-start.22 = (f32[16,1,32,128]{3,2,1,0:T(8,128)}, f32[16,1,32,128]{3,2,1,0:T(8,128)S(1)}, u32[]{:S(2)}, u32[]{:S(2)}) collective-permute-start(f32[16,1,32,128]{3,2,1,0:T(8,128)} %get-tuple-element.12), channel_id=1, source_target_pairs={{0,4},{4,8},{8,12},{12,16},{16,20},{20,24},{24,28},{1,5},{5,9},{9,... | collective-permute-start | bytes 786440 | tf_op jit(solution)/shard_map/ppermute | solution.py:18
  115.5 3.0 %collective-permute-start.24 = (f32[16,8,1,128]{3,2,1,0:T(1,128)S(1)}, f32[16,8,1,128]{3,2,1,0:T(1,128)S(1)}, u32[]{:S(2)}, u32[]{:S(2)}) collective-permute-start(f32[16,8,1,128]{3,2,1,0:T(1,128)S(1)} %get-tuple-element.11), channel_id=1, source_target_pairs={{0,1},{1,2},{2,3},{4,5},{5,6},{6,7},{8,9},{9,10},{10,11},{12,13},{... | collective-permute-start | bytes 196616 | tf_op jit(solution)/shard_map/ppermute | solution.py:18
  124.8 4.5 %fusion.73 = f32[16,16]{0,1:T(8,128)S(1)} fusion(f32[16,8,32,128]{3,2,1,0:T(8,128)S(1)} %fusion.34, f32[16,8,32,128]{3,2,1,0:T(8,128)S(1)} %get-tuple-element.2), kind=kOutput, calls=%fused_computation.124 | convolution fusion | flops 100663296 | bytes 4195328 | tf_op jit(solution)/shard_map/kc,lc->kl/dot_general | solution.py:74
  134.2 2.6 %collective-permute-start.27 = (f32[16,16]{0,1:T(8,128)S(1)}, f32[16,16]{0,1:T(8,128)S(1)}, u32[]{:S(2)}, u32[]{:S(2)}) collective-permute-start(f32[16,16]{0,1:T(8,128)S(1)} %add.152), channel_id=1, source_target_pairs={{0,4},{4,0},{8,12},{12,8},{16,20},{20,16},{24,28},{28,24},{1,5},{5... | collective-permute-start | bytes 3080 | tf_op jit(solution)/shard_map/ppermute | solution.py:68
  139.8 2.8 %fusion.28 = f32[16,32768]{1,0:T(8,128)S(1)} fusion(f32[16,16]{1,0:T(8,128)S(1)} %fusion.79, f32[2,8,256,128]{3,2,1,0:T(8,128)S(1)} %bitcast.61), kind=kOutput, calls=%fused_computation.66 | convolution fusion | flops 100663296 | bytes 4195328 | tf_op jit(solution)/shard_map/kl,lc->kc/dot_general | solution.py:78
  145.5 3.1 %fusion.25 = f32[16,32768]{1,0:T(8,128)S(1)} fusion(f32[16,16]{1,0:T(8,128)S(1)} %fusion.79, f32[2,8,256,128]{3,2,1,0:T(8,128)S(1)} %bitcast.62), kind=kOutput, calls=%fused_computation.63 | convolution fusion | flops 100663296 | bytes 4195328 | tf_op jit(solution)/shard_map/kl,lc->kc/dot_general | solution.py:78
  149.2 1.9 %fusion.69 = f32[2,8,256,128]{3,1,2,0:T(8,128)S(1)} fusion(f32[16,32768]{1,0:T(8,128)S(1)} %fusion.25, f32[16,16]{1,0:T(8,128)S(1)} %fusion.103, f32[16,32768]{1,0:T(8,128)S(1)} %fusion.28), kind=kOutput, calls=%fused_computation.122 | convolution fusion | flops 101187584 | bytes 6292480 | tf_op jit(solution)/shard_map/kl,lc->kc/dot_general | solution.py:78
  (144 shorter events, 59.6 us)
Async XLA Ops:
  4.7 19.6 %collective-permute-start.1 = (f32[21,1,32,128]{3,2,1,0:T(8,128)S(1)}, f32[21,1,32,128]{3,2,1,0:T(8,128)S(1)}, u32[]{:S(2)}, u32[]{:S(2)}) collective-permute-start(f32[21,1,32,128]{3,2,1,0:T(8,128)S(1)} %pad_maximum_fusion.20), channel_id=1, source_target_pairs={{0,4},{4,8},{8,12},{12,16},{16,20},{20,24},{24,28},{1,5},{5,9},{9,... | collective-permute-start | bytes 1032200 | tf_op jit(solution)/shard_map/ppermute | solution.py:113
  9.6 14.6 %collective-permute-start.2 = (f32[21,1,32,128]{3,2,1,0:T(8,128)S(1)}, f32[21,1,32,128]{3,2,1,0:T(8,128)S(1)}, u32[]{:S(2)}, u32[]{:S(2)}) collective-permute-start(f32[21,1,32,128]{3,2,1,0:T(8,128)S(1)} %pad_maximum_fusion.21), channel_id=1, source_target_pairs={{4,0},{8,4},{12,8},{16,12},{20,16},{24,20},{28,24},{5,1},{9,5},{13... | collective-permute-start | bytes 1032200 | tf_op jit(solution)/shard_map/ppermute | solution.py:113
  11.1 4.4 %collective-permute-start.3 = (f32[21,8,1,128]{3,2,1,0:T(1,128)S(1)}, f32[21,8,1,128]{3,2,1,0:T(1,128)S(1)}, u32[]{:S(2)}, u32[]{:S(2)}) collective-permute-start(f32[21,8,1,128]{3,2,1,0:T(1,128)S(1)} %pad_maximum_fusion.23), channel_id=1, source_target_pairs={{1,0},{2,1},{3,2},{5,4},{6,5},{7,6},{9,8},{10,9},{11,10},{13,12},{... | collective-permute-start | bytes 258056 | tf_op jit(solution)/shard_map/ppermute | solution.py:113
  29.5 11.3 %collective-permute-start.4 = (f32[16,1,32,128]{3,2,1,0:T(8,128)S(1)}, f32[16,1,32,128]{3,2,1,0:T(8,128)S(1)}, u32[]{:S(2)}, u32[]{:S(2)}) collective-permute-start(f32[16,1,32,128]{3,2,1,0:T(8,128)S(1)} %get-tuple-element.25), channel_id=1, source_target_pairs={{4,0},{8,4},{12,8},{16,12},{20,16},{24,20},{28,24},{5,1},{9,5},{13... | collective-permute-start | bytes 786440 | tf_op jit(solution)/shard_map/ppermute | solution.py:19
  30.8 15.1 %collective-permute-start.5 = (f32[16,1,32,128]{3,2,1,0:T(8,128)S(1)}, f32[16,1,32,128]{3,2,1,0:T(8,128)S(1)}, u32[]{:S(2)}, u32[]{:S(2)}) collective-permute-start(f32[16,1,32,128]{3,2,1,0:T(8,128)S(1)} %get-tuple-element.24), channel_id=1, source_target_pairs={{0,4},{4,8},{8,12},{12,16},{16,20},{20,24},{24,28},{1,5},{5,9},{9,... | collective-permute-start | bytes 786440 | tf_op jit(solution)/shard_map/ppermute | solution.py:18
  35.8 10.4 %collective-permute-start.6 = (f32[16,8,1,128]{3,2,1,0:T(1,128)S(1)}, f32[16,8,1,128]{3,2,1,0:T(1,128)S(1)}, u32[]{:S(2)}, u32[]{:S(2)}) collective-permute-start(f32[16,8,1,128]{3,2,1,0:T(1,128)S(1)} %get-tuple-element.22), channel_id=1, source_target_pairs={{1,0},{2,1},{3,2},{5,4},{6,5},{7,6},{9,8},{10,9},{11,10},{13,12},{... | collective-permute-start | bytes 196616 | tf_op jit(solution)/shard_map/ppermute | solution.py:19
  37.1 9.1 %collective-permute-start.7 = (f32[16,8,1,128]{3,2,1,0:T(1,128)S(1)}, f32[16,8,1,128]{3,2,1,0:T(1,128)S(1)}, u32[]{:S(2)}, u32[]{:S(2)}) collective-permute-start(f32[16,8,1,128]{3,2,1,0:T(1,128)S(1)} %get-tuple-element.23), channel_id=1, source_target_pairs={{0,1},{1,2},{2,3},{4,5},{5,6},{6,7},{8,9},{9,10},{10,11},{12,13},{... | collective-permute-start | bytes 196616 | tf_op jit(solution)/shard_map/ppermute | solution.py:18
  49.1 11.3 %collective-permute-start.8 = (f32[16,1,32,128]{3,2,1,0:T(8,128)S(1)}, f32[16,1,32,128]{3,2,1,0:T(8,128)S(1)}, u32[]{:S(2)}, u32[]{:S(2)}) collective-permute-start(f32[16,1,32,128]{3,2,1,0:T(8,128)S(1)} %get-tuple-element.21), channel_id=1, source_target_pairs={{4,0},{8,4},{12,8},{16,12},{20,16},{24,20},{28,24},{5,1},{9,5},{13... | collective-permute-start | bytes 786440 | tf_op jit(solution)/shard_map/ppermute | solution.py:19
  50.4 15.3 %collective-permute-start.9 = (f32[16,1,32,128]{3,2,1,0:T(8,128)S(1)}, f32[16,1,32,128]{3,2,1,0:T(8,128)S(1)}, u32[]{:S(2)}, u32[]{:S(2)}) collective-permute-start(f32[16,1,32,128]{3,2,1,0:T(8,128)S(1)} %get-tuple-element.20), channel_id=1, source_target_pairs={{0,4},{4,8},{8,12},{12,16},{16,20},{20,24},{24,28},{1,5},{5,9},{9,... | collective-permute-start | bytes 786440 | tf_op jit(solution)/shard_map/ppermute | solution.py:18
  55.4 10.6 %collective-permute-start.10 = (f32[16,8,1,128]{3,2,1,0:T(1,128)S(1)}, f32[16,8,1,128]{3,2,1,0:T(1,128)S(1)}, u32[]{:S(2)}, u32[]{:S(2)}) collective-permute-start(f32[16,8,1,128]{3,2,1,0:T(1,128)S(1)} %get-tuple-element.18), channel_id=1, source_target_pairs={{1,0},{2,1},{3,2},{5,4},{6,5},{7,6},{9,8},{10,9},{11,10},{13,12},{... | collective-permute-start | bytes 196616 | tf_op jit(solution)/shard_map/ppermute | solution.py:19
  56.7 9.3 %collective-permute-start.11 = (f32[16,8,1,128]{3,2,1,0:T(1,128)S(1)}, f32[16,8,1,128]{3,2,1,0:T(1,128)S(1)}, u32[]{:S(2)}, u32[]{:S(2)}) collective-permute-start(f32[16,8,1,128]{3,2,1,0:T(1,128)S(1)} %get-tuple-element.19), channel_id=1, source_target_pairs={{0,1},{1,2},{2,3},{4,5},{5,6},{6,7},{8,9},{9,10},{10,11},{12,13},{... | collective-permute-start | bytes 196616 | tf_op jit(solution)/shard_map/ppermute | solution.py:18
  68.5 11.5 %collective-permute-start.12 = (f32[16,1,32,128]{3,2,1,0:T(8,128)S(1)}, f32[16,1,32,128]{3,2,1,0:T(8,128)S(1)}, u32[]{:S(2)}, u32[]{:S(2)}) collective-permute-start(f32[16,1,32,128]{3,2,1,0:T(8,128)S(1)} %get-tuple-element.17), channel_id=1, source_target_pairs={{4,0},{8,4},{12,8},{16,12},{20,16},{24,20},{28,24},{5,1},{9,5},{13... | collective-permute-start | bytes 786440 | tf_op jit(solution)/shard_map/ppermute | solution.py:19
  69.8 15.3 %collective-permute-start.13 = (f32[16,1,32,128]{3,2,1,0:T(8,128)S(1)}, f32[16,1,32,128]{3,2,1,0:T(8,128)S(1)}, u32[]{:S(2)}, u32[]{:S(2)}) collective-permute-start(f32[16,1,32,128]{3,2,1,0:T(8,128)S(1)} %get-tuple-element.16), channel_id=1, source_target_pairs={{0,4},{4,8},{8,12},{12,16},{16,20},{20,24},{24,28},{1,5},{5,9},{9,... | collective-permute-start | bytes 786440 | tf_op jit(solution)/shard_map/ppermute | solution.py:18
  74.8 10.7 %collective-permute-start.14 = (f32[16,8,1,128]{3,2,1,0:T(1,128)S(1)}, f32[16,8,1,128]{3,2,1,0:T(1,128)S(1)}, u32[]{:S(2)}, u32[]{:S(2)}) collective-permute-start(f32[16,8,1,128]{3,2,1,0:T(1,128)S(1)} %get-tuple-element.14), channel_id=1, source_target_pairs={{1,0},{2,1},{3,2},{5,4},{6,5},{7,6},{9,8},{10,9},{11,10},{13,12},{... | collective-permute-start | bytes 196616 | tf_op jit(solution)/shard_map/ppermute | solution.py:19
  76.1 9.4 %collective-permute-start.15 = (f32[16,8,1,128]{3,2,1,0:T(1,128)S(1)}, f32[16,8,1,128]{3,2,1,0:T(1,128)S(1)}, u32[]{:S(2)}, u32[]{:S(2)}) collective-permute-start(f32[16,8,1,128]{3,2,1,0:T(1,128)S(1)} %get-tuple-element.15), channel_id=1, source_target_pairs={{0,1},{1,2},{2,3},{4,5},{5,6},{6,7},{8,9},{9,10},{10,11},{12,13},{... | collective-permute-start | bytes 196616 | tf_op jit(solution)/shard_map/ppermute | solution.py:18
  97.6 4.4 %collective-permute-start.18 = (f32[16,16]{0,1:T(8,128)S(1)}, f32[16,16]{0,1:T(8,128)S(1)}, u32[]{:S(2)}, u32[]{:S(2)}) collective-permute-start(f32[16,16]{0,1:T(8,128)S(1)} %add.143), channel_id=1, source_target_pairs={{0,4},{4,0},{8,12},{12,8},{16,20},{20,16},{24,28},{28,24},{1,5},{5... | collective-permute-start | bytes 3080 | tf_op jit(solution)/shard_map/ppermute | solution.py:68
  105.7 12.9 %collective-permute-start.20 = (f32[16,16]{0,1:T(8,128)S(1)}, f32[16,16]{0,1:T(8,128)S(1)}, u32[]{:S(2)}, u32[]{:S(2)}) collective-permute-start(f32[16,16]{0,1:T(8,128)S(1)} %add.145), channel_id=1, source_target_pairs={{0,16},{4,20},{8,24},{12,28},{16,0},{20,4},{24,8},{28,12},{1,17},{... | collective-permute-start | bytes 3080 | tf_op jit(solution)/shard_map/ppermute | solution.py:68
  108.4 11.8 %collective-permute-start.21 = (f32[16,1,32,128]{3,2,1,0:T(8,128)}, f32[16,1,32,128]{3,2,1,0:T(8,128)S(1)}, u32[]{:S(2)}, u32[]{:S(2)}) collective-permute-start(f32[16,1,32,128]{3,2,1,0:T(8,128)} %get-tuple-element.13), channel_id=1, source_target_pairs={{4,0},{8,4},{12,8},{16,12},{20,16},{24,20},{28,24},{5,1},{9,5},{13... | collective-permute-start | bytes 786440 | tf_op jit(solution)/shard_map/ppermute | solution.py:19
  109.7 11.3 %collective-permute-start.22 = (f32[16,1,32,128]{3,2,1,0:T(8,128)}, f32[16,1,32,128]{3,2,1,0:T(8,128)S(1)}, u32[]{:S(2)}, u32[]{:S(2)}) collective-permute-start(f32[16,1,32,128]{3,2,1,0:T(8,128)} %get-tuple-element.12), channel_id=1, source_target_pairs={{0,4},{4,8},{8,12},{12,16},{16,20},{20,24},{24,28},{1,5},{5,9},{9,... | collective-permute-start | bytes 786440 | tf_op jit(solution)/shard_map/ppermute | solution.py:18
  114.2 7.1 %collective-permute-start.23 = (f32[16,8,1,128]{3,2,1,0:T(1,128)S(1)}, f32[16,8,1,128]{3,2,1,0:T(1,128)S(1)}, u32[]{:S(2)}, u32[]{:S(2)}) collective-permute-start(f32[16,8,1,128]{3,2,1,0:T(1,128)S(1)} %get-tuple-element.10), channel_id=1, source_target_pairs={{1,0},{2,1},{3,2},{5,4},{6,5},{7,6},{9,8},{10,9},{11,10},{13,12},{... | collective-permute-start | bytes 196616 | tf_op jit(solution)/shard_map/ppermute | solution.py:19
  115.5 5.8 %collective-permute-start.24 = (f32[16,8,1,128]{3,2,1,0:T(1,128)S(1)}, f32[16,8,1,128]{3,2,1,0:T(1,128)S(1)}, u32[]{:S(2)}, u32[]{:S(2)}) collective-permute-start(f32[16,8,1,128]{3,2,1,0:T(1,128)S(1)} %get-tuple-element.11), channel_id=1, source_target_pairs={{0,1},{1,2},{2,3},{4,5},{5,6},{6,7},{8,9},{9,10},{10,11},{12,13},{... | collective-permute-start | bytes 196616 | tf_op jit(solution)/shard_map/ppermute | solution.py:18
  134.2 4.2 %collective-permute-start.27 = (f32[16,16]{0,1:T(8,128)S(1)}, f32[16,16]{0,1:T(8,128)S(1)}, u32[]{:S(2)}, u32[]{:S(2)}) collective-permute-start(f32[16,16]{0,1:T(8,128)S(1)} %add.152), channel_id=1, source_target_pairs={{0,4},{4,0},{8,12},{12,8},{16,20},{20,16},{24,28},{28,24},{1,5},{5... | collective-permute-start | bytes 3080 | tf_op jit(solution)/shard_map/ppermute | solution.py:68
  138.5 5.9 %collective-permute-start.28 = (f32[16,16]{0,1:T(8,128)S(1)}, f32[16,16]{0,1:T(8,128)S(1)}, u32[]{:S(2)}, u32[]{:S(2)}) collective-permute-start(f32[16,16]{0,1:T(8,128)S(1)} %add.153), channel_id=1, source_target_pairs={{0,8},{4,12},{8,0},{12,4},{16,24},{20,28},{24,16},{28,20},{1,9},{5... | collective-permute-start | bytes 3080 | tf_op jit(solution)/shard_map/ppermute | solution.py:68
  144.3 4.6 %collective-permute-start.29 = (f32[16,16]{0,1:T(8,128)S(1)}, f32[16,16]{0,1:T(8,128)S(1)}, u32[]{:S(2)}, u32[]{:S(2)}) collective-permute-start(f32[16,16]{0,1:T(8,128)S(1)} %add.154), channel_id=1, source_target_pairs={{0,16},{4,20},{8,24},{12,28},{16,0},{20,4},{24,8},{28,12},{1,17},{... | collective-permute-start | bytes 3080 | tf_op jit(solution)/shard_map/ppermute | solution.py:68
  (19 other events, 57.0 us)
where the time goes:
time: 154 us; the launch traced here: 153 us
  starting transfers between devices  67.9 us (44%)
  waiting for transfers between devices  31.8 us (21%)
  other arithmetic  27.6 us (18%)
  matrix products  16.5 us (11%)
  local copies, waits for them, and re-layouts  7.59 us (5%)
    ppermute x8, starting transfers between devices, halo_pair(): lax.ppermute(lax.slice_in_dim(block, block.shape[dim] - 1, None, axis=dim...  32 us
    ppermute x8, waiting for transfers between devices, halo_pair(): lax.ppermute(lax.slice_in_dim(block, block.shape[dim] - 1, None, axis=dim...  16.4 us
    ppermute x10, starting transfers between devices, reduce_all(): value = value + lax.ppermute(value, axis, pairs)  15.1 us
    ppermute x8, starting transfers between devices, halo_pair(): high = lax.ppermute(lax.slice_in_dim(block, 0, 1, axis=dim), axis, backward)  10.3 us
    ppermute x2, waiting for transfers between devices, on_device(): lax.ppermute(to_high, axis, forward)  8.63 us
    dot_general x2, matrix products, inner_products(): return jnp.einsum('kc,lc->kl', left, right, precision=lax.Precision.HIGHEST)  8.14 us
    ppermute x2, starting transfers between devices, on_device(): lax.ppermute(to_high, axis, forward)  7.93 us
    dot_general x3, matrix products, combine(): jnp.einsum('kl,lc->kc', matrix, rows, precision=lax.Precision.HIGHEST)  7.89 us
  transfers between devices with their start and end apart: 30, of which 13 were waited for; matrix products, arithmetic and copies ran while one was open for 12% of the time, Pallas kernels for 0%

commit v1 on v0

--- a/solution.py
+++ b/solution.py
@@ -98,13 +98,16 @@
     field = start_panel * ocean_cells[None]
     fields = jnp.stack([ocean_cells, conduct_x, conduct_y, conduct_z, diag_shift])
     rows, cols = field.shape[1], field.shape[2]
-    edges = [
-        jnp.concatenate([part[:, a:b] for part in (field, fields)])
-        for a, b in ((rows - 1, rows), (0, 1))
-    ] + [
-        jnp.concatenate([part[:, :, a:b] for part in (field, fields)])
-        for a, b in ((cols - 1, cols), (0, 1))
-    ]
+    inputs = (ocean_cells, conduct_x, conduct_y, conduct_z, diag_shift)
+
+    def edge(dim, first):
+        def cut(a, lead):
+            return lax.slice_in_dim(a, first, first + 1, axis=dim + lead)
+
+        panel = cut(start_panel, 1) * cut(ocean_cells, 0)[None]
+        return jnp.concatenate([panel, jnp.stack([cut(a, 0) for a in inputs])])
+
+    edges = [edge(0, rows - 1), edge(0, 0), edge(1, cols - 1), edge(1, 0)]
     halos = []
     for axis, (to_high, to_low) in (("gx", edges[0:2]), ("gy", edges[2:4])):
         count = lax.axis_size(axis)
@@ -115,8 +118,8 @@
     def assemble(block, part):
         low_x, high_x, low_y, high_y = (halo[part] for halo in halos)
         block = jnp.concatenate([low_x, block, high_x], axis=1)
-        edge = ((0, 0), (1, 1), (0, 0), (0, 0))
-        return jnp.concatenate([jnp.pad(low_y, edge), block, jnp.pad(high_y, edge)], axis=2)
+        ring = ((0, 0), (1, 1), (0, 0), (0, 0))
+        return jnp.concatenate([jnp.pad(low_y, ring), block, jnp.pad(high_y, ring)], axis=2)
 
     fields_one = assemble(fields, slice(vectors, None))
     together = assemble(field, slice(0, vectors))

time: 154 us -> 158 us (1.026)
  local copies, waits for them, and re-layouts: 7.59 us -> 13.5 us
  starting transfers between devices: 67.9 us -> 64.4 us
    ppermute x2, waiting for transfers between devices: 8.63 us -> 3.36 us  [on_device(): lax.ppermute(to_high, axis, forward)]
    unnamed x27 -> x38, local copies, waits for them, and re-layouts: 5.45 us -> 9.92 us
    ppermute x2, waiting for transfers between devices: 0.01 us -> 2.32 us  [on_device(): lax.ppermute(to_low, axis, backward)]
    ppermute x10, starting transfers between devices: 15.1 us -> 13.2 us  [reduce_all(): value = value + lax.ppermute(value, axis, pairs)]
    ppermute x10, waiting for transfers between devices: 6.75 us -> 8.62 us  [reduce_all(): value = value + lax.ppermute(value, axis, pairs)]
    mul x1, other arithmetic: 1.91 us -> 0.27 us  [on_device(): field = start_panel * ocean_cells[None]]
    ppermute x2, starting transfers between devices: 7.93 us -> 6.34 us  [on_device(): lax.ppermute(to_high, axis, forward)]
  transfers between devices with their start and end apart: 30 -> 30, of which waited for: 13 -> 13; matrix products, arithmetic and copies ran while one was open for 12% -> 14% of each run, Pallas kernels for 0% -> 0%
where the time goes in v1:
time: 158 us; the launch traced here: 156 us
  starting transfers between devices  64.4 us (41%)
  waiting for transfers between devices  31.5 us (20%)
  other arithmetic  28.8 us (18%)
  matrix products  16.5 us (10%)
  local copies, waits for them, and re-layouts  13.5 us (9%)
    ppermute x8, starting transfers between devices, halo_pair(): lax.ppermute(lax.slice_in_dim(block, block.shape[dim] - 1, None, axis=dim...  31.9 us
    ppermute x8, waiting for transfers between devices, halo_pair(): lax.ppermute(lax.slice_in_dim(block, block.shape[dim] - 1, None, axis=dim...  17.1 us
    ppermute x10, starting transfers between devices, reduce_all(): value = value + lax.ppermute(value, axis, pairs)  13.2 us
    ppermute x8, starting transfers between devices, halo_pair(): high = lax.ppermute(lax.slice_in_dim(block, 0, 1, axis=dim), axis, backward)  10.3 us
    unnamed x38, local copies, waits for them, and re-layouts  9.92 us
    ppermute x10, waiting for transfers between devices, reduce_all(): value = value + lax.ppermute(value, axis, pairs)  8.62 us
    dot_general x2, matrix products, inner_products(): return jnp.einsum('kc,lc->kl', left, right, precision=lax.Precision.HIGHEST)  8.14 us
    dot_general x3, matrix products, combine(): jnp.einsum('kl,lc->kc', matrix, rows, precision=lax.Precision.HIGHEST)  7.89 us
  transfers between devices with their start and end apart: 30, of which 13 were waited for; matrix products, arithmetic and copies ran while one was open for 14% of the time, Pallas kernels for 0%

profile of v1, /device:TPU:0, one launch (start us, length us, event | category | flops | bytes accessed | tf_op | source)
XLA Modules:
  0.0 156.2 jit_solution(6809446512937224696)
XLA Ops:
  5.9 4.9 %collective-permute-start.1 = (f32[21,1,32,128]{3,2,1,0:T(8,128)S(1)}, f32[21,1,32,128]{3,2,1,0:T(8,128)S(1)}, u32[]{:S(2)}, u32[]{:S(2)}) collective-permute-start(f32[21,1,32,128]{3,2,1,0:T(8,128)S(1)} %get-tuple-element.38), channel_id=1, source_target_pairs={{0,4},{4,8},{8,12},{12,16},{16,20},{20,24},{24,28},{1,5},{5,9},{9,... | collective-permute-start | bytes 1032200 | tf_op jit(solution)/shard_map/ppermute | solution.py:116
  19.7 2.3 %collective-permute-done.3 = f32[21,8,1,128]{3,2,1,0:T(1,128)S(1)} collective-permute-done((f32[21,8,1,128]{3,2,1,0:T(1,128)S(1)}, f32[21,8,1,128]{3,2,1,0:T(1,128)S(1)}, u32[]{:S(2)}, u32[]{:S(2)}) %collective-permute-start.3) | collective-permute-done | bytes 86048 | tf_op jit(solution)/shard_map/ppermute | solution.py:116
  22.1 3.4 %collective-permute-done.1 = f32[21,1,32,128]{3,2,1,0:T(8,128)S(1)} collective-permute-done((f32[21,1,32,128]{3,2,1,0:T(8,128)S(1)}, f32[21,1,32,128]{3,2,1,0:T(8,128)S(1)}, u32[]{:S(2)}, u32[]{:S(2)}) %collective-permute-start.1) | collective-permute-done | bytes 344096 | tf_op jit(solution)/shard_map/ppermute | solution.py:116
  31.3 5.0 %collective-permute-start.5 = (f32[16,1,32,128]{3,2,1,0:T(8,128)S(1)}, f32[16,1,32,128]{3,2,1,0:T(8,128)S(1)}, u32[]{:S(2)}, u32[]{:S(2)}) collective-permute-start(f32[16,1,32,128]{3,2,1,0:T(8,128)S(1)} %get-tuple-element.24), channel_id=1, source_target_pairs={{0,4},{4,8},{8,12},{12,16},{16,20},{20,24},{24,28},{1,5},{5,9},{9,... | collective-permute-start | bytes 786440 | tf_op jit(solution)/shard_map/ppermute | solution.py:18
  37.6 3.0 %collective-permute-start.7 = (f32[16,8,1,128]{3,2,1,0:T(1,128)S(1)}, f32[16,8,1,128]{3,2,1,0:T(1,128)S(1)}, u32[]{:S(2)}, u32[]{:S(2)}) collective-permute-start(f32[16,8,1,128]{3,2,1,0:T(1,128)S(1)} %get-tuple-element.23), channel_id=1, source_target_pairs={{0,1},{1,2},{2,3},{4,5},{5,6},{6,7},{8,9},{9,10},{10,11},{12,13},{... | collective-permute-start | bytes 196616 | tf_op jit(solution)/shard_map/ppermute | solution.py:18
  41.3 5.8 %collective-permute-done.5 = f32[16,1,32,128]{3,2,1,0:T(8,128)S(1)} collective-permute-done((f32[16,1,32,128]{3,2,1,0:T(8,128)S(1)}, f32[16,1,32,128]{3,2,1,0:T(8,128)S(1)}, u32[]{:S(2)}, u32[]{:S(2)}) %collective-permute-start.5) | collective-permute-done | bytes 262176 | tf_op jit(solution)/shard_map/ppermute | solution.py:18
  51.6 5.0 %collective-permute-start.9 = (f32[16,1,32,128]{3,2,1,0:T(8,128)S(1)}, f32[16,1,32,128]{3,2,1,0:T(8,128)S(1)}, u32[]{:S(2)}, u32[]{:S(2)}) collective-permute-start(f32[16,1,32,128]{3,2,1,0:T(8,128)S(1)} %get-tuple-element.20), channel_id=1, source_target_pairs={{0,4},{4,8},{8,12},{12,16},{16,20},{20,24},{24,28},{1,5},{5,9},{9,... | collective-permute-start | bytes 786440 | tf_op jit(solution)/shard_map/ppermute | solution.py:18
  57.9 3.0 %collective-permute-start.11 = (f32[16,8,1,128]{3,2,1,0:T(1,128)S(1)}, f32[16,8,1,128]{3,2,1,0:T(1,128)S(1)}, u32[]{:S(2)}, u32[]{:S(2)}) collective-permute-start(f32[16,8,1,128]{3,2,1,0:T(1,128)S(1)} %get-tuple-element.19), channel_id=1, source_target_pairs={{0,1},{1,2},{2,3},{4,5},{5,6},{6,7},{8,9},{9,10},{10,11},{12,13},{... | collective-permute-start | bytes 196616 | tf_op jit(solution)/shard_map/ppermute | solution.py:18
  61.6 5.4 %collective-permute-done.9 = f32[16,1,32,128]{3,2,1,0:T(8,128)S(1)} collective-permute-done((f32[16,1,32,128]{3,2,1,0:T(8,128)S(1)}, f32[16,1,32,128]{3,2,1,0:T(8,128)S(1)}, u32[]{:S(2)}, u32[]{:S(2)}) %collective-permute-start.9) | collective-permute-done | bytes 262176 | tf_op jit(solution)/shard_map/ppermute | solution.py:18
  68.2 2.7 %broadcast_multiply_fusion.2 = (f32[16,8,32,128]{3,2,1,0:T(8,128)S(1)}, f32[16,8,32,128]{3,2,1,0:T(8,128)}) fusion(f32[16,8,32,128]{3,2,1,0:T(8,128)S(1)} %get-tuple-element.7, f32[16,8,32,127]{3,2,1,0:T(8,128)S(1)} %fusion.44, f32[16,8,33,128]{3,2,1,0:T(8,128)S(1)} %fusion.10, f32[16,9,32,128]{3,2,1,0:T(8,128)S(1)} %fusion.22, ...), kind=kLoop, calls=%fused_computation.127 | loop fusion | flops 5767168 | bytes 17022976 | tf_op jit(solution)/shard_map/div | solution.py:133
  72.3 5.0 %collective-permute-start.13 = (f32[16,1,32,128]{3,2,1,0:T(8,128)S(1)}, f32[16,1,32,128]{3,2,1,0:T(8,128)S(1)}, u32[]{:S(2)}, u32[]{:S(2)}) collective-permute-start(f32[16,1,32,128]{3,2,1,0:T(8,128)S(1)} %get-tuple-element.16), channel_id=1, source_target_pairs={{0,4},{4,8},{8,12},{12,16},{16,20},{20,24},{24,28},{1,5},{5,9},{9,... | collective-permute-start | bytes 786440 | tf_op jit(solution)/shard_map/ppermute | solution.py:18
  78.7 3.2 %collective-permute-start.15 = (f32[16,8,1,128]{3,2,1,0:T(1,128)S(1)}, f32[16,8,1,128]{3,2,1,0:T(1,128)S(1)}, u32[]{:S(2)}, u32[]{:S(2)}) collective-permute-start(f32[16,8,1,128]{3,2,1,0:T(1,128)S(1)} %get-tuple-element.15), channel_id=1, source_target_pairs={{0,1},{1,2},{2,3},{4,5},{5,6},{6,7},{8,9},{9,10},{10,11},{12,13},{... | collective-permute-start | bytes 196616 | tf_op jit(solution)/shard_map/ppermute | solution.py:18
  82.5 5.2 %collective-permute-done.13 = f32[16,1,32,128]{3,2,1,0:T(8,128)S(1)} collective-permute-done((f32[16,1,32,128]{3,2,1,0:T(8,128)S(1)}, f32[16,1,32,128]{3,2,1,0:T(8,128)S(1)}, u32[]{:S(2)}, u32[]{:S(2)}) %collective-permute-start.13) | collective-permute-done | bytes 262176 | tf_op jit(solution)/shard_map/ppermute | solution.py:18
  89.7 2.7 %broadcast_multiply_fusion = (f32[16,8,32,128]{3,2,1,0:T(8,128)S(1)}, f32[16,8,32,128]{3,2,1,0:T(8,128)}) fusion(f32[16,8,32,128]{3,2,1,0:T(8,128)S(1)} %get-tuple-element.7, f32[16,8,32,128]{3,2,1,0:T(8,128)S(1)} %copy-done.5, f32[16,8,32,127]{3,2,1,0:T(8,128)S(1)} %fusion.36, f32[16,8,33,128]{3,2,1,0:T(8,128)S(1)} %fusion.6, ...), kind=kLoop, calls=%fused_computation.125 | loop fusion | flops 7340032 | bytes 19120128 | tf_op jit(solution)/shard_map/div | solution.py:134
  92.4 3.6 %fusion.70 = f32[16,16]{0,1:T(8,128)S(1)} fusion(f32[16,8,32,128]{3,2,1,0:T(8,128)S(1)} %get-tuple-element.2), kind=kOutput, calls=%fused_computation.123 | convolution fusion | flops 100663296 | bytes 2098176 | tf_op jit(solution)/shard_map/kc,lc->kl/dot_general | solution.py:74
  97.9 2.9 %collective-permute-done.17 = f32[16,16]{0,1:T(8,128)S(1)} collective-permute-done((f32[16,16]{0,1:T(8,128)S(1)}, f32[16,16]{0,1:T(8,128)S(1)}, u32[]{:S(2)}, u32[]{:S(2)}) %collective-permute-start.17) | collective-permute-done | bytes 1056 | tf_op jit(solution)/shard_map/ppermute | solution.py:68
  100.9 2.5 %collective-permute-start.18 = (f32[16,16]{0,1:T(8,128)S(1)}, f32[16,16]{0,1:T(8,128)S(1)}, u32[]{:S(2)}, u32[]{:S(2)}) collective-permute-start(f32[16,16]{0,1:T(8,128)S(1)} %add.143), channel_id=1, source_target_pairs={{0,4},{4,0},{8,12},{12,8},{16,20},{20,16},{24,28},{28,24},{1,5},{5... | collective-permute-start | bytes 3080 | tf_op jit(solution)/shard_map/ppermute | solution.py:68
  109.0 2.6 %collective-permute-start.20 = (f32[16,16]{0,1:T(8,128)S(1)}, f32[16,16]{0,1:T(8,128)S(1)}, u32[]{:S(2)}, u32[]{:S(2)}) collective-permute-start(f32[16,16]{0,1:T(8,128)S(1)} %add.145), channel_id=1, source_target_pairs={{0,16},{4,20},{8,24},{12,28},{16,0},{20,4},{24,8},{28,12},{1,17},{... | collective-permute-start | bytes 3080 | tf_op jit(solution)/shard_map/ppermute | solution.py:68
  112.9 4.6 %collective-permute-start.22 = (f32[16,1,32,128]{3,2,1,0:T(8,128)}, f32[16,1,32,128]{3,2,1,0:T(8,128)S(1)}, u32[]{:S(2)}, u32[]{:S(2)}) collective-permute-start(f32[16,1,32,128]{3,2,1,0:T(8,128)} %get-tuple-element.12), channel_id=1, source_target_pairs={{0,4},{4,8},{8,12},{12,16},{16,20},{20,24},{24,28},{1,5},{5,9},{9,... | collective-permute-start | bytes 786440 | tf_op jit(solution)/shard_map/ppermute | solution.py:18
  118.8 3.0 %collective-permute-start.24 = (f32[16,8,1,128]{3,2,1,0:T(1,128)S(1)}, f32[16,8,1,128]{3,2,1,0:T(1,128)S(1)}, u32[]{:S(2)}, u32[]{:S(2)}) collective-permute-start(f32[16,8,1,128]{3,2,1,0:T(1,128)S(1)} %get-tuple-element.11), channel_id=1, source_target_pairs={{0,1},{1,2},{2,3},{4,5},{5,6},{6,7},{8,9},{9,10},{10,11},{12,13},{... | collective-permute-start | bytes 196616 | tf_op jit(solution)/shard_map/ppermute | solution.py:18
  128.1 4.5 %fusion.73 = f32[16,16]{0,1:T(8,128)S(1)} fusion(f32[16,8,32,128]{3,2,1,0:T(8,128)S(1)} %fusion.34, f32[16,8,32,128]{3,2,1,0:T(8,128)S(1)} %get-tuple-element.2), kind=kOutput, calls=%fused_computation.124 | convolution fusion | flops 100663296 | bytes 4195328 | tf_op jit(solution)/shard_map/kc,lc->kl/dot_general | solution.py:74
  137.5 2.4 %collective-permute-start.27 = (f32[16,16]{0,1:T(8,128)S(1)}, f32[16,16]{0,1:T(8,128)S(1)}, u32[]{:S(2)}, u32[]{:S(2)}) collective-permute-start(f32[16,16]{0,1:T(8,128)S(1)} %add.152), channel_id=1, source_target_pairs={{0,4},{4,0},{8,12},{12,8},{16,20},{20,16},{24,28},{28,24},{1,5},{5... | collective-permute-start | bytes 3080 | tf_op jit(solution)/shard_map/ppermute | solution.py:68
  143.0 2.8 %fusion.28 = f32[16,32768]{1,0:T(8,128)S(1)} fusion(f32[16,16]{1,0:T(8,128)S(1)} %fusion.79, f32[2,8,256,128]{3,2,1,0:T(8,128)S(1)} %bitcast.121), kind=kOutput, calls=%fused_computation.66 | convolution fusion | flops 100663296 | bytes 4195328 | tf_op jit(solution)/shard_map/kl,lc->kc/dot_general | solution.py:78
  148.8 3.1 %fusion.25 = f32[16,32768]{1,0:T(8,128)S(1)} fusion(f32[16,16]{1,0:T(8,128)S(1)} %fusion.79, f32[2,8,256,128]{3,2,1,0:T(8,128)S(1)} %bitcast.122), kind=kOutput, calls=%fused_computation.63 | convolution fusion | flops 100663296 | bytes 4195328 | tf_op jit(solution)/shard_map/kl,lc->kc/dot_general | solution.py:78
  (153 shorter events, 66.0 us)
Async XLA Ops:
  5.9 19.5 %collective-permute-start.1 = (f32[21,1,32,128]{3,2,1,0:T(8,128)S(1)}, f32[21,1,32,128]{3,2,1,0:T(8,128)S(1)}, u32[]{:S(2)}, u32[]{:S(2)}) collective-permute-start(f32[21,1,32,128]{3,2,1,0:T(8,128)S(1)} %get-tuple-element.38), channel_id=1, source_target_pairs={{0,4},{4,8},{8,12},{12,16},{16,20},{20,24},{24,28},{1,5},{5,9},{9,... | collective-permute-start | bytes 1032200 | tf_op jit(solution)/shard_map/ppermute | solution.py:116
  10.8 14.7 %collective-permute-start.2 = (f32[21,1,32,128]{3,2,1,0:T(8,128)S(1)}, f32[21,1,32,128]{3,2,1,0:T(8,128)S(1)}, u32[]{:S(2)}, u32[]{:S(2)}) collective-permute-start(f32[21,1,32,128]{3,2,1,0:T(8,128)S(1)} %get-tuple-element.39), channel_id=1, source_target_pairs={{4,0},{8,4},{12,8},{16,12},{20,16},{24,20},{28,24},{5,1},{9,5},{13... | collective-permute-start | bytes 1032200 | tf_op jit(solution)/shard_map/ppermute | solution.py:116
  15.8 6.2 %collective-permute-start = (f32[21,8,1,128]{3,2,1,0:T(1,128)S(1)}, f32[21,8,1,128]{3,2,1,0:T(1,128)S(1)}, u32[]{:S(2)}, u32[]{:S(2)}) collective-permute-start(f32[21,8,1,128]{3,2,1,0:T(1,128)S(1)} %get-tuple-element.50), channel_id=1, source_target_pairs={{0,1},{1,2},{2,3},{4,5},{5,6},{6,7},{8,9},{9,10},{10,11},{12,13},{... | collective-permute-start | bytes 258056 | tf_op jit(solution)/shard_map/ppermute | solution.py:116
  17.3 4.7 %collective-permute-start.3 = (f32[21,8,1,128]{3,2,1,0:T(1,128)S(1)}, f32[21,8,1,128]{3,2,1,0:T(1,128)S(1)}, u32[]{:S(2)}, u32[]{:S(2)}) collective-permute-start(f32[21,8,1,128]{3,2,1,0:T(1,128)S(1)} %get-tuple-element.51), channel_id=1, source_target_pairs={{1,0},{2,1},{3,2},{5,4},{6,5},{7,6},{9,8},{10,9},{11,10},{13,12},{... | collective-permute-start | bytes 258056 | tf_op jit(solution)/shard_map/ppermute | solution.py:116
  30.0 11.3 %collective-permute-start.4 = (f32[16,1,32,128]{3,2,1,0:T(8,128)S(1)}, f32[16,1,32,128]{3,2,1,0:T(8,128)S(1)}, u32[]{:S(2)}, u32[]{:S(2)}) collective-permute-start(f32[16,1,32,128]{3,2,1,0:T(8,128)S(1)} %get-tuple-element.25), channel_id=1, source_target_pairs={{4,0},{8,4},{12,8},{16,12},{20,16},{24,20},{28,24},{5,1},{9,5},{13... | collective-permute-start | bytes 786440 | tf_op jit(solution)/shard_map/ppermute | solution.py:19
  31.3 15.8 %collective-permute-start.5 = (f32[16,1,32,128]{3,2,1,0:T(8,128)S(1)}, f32[16,1,32,128]{3,2,1,0:T(8,128)S(1)}, u32[]{:S(2)}, u32[]{:S(2)}) collective-permute-start(f32[16,1,32,128]{3,2,1,0:T(8,128)S(1)} %get-tuple-element.24), channel_id=1, source_target_pairs={{0,4},{4,8},{8,12},{12,16},{16,20},{20,24},{24,28},{1,5},{5,9},{9,... | collective-permute-start | bytes 786440 | tf_op jit(solution)/shard_map/ppermute | solution.py:18
  36.3 11.1 %collective-permute-start.6 = (f32[16,8,1,128]{3,2,1,0:T(1,128)S(1)}, f32[16,8,1,128]{3,2,1,0:T(1,128)S(1)}, u32[]{:S(2)}, u32[]{:S(2)}) collective-permute-start(f32[16,8,1,128]{3,2,1,0:T(1,128)S(1)} %get-tuple-element.22), channel_id=1, source_target_pairs={{1,0},{2,1},{3,2},{5,4},{6,5},{7,6},{9,8},{10,9},{11,10},{13,12},{... | collective-permute-start | bytes 196616 | tf_op jit(solution)/shard_map/ppermute | solution.py:19
  37.6 9.8 %collective-permute-start.7 = (f32[16,8,1,128]{3,2,1,0:T(1,128)S(1)}, f32[16,8,1,128]{3,2,1,0:T(1,128)S(1)}, u32[]{:S(2)}, u32[]{:S(2)}) collective-permute-start(f32[16,8,1,128]{3,2,1,0:T(1,128)S(1)} %get-tuple-element.23), channel_id=1, source_target_pairs={{0,1},{1,2},{2,3},{4,5},{5,6},{6,7},{8,9},{9,10},{10,11},{12,13},{... | collective-permute-start | bytes 196616 | tf_op jit(solution)/shard_map/ppermute | solution.py:18
  50.3 11.3 %collective-permute-start.8 = (f32[16,1,32,128]{3,2,1,0:T(8,128)S(1)}, f32[16,1,32,128]{3,2,1,0:T(8,128)S(1)}, u32[]{:S(2)}, u32[]{:S(2)}) collective-permute-start(f32[16,1,32,128]{3,2,1,0:T(8,128)S(1)} %get-tuple-element.21), channel_id=1, source_target_pairs={{4,0},{8,4},{12,8},{16,12},{20,16},{24,20},{28,24},{5,1},{9,5},{13... | collective-permute-start | bytes 786440 | tf_op jit(solution)/shard_map/ppermute | solution.py:19
  51.6 15.4 %collective-permute-start.9 = (f32[16,1,32,128]{3,2,1,0:T(8,128)S(1)}, f32[16,1,32,128]{3,2,1,0:T(8,128)S(1)}, u32[]{:S(2)}, u32[]{:S(2)}) collective-permute-start(f32[16,1,32,128]{3,2,1,0:T(8,128)S(1)} %get-tuple-element.20), channel_id=1, source_target_pairs={{0,4},{4,8},{8,12},{12,16},{16,20},{20,24},{24,28},{1,5},{5,9},{9,... | collective-permute-start | bytes 786440 | tf_op jit(solution)/shard_map/ppermute | solution.py:18
  56.6 10.7 %collective-permute-start.10 = (f32[16,8,1,128]{3,2,1,0:T(1,128)S(1)}, f32[16,8,1,128]{3,2,1,0:T(1,128)S(1)}, u32[]{:S(2)}, u32[]{:S(2)}) collective-permute-start(f32[16,8,1,128]{3,2,1,0:T(1,128)S(1)} %get-tuple-element.18), channel_id=1, source_target_pairs={{1,0},{2,1},{3,2},{5,4},{6,5},{7,6},{9,8},{10,9},{11,10},{13,12},{... | collective-permute-start | bytes 196616 | tf_op jit(solution)/shard_map/ppermute | solution.py:19
  57.9 9.4 %collective-permute-start.11 = (f32[16,8,1,128]{3,2,1,0:T(1,128)S(1)}, f32[16,8,1,128]{3,2,1,0:T(1,128)S(1)}, u32[]{:S(2)}, u32[]{:S(2)}) collective-permute-start(f32[16,8,1,128]{3,2,1,0:T(1,128)S(1)} %get-tuple-element.19), channel_id=1, source_target_pairs={{0,1},{1,2},{2,3},{4,5},{5,6},{6,7},{8,9},{9,10},{10,11},{12,13},{... | collective-permute-start | bytes 196616 | tf_op jit(solution)/shard_map/ppermute | solution.py:18
  71.0 11.5 %collective-permute-start.12 = (f32[16,1,32,128]{3,2,1,0:T(8,128)S(1)}, f32[16,1,32,128]{3,2,1,0:T(8,128)S(1)}, u32[]{:S(2)}, u32[]{:S(2)}) collective-permute-start(f32[16,1,32,128]{3,2,1,0:T(8,128)S(1)} %get-tuple-element.17), channel_id=1, source_target_pairs={{4,0},{8,4},{12,8},{16,12},{20,16},{24,20},{28,24},{5,1},{9,5},{13... | collective-permute-start | bytes 786440 | tf_op jit(solution)/shard_map/ppermute | solution.py:19
  72.3 15.3 %collective-permute-start.13 = (f32[16,1,32,128]{3,2,1,0:T(8,128)S(1)}, f32[16,1,32,128]{3,2,1,0:T(8,128)S(1)}, u32[]{:S(2)}, u32[]{:S(2)}) collective-permute-start(f32[16,1,32,128]{3,2,1,0:T(8,128)S(1)} %get-tuple-element.16), channel_id=1, source_target_pairs={{0,4},{4,8},{8,12},{12,16},{16,20},{20,24},{24,28},{1,5},{5,9},{9,... | collective-permute-start | bytes 786440 | tf_op jit(solution)/shard_map/ppermute | solution.py:18
  77.4 10.8 %collective-permute-start.14 = (f32[16,8,1,128]{3,2,1,0:T(1,128)S(1)}, f32[16,8,1,128]{3,2,1,0:T(1,128)S(1)}, u32[]{:S(2)}, u32[]{:S(2)}) collective-permute-start(f32[16,8,1,128]{3,2,1,0:T(1,128)S(1)} %get-tuple-element.14), channel_id=1, source_target_pairs={{1,0},{2,1},{3,2},{5,4},{6,5},{7,6},{9,8},{10,9},{11,10},{13,12},{... | collective-permute-start | bytes 196616 | tf_op jit(solution)/shard_map/ppermute | solution.py:19
  78.7 9.5 %collective-permute-start.15 = (f32[16,8,1,128]{3,2,1,0:T(1,128)S(1)}, f32[16,8,1,128]{3,2,1,0:T(1,128)S(1)}, u32[]{:S(2)}, u32[]{:S(2)}) collective-permute-start(f32[16,8,1,128]{3,2,1,0:T(1,128)S(1)} %get-tuple-element.15), channel_id=1, source_target_pairs={{0,1},{1,2},{2,3},{4,5},{5,6},{6,7},{8,9},{9,10},{10,11},{12,13},{... | collective-permute-start | bytes 196616 | tf_op jit(solution)/shard_map/ppermute | solution.py:18
  100.9 4.4 %collective-permute-start.18 = (f32[16,16]{0,1:T(8,128)S(1)}, f32[16,16]{0,1:T(8,128)S(1)}, u32[]{:S(2)}, u32[]{:S(2)}) collective-permute-start(f32[16,16]{0,1:T(8,128)S(1)} %add.143), channel_id=1, source_target_pairs={{0,4},{4,0},{8,12},{12,8},{16,20},{20,16},{24,28},{28,24},{1,5},{5... | collective-permute-start | bytes 3080 | tf_op jit(solution)/shard_map/ppermute | solution.py:68
  109.0 12.9 %collective-permute-start.20 = (f32[16,16]{0,1:T(8,128)S(1)}, f32[16,16]{0,1:T(8,128)S(1)}, u32[]{:S(2)}, u32[]{:S(2)}) collective-permute-start(f32[16,16]{0,1:T(8,128)S(1)} %add.145), channel_id=1, source_target_pairs={{0,16},{4,20},{8,24},{12,28},{16,0},{20,4},{24,8},{28,12},{1,17},{... | collective-permute-start | bytes 3080 | tf_op jit(solution)/shard_map/ppermute | solution.py:68
  111.6 11.8 %collective-permute-start.21 = (f32[16,1,32,128]{3,2,1,0:T(8,128)}, f32[16,1,32,128]{3,2,1,0:T(8,128)S(1)}, u32[]{:S(2)}, u32[]{:S(2)}) collective-permute-start(f32[16,1,32,128]{3,2,1,0:T(8,128)} %get-tuple-element.13), channel_id=1, source_target_pairs={{4,0},{8,4},{12,8},{16,12},{20,16},{24,20},{28,24},{5,1},{9,5},{13... | collective-permute-start | bytes 786440 | tf_op jit(solution)/shard_map/ppermute | solution.py:19
  112.9 11.3 %collective-permute-start.22 = (f32[16,1,32,128]{3,2,1,0:T(8,128)}, f32[16,1,32,128]{3,2,1,0:T(8,128)S(1)}, u32[]{:S(2)}, u32[]{:S(2)}) collective-permute-start(f32[16,1,32,128]{3,2,1,0:T(8,128)} %get-tuple-element.12), channel_id=1, source_target_pairs={{0,4},{4,8},{8,12},{12,16},{16,20},{20,24},{24,28},{1,5},{5,9},{9,... | collective-permute-start | bytes 786440 | tf_op jit(solution)/shard_map/ppermute | solution.py:18
  117.5 7.1 %collective-permute-start.23 = (f32[16,8,1,128]{3,2,1,0:T(1,128)S(1)}, f32[16,8,1,128]{3,2,1,0:T(1,128)S(1)}, u32[]{:S(2)}, u32[]{:S(2)}) collective-permute-start(f32[16,8,1,128]{3,2,1,0:T(1,128)S(1)} %get-tuple-element.10), channel_id=1, source_target_pairs={{1,0},{2,1},{3,2},{5,4},{6,5},{7,6},{9,8},{10,9},{11,10},{13,12},{... | collective-permute-start | bytes 196616 | tf_op jit(solution)/shard_map/ppermute | solution.py:19
  118.8 5.8 %collective-permute-start.24 = (f32[16,8,1,128]{3,2,1,0:T(1,128)S(1)}, f32[16,8,1,128]{3,2,1,0:T(1,128)S(1)}, u32[]{:S(2)}, u32[]{:S(2)}) collective-permute-start(f32[16,8,1,128]{3,2,1,0:T(1,128)S(1)} %get-tuple-element.11), channel_id=1, source_target_pairs={{0,1},{1,2},{2,3},{4,5},{5,6},{6,7},{8,9},{9,10},{10,11},{12,13},{... | collective-permute-start | bytes 196616 | tf_op jit(solution)/shard_map/ppermute | solution.py:18
  141.5 6.1 %collective-permute-start.28 = (f32[16,16]{0,1:T(8,128)S(1)}, f32[16,16]{0,1:T(8,128)S(1)}, u32[]{:S(2)}, u32[]{:S(2)}) collective-permute-start(f32[16,16]{0,1:T(8,128)S(1)} %add.153), channel_id=1, source_target_pairs={{0,8},{4,12},{8,0},{12,4},{16,24},{20,28},{24,16},{28,20},{1,9},{5... | collective-permute-start | bytes 3080 | tf_op jit(solution)/shard_map/ppermute | solution.py:68
  147.6 4.6 %collective-permute-start.29 = (f32[16,16]{0,1:T(8,128)S(1)}, f32[16,16]{0,1:T(8,128)S(1)}, u32[]{:S(2)}, u32[]{:S(2)}) collective-permute-start(f32[16,16]{0,1:T(8,128)S(1)} %add.154), channel_id=1, source_target_pairs={{0,16},{4,20},{8,24},{12,28},{16,0},{20,4},{24,8},{28,12},{1,17},{... | collective-permute-start | bytes 3080 | tf_op jit(solution)/shard_map/ppermute | solution.py:68
  (20 other events, 90.1 us)

commit v2 on v0

--- a/solution.py
+++ b/solution.py
@@ -56,6 +56,18 @@
 def operate(block, fields_one):
     padded = padded_2(block, (("gx", 1), ("gy", 2)), 1)
     return stencil(padded, fields_one)
+
+
+def boundary_faces(fields_one):
+    wet, along_x, along_y = fields_one[0], fields_one[1], fields_one[2]
+    rows = wet.shape[0] - 2
+    cols = wet.shape[1] - 2
+    return (
+        along_x[0:1, 1:-1] * wet[0:1, 1:-1] * wet[1:2, 1:-1],
+        along_x[rows : rows + 1, 1:-1] * wet[rows : rows + 1, 1:-1] * wet[rows + 1 :, 1:-1],
+        along_y[1:-1, 0:1] * wet[1:-1, 0:1] * wet[1:-1, 1:2],
+        along_y[1:-1, cols : cols + 1] * wet[1:-1, cols : cols + 1] * wet[1:-1, cols + 1 :],
+    )
 
 
 def reduce_all(value):
@@ -135,8 +147,27 @@
     gram_sum = reduce_all(inner_products(flattened, flattened)) / cell_total
     inverse = triangle_inverse(gram_sum, vectors)
     basis_rows = combine(inverse, flattened)
-    raw_images = operate(field, fields_one).reshape(vectors, -1)
-    mixed_sum = reduce_all(inner_products(flattened, raw_images)) / cell_total
+    low_x, high_x = halo_pair(field, "gx", 1)
+    low_y, high_y = halo_pair(field, "gy", 2)
+    zero_halo = jnp.pad(field, ((0, 0), (1, 1), (1, 1), (0, 0)))
+    mixed_local = inner_products(
+        flattened, stencil(zero_halo, fields_one).reshape(vectors, -1)
+    )
+    face_lx, face_hx, face_ly, face_hy = boundary_faces(fields_one)
+    for outer, face, halo in (
+        (field[:, 0:1], face_lx, low_x),
+        (field[:, rows - 1 : rows], face_hx, high_x),
+        (field[:, :, 0:1], face_ly, low_y),
+        (field[:, :, cols - 1 : cols], face_hy, high_y),
+    ):
+        mixed_local = mixed_local - inner_products(
+            outer.reshape(vectors, -1), (face * halo).reshape(vectors, -1)
+        )
+    mixed_sum = reduce_all(mixed_local) / cell_total
+    block = jnp.concatenate([low_x, field, high_x], axis=1)
+    ring = ((0, 0), (1, 1), (0, 0), (0, 0))
+    padded = jnp.concatenate([jnp.pad(low_y, ring), block, jnp.pad(high_y, ring)], axis=2)
+    raw_images = stencil(padded, fields_one).reshape(vectors, -1)
     projected = jnp.einsum(
         "ka,ab,lb->kl", inverse, mixed_sum, inverse, precision=lax.Precision.HIGHEST
     )

time: 154 us -> 167 us (1.084)
  waiting for transfers between devices: 31.8 us -> 39.8 us
  local copies, waits for them, and re-layouts: 7.59 us -> 14.7 us
  starting transfers between devices: 67.9 us -> 61.9 us
  other arithmetic: 27.6 us -> 30.7 us
    ppermute x2, waiting for transfers between devices: 0.01 us -> 3.42 us  [on_device(): lax.ppermute(to_low, axis, backward)]
    ppermute x8, starting transfers between devices: 32 us -> 29.2 us  [halo_pair(): lax.ppermute(lax.slice_in_dim(block, block.shape[dim] - 1, None, axis=dim...]
    ppermute x10, waiting for transfers between devices: 6.75 us -> 9.46 us  [reduce_all(): value = value + lax.ppermute(value, axis, pairs)]
    another operation x1, local copies, waits for them, and re-layouts: 0.01 us -> 2.37 us  [on_device(): jnp.stack([ocean_cells, conduct_x, conduct_y, conduct_z, diag_shift])]
    div x0 -> x1, local copies, waits for them, and re-layouts: none -> 1.96 us  [on_device(): (2.0 * (operate(middle, fields_one) - FILTER_CENTRE * middle) / FILTER_HA...]
    unnamed x27 -> x24, local copies, waits for them, and re-layouts: 5.45 us -> 6.52 us
    dot_general x2 -> x6, matrix products: 8.14 us -> 7.57 us  [inner_products(): return jnp.einsum('kc,lc->kl', left, right, precision=lax.Precision.HIGHEST)]
  transfers between devices with their start and end apart: 30 -> 30, of which waited for: 13 -> 13; matrix products, arithmetic and copies ran while one was open for 12% -> 14% of each run, Pallas kernels for 0% -> 0%
where the time goes in v2:
time: 167 us; the launch traced here: 166 us
  starting transfers between devices  61.9 us (37%)
  waiting for transfers between devices  39.8 us (24%)
  other arithmetic  30.7 us (18%)
  matrix products  17.4 us (10%)
  local copies, waits for them, and re-layouts  14.7 us (9%)
    ppermute x8, starting transfers between devices, halo_pair(): lax.ppermute(lax.slice_in_dim(block, block.shape[dim] - 1, None, axis=dim...  29.2 us
    ppermute x8, waiting for transfers between devices, halo_pair(): lax.ppermute(lax.slice_in_dim(block, block.shape[dim] - 1, None, axis=dim...  16.6 us
    ppermute x10, starting transfers between devices, reduce_all(): value = value + lax.ppermute(value, axis, pairs)  13.4 us
    ppermute x8, starting transfers between devices, halo_pair(): high = lax.ppermute(lax.slice_in_dim(block, 0, 1, axis=dim), axis, backward)  10.3 us
    ppermute x10, waiting for transfers between devices, reduce_all(): value = value + lax.ppermute(value, axis, pairs)  9.46 us
    dot_general x3, matrix products, combine(): jnp.einsum('kl,lc->kc', matrix, rows, precision=lax.Precision.HIGHEST)  9.28 us
    ppermute x2, waiting for transfers between devices, on_device(): lax.ppermute(to_high, axis, forward)  9.13 us
    dot_general x6, matrix products, inner_products(): return jnp.einsum('kc,lc->kl', left, right, precision=lax.Precision.HIGHEST)  7.57 us
  transfers between devices with their start and end apart: 30, of which 13 were waited for; matrix products, arithmetic and copies ran while one was open for 14% of the time, Pallas kernels for 0%

profile of v2, /device:TPU:0, one launch (start us, length us, event | category | flops | bytes accessed | tf_op | source)
XLA Modules:
  0.0 165.8 jit_solution(1005387272671224711)
XLA Ops:
  1.5 2.9 %copy_multiply_fusion = f32[16,8,32,128]{3,0,2,1:T(8,128)S(1)} fusion(f32[16,8,32,128]{3,2,1,0:T(8,128)} %param.6, f32[8,32,128]{2,1,0:T(8,128)S(1)} %convert_element_type.34), kind=kLoop, calls=%fused_computation.134 | loop fusion | flops 524288 | bytes 4325376 | tf_op jit(solution)/shard_map/mul | solution.py:110
  8.6 4.9 %collective-permute-start.1 = (f32[21,1,32,128]{3,0,2,1:T(8,128)S(1)}, f32[21,1,32,128]{3,0,2,1:T(8,128)S(1)}, u32[]{:S(2)}, u32[]{:S(2)}) collective-permute-start(f32[21,1,32,128]{3,0,2,1:T(8,128)S(1)} %pad_maximum_fusion.20), channel_id=1, source_target_pairs={{0,4},{4,8},{8,12},{12,16},{16,20},{20,24},{24,28},{1,5},{5,9},{9,... | collective-permute-start | bytes 1032200 | tf_op jit(solution)/shard_map/ppermute | solution.py:125
  17.7 3.4 %collective-permute-done.3 = f32[21,8,1,128]{3,0,2,1:T(8,128)S(1)} collective-permute-done((f32[21,8,1,128]{3,0,2,1:T(8,128)S(1)}, f32[21,8,1,128]{3,0,2,1:T(8,128)S(1)}, u32[]{:S(2)}, u32[]{:S(2)}) %collective-permute-start.3) | collective-permute-done | bytes 86048 | tf_op jit(solution)/shard_map/ppermute | solution.py:125
  21.1 9.1 %collective-permute-done.1 = f32[21,1,32,128]{3,0,2,1:T(8,128)S(1)} collective-permute-done((f32[21,1,32,128]{3,0,2,1:T(8,128)S(1)}, f32[21,1,32,128]{3,0,2,1:T(8,128)S(1)}, u32[]{:S(2)}, u32[]{:S(2)}) %collective-permute-start.1) | collective-permute-done | bytes 344096 | tf_op jit(solution)/shard_map/ppermute | solution.py:125
  34.6 2.7 %broadcast_multiply_fusion.3 = (f32[16,8,32,128]{3,0,2,1:T(8,128)S(1)}, f32[16,8,32,128]{3,0,2,1:T(8,128)S(1)}) fusion(f32[16,8,32,127]{3,0,2,1:T(8,128)S(1)} %fusion.71, f32[16,8,33,128]{3,0,2,1:T(8,128)S(1)} %fusion.27, f32[16,9,32,128]{3,0,2,1:T(8,128)S(1)} %fusion.2, f32[8,32,128]{2,1,0:T(8,128)S(1)} %get-tuple-element.49, ...), kind=kLoop, calls=%fused_computation.156 | loop fusion | flops 6291456 | bytes 17154048 | tf_op jit(solution)/shard_map/div | solution.py:142
  38.7 5.0 %collective-permute-start.5 = (f32[16,1,32,128]{3,0,2,1:T(8,128)S(1)}, f32[16,1,32,128]{3,0,2,1:T(8,128)S(1)}, u32[]{:S(2)}, u32[]{:S(2)}) collective-permute-start(f32[16,1,32,128]{3,0,2,1:T(8,128)S(1)} %get-tuple-element.28), channel_id=1, source_target_pairs={{0,4},{4,8},{8,12},{12,16},{16,20},{20,24},{24,28},{1,5},{5,9},{9,... | collective-permute-start | bytes 786440 | tf_op jit(solution)/shard_map/ppermute | solution.py:18
  45.0 3.0 %collective-permute-start.7 = (f32[16,8,1,128]{3,0,2,1:T(8,128)S(1)}, f32[16,8,1,128]{3,0,2,1:T(8,128)S(1)}, u32[]{:S(2)}, u32[]{:S(2)}) collective-permute-start(f32[16,8,1,128]{3,0,2,1:T(8,128)S(1)} %get-tuple-element.27), channel_id=1, source_target_pairs={{0,1},{1,2},{2,3},{4,5},{5,6},{6,7},{8,9},{9,10},{10,11},{12,13},{... | collective-permute-start | bytes 196616 | tf_op jit(solution)/shard_map/ppermute | solution.py:18
  48.7 5.0 %collective-permute-done.5 = f32[16,1,32,128]{3,0,2,1:T(8,128)S(1)} collective-permute-done((f32[16,1,32,128]{3,0,2,1:T(8,128)S(1)}, f32[16,1,32,128]{3,0,2,1:T(8,128)S(1)}, u32[]{:S(2)}, u32[]{:S(2)}) %collective-permute-start.5) | collective-permute-done | bytes 262176 | tf_op jit(solution)/shard_map/ppermute | solution.py:18
  54.4 3.4 %broadcast_multiply_fusion.1 = (f32[16,8,32,128]{3,0,2,1:T(8,128)S(1)}, f32[16,8,32,128]{3,0,2,1:T(8,128)S(1)}) fusion(f32[16,8,32,128]{3,0,2,1:T(8,128)S(1)} %get-tuple-element.9, f32[16,8,32,127]{3,0,2,1:T(8,128)S(1)} %fusion.63, f32[16,8,33,128]{3,0,2,1:T(8,128)S(1)} %fusion.23, f32[16,9,32,128]{3,0,2,1:T(8,128)S(1)} %fusion.3, ...), kind=kLoop, calls=%fused_computation.153 | loop fusion | flops 7340032 | bytes 19251200 | tf_op jit(solution)/shard_map/div | solution.py:143
  59.2 5.0 %collective-permute-start.9 = (f32[16,1,32,128]{3,0,2,1:T(8,128)S(1)}, f32[16,1,32,128]{3,0,2,1:T(8,128)S(1)}, u32[]{:S(2)}, u32[]{:S(2)}) collective-permute-start(f32[16,1,32,128]{3,0,2,1:T(8,128)S(1)} %get-tuple-element.24), channel_id=1, source_target_pairs={{0,4},{4,8},{8,12},{12,16},{16,20},{20,24},{24,28},{1,5},{5,9},{9,... | collective-permute-start | bytes 786440 | tf_op jit(solution)/shard_map/ppermute | solution.py:18
  65.5 3.0 %collective-permute-start.11 = (f32[16,8,1,128]{3,0,2,1:T(8,128)S(1)}, f32[16,8,1,128]{3,0,2,1:T(8,128)S(1)}, u32[]{:S(2)}, u32[]{:S(2)}) collective-permute-start(f32[16,8,1,128]{3,0,2,1:T(8,128)S(1)} %get-tuple-element.23), channel_id=1, source_target_pairs={{0,1},{1,2},{2,3},{4,5},{5,6},{6,7},{8,9},{9,10},{10,11},{12,13},{... | collective-permute-start | bytes 196616 | tf_op jit(solution)/shard_map/ppermute | solution.py:18
  69.3 5.3 %collective-permute-done.9 = f32[16,1,32,128]{3,0,2,1:T(8,128)S(1)} collective-permute-done((f32[16,1,32,128]{3,0,2,1:T(8,128)S(1)}, f32[16,1,32,128]{3,0,2,1:T(8,128)S(1)}, u32[]{:S(2)}, u32[]{:S(2)}) %collective-permute-start.9) | collective-permute-done | bytes 262176 | tf_op jit(solution)/shard_map/ppermute | solution.py:18
  78.2 5.0 %collective-permute-start.13 = (f32[16,1,32,128]{3,0,2,1:T(8,128)S(1)}, f32[16,1,32,128]{3,0,2,1:T(8,128)S(1)}, u32[]{:S(2)}, u32[]{:S(2)}) collective-permute-start(f32[16,1,32,128]{3,0,2,1:T(8,128)S(1)} %get-tuple-element.20), channel_id=1, source_target_pairs={{0,4},{4,8},{8,12},{12,16},{16,20},{20,24},{24,28},{1,5},{5,9},{9,... | collective-permute-start | bytes 786440 | tf_op jit(solution)/shard_map/ppermute | solution.py:18
  84.5 3.2 %collective-permute-start.15 = (f32[16,8,1,128]{3,0,2,1:T(8,128)S(1)}, f32[16,8,1,128]{3,0,2,1:T(8,128)S(1)}, u32[]{:S(2)}, u32[]{:S(2)}) collective-permute-start(f32[16,8,1,128]{3,0,2,1:T(8,128)S(1)} %get-tuple-element.19), channel_id=1, source_target_pairs={{0,1},{1,2},{2,3},{4,5},{5,6},{6,7},{8,9},{9,10},{10,11},{12,13},{... | collective-permute-start | bytes 196616 | tf_op jit(solution)/shard_map/ppermute | solution.py:18
  88.4 5.1 %collective-permute-done.13 = f32[16,1,32,128]{3,0,2,1:T(8,128)S(1)} collective-permute-done((f32[16,1,32,128]{3,0,2,1:T(8,128)S(1)}, f32[16,1,32,128]{3,0,2,1:T(8,128)S(1)}, u32[]{:S(2)}, u32[]{:S(2)}) %collective-permute-start.13) | collective-permute-done | bytes 262176 | tf_op jit(solution)/shard_map/ppermute | solution.py:18
  96.1 2.9 %convolution_bitcast_fusion.2 = f32[16,16]{0,1:T(8,128)S(1)} fusion(f32[16,8,32,128]{3,0,2,1:T(8,128)S(1)} %get-tuple-element.3), kind=kOutput, calls=%fused_computation.145 | convolution fusion | flops 101187584 | bytes 2098176 | tf_op jit(solution)/shard_map/kc,lc->kl/dot_general | solution.py:86
  103.8 2.5 %collective-permute-start.18 = (f32[16,16]{0,1:T(8,128)S(1)}, f32[16,16]{0,1:T(8,128)S(1)}, u32[]{:S(2)}, u32[]{:S(2)}) collective-permute-start(f32[16,16]{0,1:T(8,128)S(1)} %add.154), channel_id=1, source_target_pairs={{0,4},{4,0},{8,12},{12,8},{16,20},{20,16},{24,28},{28,24},{1,5},{5... | collective-permute-start | bytes 3080 | tf_op jit(solution)/shard_map/ppermute | solution.py:80
  112.0 2.6 %collective-permute-start.20 = (f32[16,16]{0,1:T(8,128)S(1)}, f32[16,16]{0,1:T(8,128)S(1)}, u32[]{:S(2)}, u32[]{:S(2)}) collective-permute-start(f32[16,16]{0,1:T(8,128)S(1)} %add.156), channel_id=1, source_target_pairs={{0,16},{4,20},{8,24},{12,28},{16,0},{20,4},{24,8},{28,12},{1,17},{... | collective-permute-start | bytes 3080 | tf_op jit(solution)/shard_map/ppermute | solution.py:80
  116.6 3.5 %collective-permute-start.22 = (f32[16,1,32,128]{3,0,2,1:T(8,128)}, f32[16,1,32,128]{3,0,2,1:T(8,128)S(1)}, u32[]{:S(2)}, u32[]{:S(2)}) collective-permute-start(f32[16,1,32,128]{3,0,2,1:T(8,128)} %get-tuple-element.16), channel_id=1, source_target_pairs={{0,4},{4,8},{8,12},{12,16},{16,20},{20,24},{24,28},{1,5},{5,9},{9,... | collective-permute-start | bytes 786440 | tf_op jit(solution)/shard_map/ppermute | solution.py:18
  133.8 3.4 %fusion.91 = f32[16,16]{0,1:T(8,128)S(1)} fusion(f32[16,16]{0,1:T(8,128)S(1)} %convolution_bitcast_fusion, f32[16,16]{0,1:T(8,128)S(1)} %convolution_bitcast_fusion.1, f32[16,16]{0,1:T(8,128)S(1)} %convolution_bitcast_fusion.3, f32[16,16]{0,1:T(8,128)S(1)} %convolution_bitcast_fusion.4, f32[16,8,33,128]{3,0,2,1:T(8,128)S(1)} %get-tuple-element.10, ...), kind=kOutput, calls=%fused_computation.151 | convolution fusion | flops 105382912 | bytes 14976000 | tf_op jit(solution)/shard_map/kc,lc->kl/dot_general | solution.py:86
  141.6 3.0 %collective-permute-done.26 = f32[16,16]{0,1:T(8,128)S(1)} collective-permute-done((f32[16,16]{0,1:T(8,128)S(1)}, f32[16,16]{0,1:T(8,128)S(1)}, u32[]{:S(2)}, u32[]{:S(2)}) %collective-permute-start.26) | collective-permute-done | bytes 1056 | tf_op jit(solution)/shard_map/ppermute | solution.py:80
  144.6 2.6 %collective-permute-start.27 = (f32[16,16]{0,1:T(8,128)S(1)}, f32[16,16]{0,1:T(8,128)S(1)}, u32[]{:S(2)}, u32[]{:S(2)}) collective-permute-start(f32[16,16]{0,1:T(8,128)S(1)} %add.166), channel_id=1, source_target_pairs={{0,4},{4,0},{8,12},{12,8},{16,20},{20,16},{24,28},{28,24},{1,5},{5... | collective-permute-start | bytes 3080 | tf_op jit(solution)/shard_map/ppermute | solution.py:80
  147.3 4.5 %fusion.32 = f32[16,32768]{1,0:T(8,128)S(1)} fusion(f32[16,16]{1,0:T(8,128)S(1)} %fusion.115, f32[2,8,256,128]{3,2,1,0:T(8,128)} %bitcast.102), kind=kOutput, calls=%fused_computation.74 | convolution fusion | flops 100663296 | bytes 4195328 | tf_op jit(solution)/shard_map/kl,lc->kc/dot_general | solution.py:90
  157.5 2.8 %fusion.29 = f32[16,32768]{1,0:T(8,128)S(1)} fusion(f32[16,16]{1,0:T(8,128)S(1)} %fusion.115, f32[2,8,256,128]{3,2,1,0:T(8,128)S(1)} %bitcast.103), kind=kOutput, calls=%fused_computation.71 | convolution fusion | flops 100663296 | bytes 4195328 | tf_op jit(solution)/shard_map/kl,lc->kc/dot_general | solution.py:90
  (149 shorter events, 70.2 us)
Async XLA Ops:
  8.6 21.7 %collective-permute-start.1 = (f32[21,1,32,128]{3,0,2,1:T(8,128)S(1)}, f32[21,1,32,128]{3,0,2,1:T(8,128)S(1)}, u32[]{:S(2)}, u32[]{:S(2)}) collective-permute-start(f32[21,1,32,128]{3,0,2,1:T(8,128)S(1)} %pad_maximum_fusion.20), channel_id=1, source_target_pairs={{0,4},{4,8},{8,12},{12,16},{16,20},{20,24},{24,28},{1,5},{5,9},{9,... | collective-permute-start | bytes 1032200 | tf_op jit(solution)/shard_map/ppermute | solution.py:125
  13.5 16.7 %collective-permute-start.2 = (f32[21,1,32,128]{3,0,2,1:T(8,128)S(1)}, f32[21,1,32,128]{3,0,2,1:T(8,128)S(1)}, u32[]{:S(2)}, u32[]{:S(2)}) collective-permute-start(f32[21,1,32,128]{3,0,2,1:T(8,128)S(1)} %pad_maximum_fusion.21), channel_id=1, source_target_pairs={{4,0},{8,4},{12,8},{16,12},{20,16},{24,20},{28,24},{5,1},{9,5},{13... | collective-permute-start | bytes 1032200 | tf_op jit(solution)/shard_map/ppermute | solution.py:125
  16.4 4.7 %collective-permute-start.3 = (f32[21,8,1,128]{3,0,2,1:T(8,128)S(1)}, f32[21,8,1,128]{3,0,2,1:T(8,128)S(1)}, u32[]{:S(2)}, u32[]{:S(2)}) collective-permute-start(f32[21,8,1,128]{3,0,2,1:T(8,128)S(1)} %pad_maximum_fusion.23), channel_id=1, source_target_pairs={{1,0},{2,1},{3,2},{5,4},{6,5},{7,6},{9,8},{10,9},{11,10},{13,12},{... | collective-permute-start | bytes 258056 | tf_op jit(solution)/shard_map/ppermute | solution.py:125
  37.4 11.3 %collective-permute-start.4 = (f32[16,1,32,128]{3,0,2,1:T(8,128)S(1)}, f32[16,1,32,128]{3,0,2,1:T(8,128)S(1)}, u32[]{:S(2)}, u32[]{:S(2)}) collective-permute-start(f32[16,1,32,128]{3,0,2,1:T(8,128)S(1)} %get-tuple-element.29), channel_id=1, source_target_pairs={{4,0},{8,4},{12,8},{16,12},{20,16},{24,20},{28,24},{5,1},{9,5},{13... | collective-permute-start | bytes 786440 | tf_op jit(solution)/shard_map/ppermute | solution.py:19
  38.7 15.1 %collective-permute-start.5 = (f32[16,1,32,128]{3,0,2,1:T(8,128)S(1)}, f32[16,1,32,128]{3,0,2,1:T(8,128)S(1)}, u32[]{:S(2)}, u32[]{:S(2)}) collective-permute-start(f32[16,1,32,128]{3,0,2,1:T(8,128)S(1)} %get-tuple-element.28), channel_id=1, source_target_pairs={{0,4},{4,8},{8,12},{12,16},{16,20},{20,24},{24,28},{1,5},{5,9},{9,... | collective-permute-start | bytes 786440 | tf_op jit(solution)/shard_map/ppermute | solution.py:18
  43.7 10.4 %collective-permute-start.6 = (f32[16,8,1,128]{3,0,2,1:T(8,128)S(1)}, f32[16,8,1,128]{3,0,2,1:T(8,128)S(1)}, u32[]{:S(2)}, u32[]{:S(2)}) collective-permute-start(f32[16,8,1,128]{3,0,2,1:T(8,128)S(1)} %get-tuple-element.26), channel_id=1, source_target_pairs={{1,0},{2,1},{3,2},{5,4},{6,5},{7,6},{9,8},{10,9},{11,10},{13,12},{... | collective-permute-start | bytes 196616 | tf_op jit(solution)/shard_map/ppermute | solution.py:19
  45.0 9.1 %collective-permute-start.7 = (f32[16,8,1,128]{3,0,2,1:T(8,128)S(1)}, f32[16,8,1,128]{3,0,2,1:T(8,128)S(1)}, u32[]{:S(2)}, u32[]{:S(2)}) collective-permute-start(f32[16,8,1,128]{3,0,2,1:T(8,128)S(1)} %get-tuple-element.27), channel_id=1, source_target_pairs={{0,1},{1,2},{2,3},{4,5},{5,6},{6,7},{8,9},{9,10},{10,11},{12,13},{... | collective-permute-start | bytes 196616 | tf_op jit(solution)/shard_map/ppermute | solution.py:18
  57.9 11.3 %collective-permute-start.8 = (f32[16,1,32,128]{3,0,2,1:T(8,128)S(1)}, f32[16,1,32,128]{3,0,2,1:T(8,128)S(1)}, u32[]{:S(2)}, u32[]{:S(2)}) collective-permute-start(f32[16,1,32,128]{3,0,2,1:T(8,128)S(1)} %get-tuple-element.25), channel_id=1, source_target_pairs={{4,0},{8,4},{12,8},{16,12},{20,16},{24,20},{28,24},{5,1},{9,5},{13... | collective-permute-start | bytes 786440 | tf_op jit(solution)/shard_map/ppermute | solution.py:19
  59.2 15.3 %collective-permute-start.9 = (f32[16,1,32,128]{3,0,2,1:T(8,128)S(1)}, f32[16,1,32,128]{3,0,2,1:T(8,128)S(1)}, u32[]{:S(2)}, u32[]{:S(2)}) collective-permute-start(f32[16,1,32,128]{3,0,2,1:T(8,128)S(1)} %get-tuple-element.24), channel_id=1, source_target_pairs={{0,4},{4,8},{8,12},{12,16},{16,20},{20,24},{24,28},{1,5},{5,9},{9,... | collective-permute-start | bytes 786440 | tf_op jit(solution)/shard_map/ppermute | solution.py:18
  64.2 10.6 %collective-permute-start.10 = (f32[16,8,1,128]{3,0,2,1:T(8,128)S(1)}, f32[16,8,1,128]{3,0,2,1:T(8,128)S(1)}, u32[]{:S(2)}, u32[]{:S(2)}) collective-permute-start(f32[16,8,1,128]{3,0,2,1:T(8,128)S(1)} %get-tuple-element.22), channel_id=1, source_target_pairs={{1,0},{2,1},{3,2},{5,4},{6,5},{7,6},{9,8},{10,9},{11,10},{13,12},{... | collective-permute-start | bytes 196616 | tf_op jit(solution)/shard_map/ppermute | solution.py:19
  65.5 9.3 %collective-permute-start.11 = (f32[16,8,1,128]{3,0,2,1:T(8,128)S(1)}, f32[16,8,1,128]{3,0,2,1:T(8,128)S(1)}, u32[]{:S(2)}, u32[]{:S(2)}) collective-permute-start(f32[16,8,1,128]{3,0,2,1:T(8,128)S(1)} %get-tuple-element.23), channel_id=1, source_target_pairs={{0,1},{1,2},{2,3},{4,5},{5,6},{6,7},{8,9},{9,10},{10,11},{12,13},{... | collective-permute-start | bytes 196616 | tf_op jit(solution)/shard_map/ppermute | solution.py:18
  76.9 11.5 %collective-permute-start.12 = (f32[16,1,32,128]{3,0,2,1:T(8,128)S(1)}, f32[16,1,32,128]{3,0,2,1:T(8,128)S(1)}, u32[]{:S(2)}, u32[]{:S(2)}) collective-permute-start(f32[16,1,32,128]{3,0,2,1:T(8,128)S(1)} %get-tuple-element.21), channel_id=1, source_target_pairs={{4,0},{8,4},{12,8},{16,12},{20,16},{24,20},{28,24},{5,1},{9,5},{13... | collective-permute-start | bytes 786440 | tf_op jit(solution)/shard_map/ppermute | solution.py:19
  78.2 15.3 %collective-permute-start.13 = (f32[16,1,32,128]{3,0,2,1:T(8,128)S(1)}, f32[16,1,32,128]{3,0,2,1:T(8,128)S(1)}, u32[]{:S(2)}, u32[]{:S(2)}) collective-permute-start(f32[16,1,32,128]{3,0,2,1:T(8,128)S(1)} %get-tuple-element.20), channel_id=1, source_target_pairs={{0,4},{4,8},{8,12},{12,16},{16,20},{20,24},{24,28},{1,5},{5,9},{9,... | collective-permute-start | bytes 786440 | tf_op jit(solution)/shard_map/ppermute | solution.py:18
  83.2 10.7 %collective-permute-start.14 = (f32[16,8,1,128]{3,0,2,1:T(8,128)S(1)}, f32[16,8,1,128]{3,0,2,1:T(8,128)S(1)}, u32[]{:S(2)}, u32[]{:S(2)}) collective-permute-start(f32[16,8,1,128]{3,0,2,1:T(8,128)S(1)} %get-tuple-element.18), channel_id=1, source_target_pairs={{1,0},{2,1},{3,2},{5,4},{6,5},{7,6},{9,8},{10,9},{11,10},{13,12},{... | collective-permute-start | bytes 196616 | tf_op jit(solution)/shard_map/ppermute | solution.py:19
  84.5 9.4 %collective-permute-start.15 = (f32[16,8,1,128]{3,0,2,1:T(8,128)S(1)}, f32[16,8,1,128]{3,0,2,1:T(8,128)S(1)}, u32[]{:S(2)}, u32[]{:S(2)}) collective-permute-start(f32[16,8,1,128]{3,0,2,1:T(8,128)S(1)} %get-tuple-element.19), channel_id=1, source_target_pairs={{0,1},{1,2},{2,3},{4,5},{5,6},{6,7},{8,9},{9,10},{10,11},{12,13},{... | collective-permute-start | bytes 196616 | tf_op jit(solution)/shard_map/ppermute | solution.py:18
  103.8 4.5 %collective-permute-start.18 = (f32[16,16]{0,1:T(8,128)S(1)}, f32[16,16]{0,1:T(8,128)S(1)}, u32[]{:S(2)}, u32[]{:S(2)}) collective-permute-start(f32[16,16]{0,1:T(8,128)S(1)} %add.154), channel_id=1, source_target_pairs={{0,4},{4,0},{8,12},{12,8},{16,20},{20,16},{24,28},{28,24},{1,5},{5... | collective-permute-start | bytes 3080 | tf_op jit(solution)/shard_map/ppermute | solution.py:80
  108.3 3.7 %collective-permute-start.19 = (f32[16,16]{0,1:T(8,128)S(1)}, f32[16,16]{0,1:T(8,128)S(1)}, u32[]{:S(2)}, u32[]{:S(2)}) collective-permute-start(f32[16,16]{0,1:T(8,128)S(1)} %add.155), channel_id=1, source_target_pairs={{0,8},{4,12},{8,0},{12,4},{16,24},{20,28},{24,16},{28,20},{1,9},{5... | collective-permute-start | bytes 3080 | tf_op jit(solution)/shard_map/ppermute | solution.py:80
  112.0 12.0 %collective-permute-start.20 = (f32[16,16]{0,1:T(8,128)S(1)}, f32[16,16]{0,1:T(8,128)S(1)}, u32[]{:S(2)}, u32[]{:S(2)}) collective-permute-start(f32[16,16]{0,1:T(8,128)S(1)} %add.156), channel_id=1, source_target_pairs={{0,16},{4,20},{8,24},{12,28},{16,0},{20,4},{24,8},{28,12},{1,17},{... | collective-permute-start | bytes 3080 | tf_op jit(solution)/shard_map/ppermute | solution.py:80
  116.6 12.3 %collective-permute-start.22 = (f32[16,1,32,128]{3,0,2,1:T(8,128)}, f32[16,1,32,128]{3,0,2,1:T(8,128)S(1)}, u32[]{:S(2)}, u32[]{:S(2)}) collective-permute-start(f32[16,1,32,128]{3,0,2,1:T(8,128)} %get-tuple-element.16), channel_id=1, source_target_pairs={{0,4},{4,8},{8,12},{12,16},{16,20},{20,24},{24,28},{1,5},{5,9},{9,... | collective-permute-start | bytes 786440 | tf_op jit(solution)/shard_map/ppermute | solution.py:18
  120.1 8.8 %collective-permute-start.21 = (f32[16,1,32,128]{3,0,2,1:T(8,128)}, f32[16,1,32,128]{3,0,2,1:T(8,128)S(1)}, u32[]{:S(2)}, u32[]{:S(2)}) collective-permute-start(f32[16,1,32,128]{3,0,2,1:T(8,128)} %get-tuple-element.17), channel_id=1, source_target_pairs={{4,0},{8,4},{12,8},{16,12},{20,16},{24,20},{28,24},{5,1},{9,5},{13... | collective-permute-start | bytes 786440 | tf_op jit(solution)/shard_map/ppermute | solution.py:19
  121.4 4.8 %collective-permute-start.24 = (f32[16,8,1,128]{3,0,2,1:T(8,128)S(1)}, f32[16,8,1,128]{3,0,2,1:T(8,128)S(1)}, u32[]{:S(2)}, u32[]{:S(2)}) collective-permute-start(f32[16,8,1,128]{3,0,2,1:T(8,128)S(1)} %get-tuple-element.15), channel_id=1, source_target_pairs={{0,1},{1,2},{2,3},{4,5},{5,6},{6,7},{8,9},{9,10},{10,11},{12,13},{... | collective-permute-start | bytes 196616 | tf_op jit(solution)/shard_map/ppermute | solution.py:18
  122.7 4.9 %collective-permute-start.23 = (f32[16,8,1,128]{3,0,2,1:T(8,128)S(1)}, f32[16,8,1,128]{3,0,2,1:T(8,128)S(1)}, u32[]{:S(2)}, u32[]{:S(2)}) collective-permute-start(f32[16,8,1,128]{3,0,2,1:T(8,128)S(1)} %get-tuple-element.14), channel_id=1, source_target_pairs={{1,0},{2,1},{3,2},{5,4},{6,5},{7,6},{9,8},{10,9},{11,10},{13,12},{... | collective-permute-start | bytes 196616 | tf_op jit(solution)/shard_map/ppermute | solution.py:19
  144.6 8.9 %collective-permute-start.27 = (f32[16,16]{0,1:T(8,128)S(1)}, f32[16,16]{0,1:T(8,128)S(1)}, u32[]{:S(2)}, u32[]{:S(2)}) collective-permute-start(f32[16,16]{0,1:T(8,128)S(1)} %add.166), channel_id=1, source_target_pairs={{0,4},{4,0},{8,12},{12,8},{16,20},{20,16},{24,28},{28,24},{1,5},{5... | collective-permute-start | bytes 3080 | tf_op jit(solution)/shard_map/ppermute | solution.py:80
  157.2 4.5 %collective-permute-start.29 = (f32[16,16]{0,1:T(8,128)S(1)}, f32[16,16]{0,1:T(8,128)S(1)}, u32[]{:S(2)}, u32[]{:S(2)}) collective-permute-start(f32[16,16]{0,1:T(8,128)S(1)} %add.168), channel_id=1, source_target_pairs={{0,16},{4,20},{8,24},{12,28},{16,0},{20,4},{24,8},{28,12},{1,17},{... | collective-permute-start | bytes 3080 | tf_op jit(solution)/shard_map/ppermute | solution.py:80
  (18 other events, 94.2 us)

commit v3 on v0

--- a/solution.py
+++ b/solution.py
@@ -132,10 +132,16 @@
             2.0 * (operate(middle, fields_one) - FILTER_CENTRE * middle) / FILTER_HALF - field
         ) / FILTER_NORM
     flattened = field.reshape(vectors, -1)
-    gram_sum = reduce_all(inner_products(flattened, flattened)) / cell_total
+    low_x, high_x = halo_pair(field, "gx", 1)
+    low_y, high_y = halo_pair(field, "gy", 2)
+    tie = 0.0 * (low_y[0, 0, 0, 0] + high_y[0, 0, 0, 0])
+    gram_sum = reduce_all(inner_products(flattened, flattened) + tie) / cell_total
     inverse = triangle_inverse(gram_sum, vectors)
     basis_rows = combine(inverse, flattened)
-    raw_images = operate(field, fields_one).reshape(vectors, -1)
+    block = jnp.concatenate([low_x, field, high_x], axis=1)
+    ring = ((0, 0), (1, 1), (0, 0), (0, 0))
+    padded = jnp.concatenate([jnp.pad(low_y, ring), block, jnp.pad(high_y, ring)], axis=2)
+    raw_images = stencil(padded, fields_one).reshape(vectors, -1)
     mixed_sum = reduce_all(inner_products(flattened, raw_images)) / cell_total
     projected = jnp.einsum(
         "ka,ab,lb->kl", inverse, mixed_sum, inverse, precision=lax.Precision.HIGHEST

time: 154 us -> 165 us (1.071)
  waiting for transfers between devices: 31.8 us -> 42 us
    ppermute x8, waiting for transfers between devices: 16.4 us -> 20.2 us  [halo_pair(): lax.ppermute(lax.slice_in_dim(block, block.shape[dim] - 1, None, axis=dim...]
    ppermute x8, waiting for transfers between devices: 0.02 us -> 3.44 us  [halo_pair(): high = lax.ppermute(lax.slice_in_dim(block, 0, 1, axis=dim), axis, backward)]
    ppermute x10, waiting for transfers between devices: 6.75 us -> 9.7 us  [reduce_all(): value = value + lax.ppermute(value, axis, pairs)]
  transfers between devices with their start and end apart: 30 -> 30, of which waited for: 13 -> 16; matrix products, arithmetic and copies ran while one was open for 12% -> 11% of each run, Pallas kernels for 0% -> 0%
where the time goes in v3:
time: 165 us; the launch traced here: 164 us
  starting transfers between devices  66.8 us (40%)
  waiting for transfers between devices  42 us (25%)
  other arithmetic  27.6 us (17%)
  matrix products  16.6 us (10%)
  local copies, waits for them, and re-layouts  8.7 us (5%)
  between operations  2.74 us (2%)
    ppermute x8, starting transfers between devices, halo_pair(): lax.ppermute(lax.slice_in_dim(block, block.shape[dim] - 1, None, axis=dim...  30.9 us
    ppermute x8, waiting for transfers between devices, halo_pair(): lax.ppermute(lax.slice_in_dim(block, block.shape[dim] - 1, None, axis=dim...  20.2 us
    ppermute x10, starting transfers between devices, reduce_all(): value = value + lax.ppermute(value, axis, pairs)  15.1 us
    ppermute x8, starting transfers between devices, halo_pair(): high = lax.ppermute(lax.slice_in_dim(block, 0, 1, axis=dim), axis, backward)  10.3 us
    ppermute x10, waiting for transfers between devices, reduce_all(): value = value + lax.ppermute(value, axis, pairs)  9.7 us
    ppermute x2, waiting for transfers between devices, on_device(): lax.ppermute(to_high, axis, forward)  8.63 us
    dot_general x2, matrix products, inner_products(): return jnp.einsum('kc,lc->kl', left, right, precision=lax.Precision.HIGHEST)  8.15 us
    ppermute x2, starting transfers between devices, on_device(): lax.ppermute(to_high, axis, forward)  7.93 us
  transfers between devices with their start and end apart: 30, of which 16 were waited for; matrix products, arithmetic and copies ran while one was open for 11% of the time, Pallas kernels for 0%

profile of v3, /device:TPU:0, one launch (start us, length us, event | category | flops | bytes accessed | tf_op | source)
XLA Modules:
  0.0 164.4 jit_solution(2117662556099583651)
XLA Ops:
  4.7 4.9 %collective-permute-start.1 = (f32[21,1,32,128]{3,2,1,0:T(8,128)S(1)}, f32[21,1,32,128]{3,2,1,0:T(8,128)S(1)}, u32[]{:S(2)}, u32[]{:S(2)}) collective-permute-start(f32[21,1,32,128]{3,2,1,0:T(8,128)S(1)} %pad_maximum_fusion.20), channel_id=1, source_target_pairs={{0,4},{4,8},{8,12},{12,16},{16,20},{20,24},{24,28},{1,5},{5,9},{9,... | collective-permute-start | bytes 1032200 | tf_op jit(solution)/shard_map/ppermute | solution.py:113
  12.5 3.0 %collective-permute-start = (f32[21,8,1,128]{3,2,1,0:T(1,128)S(1)}, f32[21,8,1,128]{3,2,1,0:T(1,128)S(1)}, u32[]{:S(2)}, u32[]{:S(2)}) collective-permute-start(f32[21,8,1,128]{3,2,1,0:T(1,128)S(1)} %pad_maximum_fusion.22), channel_id=1, source_target_pairs={{0,1},{1,2},{2,3},{4,5},{5,6},{6,7},{8,9},{9,10},{10,11},{12,13},{... | collective-permute-start | bytes 258056 | tf_op jit(solution)/shard_map/ppermute | solution.py:113
  16.5 7.8 %collective-permute-done.1 = f32[21,1,32,128]{3,2,1,0:T(8,128)S(1)} collective-permute-done((f32[21,1,32,128]{3,2,1,0:T(8,128)S(1)}, f32[21,1,32,128]{3,2,1,0:T(8,128)S(1)}, u32[]{:S(2)}, u32[]{:S(2)}) %collective-permute-start.1) | collective-permute-done | bytes 344096 | tf_op jit(solution)/shard_map/ppermute | solution.py:113
  30.8 5.0 %collective-permute-start.5 = (f32[16,1,32,128]{3,2,1,0:T(8,128)S(1)}, f32[16,1,32,128]{3,2,1,0:T(8,128)S(1)}, u32[]{:S(2)}, u32[]{:S(2)}) collective-permute-start(f32[16,1,32,128]{3,2,1,0:T(8,128)S(1)} %get-tuple-element.24), channel_id=1, source_target_pairs={{0,4},{4,8},{8,12},{12,16},{16,20},{20,24},{24,28},{1,5},{5,9},{9,... | collective-permute-start | bytes 786440 | tf_op jit(solution)/shard_map/ppermute | solution.py:18
  37.1 3.0 %collective-permute-start.7 = (f32[16,8,1,128]{3,2,1,0:T(1,128)S(1)}, f32[16,8,1,128]{3,2,1,0:T(1,128)S(1)}, u32[]{:S(2)}, u32[]{:S(2)}) collective-permute-start(f32[16,8,1,128]{3,2,1,0:T(1,128)S(1)} %get-tuple-element.23), channel_id=1, source_target_pairs={{0,1},{1,2},{2,3},{4,5},{5,6},{6,7},{8,9},{9,10},{10,11},{12,13},{... | collective-permute-start | bytes 196616 | tf_op jit(solution)/shard_map/ppermute | solution.py:18
  40.8 5.1 %collective-permute-done.5 = f32[16,1,32,128]{3,2,1,0:T(8,128)S(1)} collective-permute-done((f32[16,1,32,128]{3,2,1,0:T(8,128)S(1)}, f32[16,1,32,128]{3,2,1,0:T(8,128)S(1)}, u32[]{:S(2)}, u32[]{:S(2)}) %collective-permute-start.5) | collective-permute-done | bytes 262176 | tf_op jit(solution)/shard_map/ppermute | solution.py:18
  50.4 5.0 %collective-permute-start.9 = (f32[16,1,32,128]{3,2,1,0:T(8,128)S(1)}, f32[16,1,32,128]{3,2,1,0:T(8,128)S(1)}, u32[]{:S(2)}, u32[]{:S(2)}) collective-permute-start(f32[16,1,32,128]{3,2,1,0:T(8,128)S(1)} %get-tuple-element.20), channel_id=1, source_target_pairs={{0,4},{4,8},{8,12},{12,16},{16,20},{20,24},{24,28},{1,5},{5,9},{9,... | collective-permute-start | bytes 786440 | tf_op jit(solution)/shard_map/ppermute | solution.py:18
  56.7 3.0 %collective-permute-start.11 = (f32[16,8,1,128]{3,2,1,0:T(1,128)S(1)}, f32[16,8,1,128]{3,2,1,0:T(1,128)S(1)}, u32[]{:S(2)}, u32[]{:S(2)}) collective-permute-start(f32[16,8,1,128]{3,2,1,0:T(1,128)S(1)} %get-tuple-element.19), channel_id=1, source_target_pairs={{0,1},{1,2},{2,3},{4,5},{5,6},{6,7},{8,9},{9,10},{10,11},{12,13},{... | collective-permute-start | bytes 196616 | tf_op jit(solution)/shard_map/ppermute | solution.py:18
  60.4 5.3 %collective-permute-done.9 = f32[16,1,32,128]{3,2,1,0:T(8,128)S(1)} collective-permute-done((f32[16,1,32,128]{3,2,1,0:T(8,128)S(1)}, f32[16,1,32,128]{3,2,1,0:T(8,128)S(1)}, u32[]{:S(2)}, u32[]{:S(2)}) %collective-permute-start.9) | collective-permute-done | bytes 262176 | tf_op jit(solution)/shard_map/ppermute | solution.py:18
  69.8 5.0 %collective-permute-start.13 = (f32[16,1,32,128]{3,2,1,0:T(8,128)S(1)}, f32[16,1,32,128]{3,2,1,0:T(8,128)S(1)}, u32[]{:S(2)}, u32[]{:S(2)}) collective-permute-start(f32[16,1,32,128]{3,2,1,0:T(8,128)S(1)} %get-tuple-element.16), channel_id=1, source_target_pairs={{0,4},{4,8},{8,12},{12,16},{16,20},{20,24},{24,28},{1,5},{5,9},{9,... | collective-permute-start | bytes 786440 | tf_op jit(solution)/shard_map/ppermute | solution.py:18
  76.1 3.2 %collective-permute-start.15 = (f32[16,8,1,128]{3,2,1,0:T(1,128)S(1)}, f32[16,8,1,128]{3,2,1,0:T(1,128)S(1)}, u32[]{:S(2)}, u32[]{:S(2)}) collective-permute-start(f32[16,8,1,128]{3,2,1,0:T(1,128)S(1)} %get-tuple-element.15), channel_id=1, source_target_pairs={{0,1},{1,2},{2,3},{4,5},{5,6},{6,7},{8,9},{9,10},{10,11},{12,13},{... | collective-permute-start | bytes 196616 | tf_op jit(solution)/shard_map/ppermute | solution.py:18
  80.0 5.2 %collective-permute-done.13 = f32[16,1,32,128]{3,2,1,0:T(8,128)S(1)} collective-permute-done((f32[16,1,32,128]{3,2,1,0:T(8,128)S(1)}, f32[16,1,32,128]{3,2,1,0:T(8,128)S(1)}, u32[]{:S(2)}, u32[]{:S(2)}) %collective-permute-start.13) | collective-permute-done | bytes 262176 | tf_op jit(solution)/shard_map/ppermute | solution.py:18
  86.4 2.7 %broadcast_multiply_fusion = (f32[16,8,32,128]{3,2,1,0:T(8,128)S(1)}, f32[16,8,32,128]{3,2,1,0:T(8,128)}) fusion(f32[16,8,32,128]{3,2,1,0:T(8,128)S(1)} %get-tuple-element.7, f32[16,8,32,128]{3,2,1,0:T(8,128)S(1)} %get-tuple-element.5, f32[16,8,32,127]{3,2,1,0:T(8,128)S(1)} %fusion.36, f32[16,8,33,128]{3,2,1,0:T(8,128)S(1)} %fusion.6, ...), kind=kLoop, calls=%fused_computation.126 | loop fusion | flops 7340032 | bytes 19120128 | tf_op jit(solution)/shard_map/div | solution.py:131
  93.0 2.4 %collective-permute-done.17 = f32[16,8,1,128]{3,2,1,0:T(1,128)S(1)} collective-permute-done((f32[16,8,1,128]{3,2,1,0:T(1,128)S(1)}, f32[16,8,1,128]{3,2,1,0:T(1,128)S(1)}, u32[]{:S(2)}, u32[]{:S(2)}) %collective-permute-start.17) | collective-permute-done | bytes 65568 | tf_op jit(solution)/shard_map/ppermute | solution.py:19
  97.3 3.6 %fusion.78 = f32[16,16]{0,1:T(8,128)S(1)} fusion(f32[16,8,32,128]{3,2,1,0:T(8,128)S(1)} %get-tuple-element.2, f32[]{:T(128)} %bitcast.11), kind=kOutput, calls=%fused_computation.125 | convolution fusion | flops 100663552 | bytes 2098180 | tf_op jit(solution)/shard_map/kc,lc->kl/dot_general | solution.py:74
  100.9 3.0 %collective-permute-start.18 = (f32[16,16]{0,1:T(8,128)S(1)}, f32[16,16]{0,1:T(8,128)S(1)}, u32[]{:S(2)}, u32[]{:S(2)}) collective-permute-start(f32[16,16]{0,1:T(8,128)S(1)} %fusion.78), channel_id=1, source_target_pairs={{0,1},{1,0},{2,3},{3,2},{4,5},{5,4},{6,7},{7,6},{8,9},{9,8},{10,11... | collective-permute-start | bytes 3080 | tf_op jit(solution)/shard_map/ppermute | solution.py:68
  104.9 3.5 %collective-permute-done.19 = f32[16,16]{0,1:T(8,128)S(1)} collective-permute-done((f32[16,16]{0,1:T(8,128)S(1)}, f32[16,16]{0,1:T(8,128)S(1)}, u32[]{:S(2)}, u32[]{:S(2)}) %collective-permute-start.19) | collective-permute-done | bytes 1056 | tf_op jit(solution)/shard_map/ppermute | solution.py:68
  108.4 2.5 %collective-permute-start.20 = (f32[16,16]{0,1:T(8,128)S(1)}, f32[16,16]{0,1:T(8,128)S(1)}, u32[]{:S(2)}, u32[]{:S(2)}) collective-permute-start(f32[16,16]{0,1:T(8,128)S(1)} %add.156), channel_id=1, source_target_pairs={{0,4},{4,0},{8,12},{12,8},{16,20},{20,16},{24,28},{28,24},{1,5},{5... | collective-permute-start | bytes 3080 | tf_op jit(solution)/shard_map/ppermute | solution.py:68
  116.1 2.6 %collective-permute-start.22 = (f32[16,16]{0,1:T(8,128)S(1)}, f32[16,16]{0,1:T(8,128)S(1)}, u32[]{:S(2)}, u32[]{:S(2)}) collective-permute-start(f32[16,16]{0,1:T(8,128)S(1)} %add.158), channel_id=1, source_target_pairs={{0,16},{4,20},{8,24},{12,28},{16,0},{20,4},{24,8},{28,12},{1,17},{... | collective-permute-start | bytes 3080 | tf_op jit(solution)/shard_map/ppermute | solution.py:68
  120.8 4.6 %collective-permute-start.24 = (f32[16,1,32,128]{3,2,1,0:T(8,128)}, f32[16,1,32,128]{3,2,1,0:T(8,128)S(1)}, u32[]{:S(2)}, u32[]{:S(2)}) collective-permute-start(f32[16,1,32,128]{3,2,1,0:T(8,128)} %get-tuple-element.10), channel_id=1, source_target_pairs={{0,4},{4,8},{8,12},{12,16},{16,20},{20,24},{24,28},{1,5},{5,9},{9,... | collective-permute-start | bytes 786440 | tf_op jit(solution)/shard_map/ppermute | solution.py:18
  128.0 4.6 %collective-permute-done.24 = f32[16,1,32,128]{3,2,1,0:T(8,128)S(1)} collective-permute-done((f32[16,1,32,128]{3,2,1,0:T(8,128)}, f32[16,1,32,128]{3,2,1,0:T(8,128)S(1)}, u32[]{:S(2)}, u32[]{:S(2)}) %collective-permute-start.24) | collective-permute-done | bytes 262176 | tf_op jit(solution)/shard_map/ppermute | solution.py:18
  136.5 4.5 %fusion.73 = f32[16,16]{0,1:T(8,128)S(1)} fusion(f32[16,8,32,128]{3,2,1,0:T(8,128)S(1)} %fusion.34, f32[16,8,32,128]{3,2,1,0:T(8,128)S(1)} %get-tuple-element.2), kind=kOutput, calls=%fused_computation.124 | convolution fusion | flops 100663296 | bytes 4195328 | tf_op jit(solution)/shard_map/kc,lc->kl/dot_general | solution.py:74
  151.2 2.8 %fusion.28 = f32[16,32768]{1,0:T(8,128)S(1)} fusion(f32[16,16]{1,0:T(8,128)S(1)} %fusion.82, f32[2,8,256,128]{3,2,1,0:T(8,128)S(1)} %bitcast.62), kind=kOutput, calls=%fused_computation.66 | convolution fusion | flops 100663296 | bytes 4195328 | tf_op jit(solution)/shard_map/kl,lc->kc/dot_general | solution.py:78
  157.1 3.1 %fusion.25 = f32[16,32768]{1,0:T(8,128)S(1)} fusion(f32[16,16]{1,0:T(8,128)S(1)} %fusion.82, f32[2,8,256,128]{3,2,1,0:T(8,128)S(1)} %bitcast.63), kind=kOutput, calls=%fused_computation.63 | convolution fusion | flops 100663296 | bytes 4195328 | tf_op jit(solution)/shard_map/kl,lc->kc/dot_general | solution.py:78
  (146 shorter events, 66.1 us)
Async XLA Ops:
  4.7 19.6 %collective-permute-start.1 = (f32[21,1,32,128]{3,2,1,0:T(8,128)S(1)}, f32[21,1,32,128]{3,2,1,0:T(8,128)S(1)}, u32[]{:S(2)}, u32[]{:S(2)}) collective-permute-start(f32[21,1,32,128]{3,2,1,0:T(8,128)S(1)} %pad_maximum_fusion.20), channel_id=1, source_target_pairs={{0,4},{4,8},{8,12},{12,16},{16,20},{20,24},{24,28},{1,5},{5,9},{9,... | collective-permute-start | bytes 1032200 | tf_op jit(solution)/shard_map/ppermute | solution.py:113
  9.6 14.6 %collective-permute-start.2 = (f32[21,1,32,128]{3,2,1,0:T(8,128)S(1)}, f32[21,1,32,128]{3,2,1,0:T(8,128)S(1)}, u32[]{:S(2)}, u32[]{:S(2)}) collective-permute-start(f32[21,1,32,128]{3,2,1,0:T(8,128)S(1)} %pad_maximum_fusion.21), channel_id=1, source_target_pairs={{4,0},{8,4},{12,8},{16,12},{20,16},{24,20},{28,24},{5,1},{9,5},{13... | collective-permute-start | bytes 1032200 | tf_op jit(solution)/shard_map/ppermute | solution.py:113
  11.1 4.4 %collective-permute-start.3 = (f32[21,8,1,128]{3,2,1,0:T(1,128)S(1)}, f32[21,8,1,128]{3,2,1,0:T(1,128)S(1)}, u32[]{:S(2)}, u32[]{:S(2)}) collective-permute-start(f32[21,8,1,128]{3,2,1,0:T(1,128)S(1)} %pad_maximum_fusion.23), channel_id=1, source_target_pairs={{1,0},{2,1},{3,2},{5,4},{6,5},{7,6},{9,8},{10,9},{11,10},{13,12},{... | collective-permute-start | bytes 258056 | tf_op jit(solution)/shard_map/ppermute | solution.py:113
  12.5 3.9 %collective-permute-start = (f32[21,8,1,128]{3,2,1,0:T(1,128)S(1)}, f32[21,8,1,128]{3,2,1,0:T(1,128)S(1)}, u32[]{:S(2)}, u32[]{:S(2)}) collective-permute-start(f32[21,8,1,128]{3,2,1,0:T(1,128)S(1)} %pad_maximum_fusion.22), channel_id=1, source_target_pairs={{0,1},{1,2},{2,3},{4,5},{5,6},{6,7},{8,9},{9,10},{10,11},{12,13},{... | collective-permute-start | bytes 258056 | tf_op jit(solution)/shard_map/ppermute | solution.py:113
  29.5 11.3 %collective-permute-start.4 = (f32[16,1,32,128]{3,2,1,0:T(8,128)S(1)}, f32[16,1,32,128]{3,2,1,0:T(8,128)S(1)}, u32[]{:S(2)}, u32[]{:S(2)}) collective-permute-start(f32[16,1,32,128]{3,2,1,0:T(8,128)S(1)} %get-tuple-element.25), channel_id=1, source_target_pairs={{4,0},{8,4},{12,8},{16,12},{20,16},{24,20},{28,24},{5,1},{9,5},{13... | collective-permute-start | bytes 786440 | tf_op jit(solution)/shard_map/ppermute | solution.py:19
  30.8 15.1 %collective-permute-start.5 = (f32[16,1,32,128]{3,2,1,0:T(8,128)S(1)}, f32[16,1,32,128]{3,2,1,0:T(8,128)S(1)}, u32[]{:S(2)}, u32[]{:S(2)}) collective-permute-start(f32[16,1,32,128]{3,2,1,0:T(8,128)S(1)} %get-tuple-element.24), channel_id=1, source_target_pairs={{0,4},{4,8},{8,12},{12,16},{16,20},{20,24},{24,28},{1,5},{5,9},{9,... | collective-permute-start | bytes 786440 | tf_op jit(solution)/shard_map/ppermute | solution.py:18
  35.8 10.4 %collective-permute-start.6 = (f32[16,8,1,128]{3,2,1,0:T(1,128)S(1)}, f32[16,8,1,128]{3,2,1,0:T(1,128)S(1)}, u32[]{:S(2)}, u32[]{:S(2)}) collective-permute-start(f32[16,8,1,128]{3,2,1,0:T(1,128)S(1)} %get-tuple-element.22), channel_id=1, source_target_pairs={{1,0},{2,1},{3,2},{5,4},{6,5},{7,6},{9,8},{10,9},{11,10},{13,12},{... | collective-permute-start | bytes 196616 | tf_op jit(solution)/shard_map/ppermute | solution.py:19
  37.1 9.1 %collective-permute-start.7 = (f32[16,8,1,128]{3,2,1,0:T(1,128)S(1)}, f32[16,8,1,128]{3,2,1,0:T(1,128)S(1)}, u32[]{:S(2)}, u32[]{:S(2)}) collective-permute-start(f32[16,8,1,128]{3,2,1,0:T(1,128)S(1)} %get-tuple-element.23), channel_id=1, source_target_pairs={{0,1},{1,2},{2,3},{4,5},{5,6},{6,7},{8,9},{9,10},{10,11},{12,13},{... | collective-permute-start | bytes 196616 | tf_op jit(solution)/shard_map/ppermute | solution.py:18
  49.1 11.3 %collective-permute-start.8 = (f32[16,1,32,128]{3,2,1,0:T(8,128)S(1)}, f32[16,1,32,128]{3,2,1,0:T(8,128)S(1)}, u32[]{:S(2)}, u32[]{:S(2)}) collective-permute-start(f32[16,1,32,128]{3,2,1,0:T(8,128)S(1)} %get-tuple-element.21), channel_id=1, source_target_pairs={{4,0},{8,4},{12,8},{16,12},{20,16},{24,20},{28,24},{5,1},{9,5},{13... | collective-permute-start | bytes 786440 | tf_op jit(solution)/shard_map/ppermute | solution.py:19
  50.4 15.3 %collective-permute-start.9 = (f32[16,1,32,128]{3,2,1,0:T(8,128)S(1)}, f32[16,1,32,128]{3,2,1,0:T(8,128)S(1)}, u32[]{:S(2)}, u32[]{:S(2)}) collective-permute-start(f32[16,1,32,128]{3,2,1,0:T(8,128)S(1)} %get-tuple-element.20), channel_id=1, source_target_pairs={{0,4},{4,8},{8,12},{12,16},{16,20},{20,24},{24,28},{1,5},{5,9},{9,... | collective-permute-start | bytes 786440 | tf_op jit(solution)/shard_map/ppermute | solution.py:18
  55.4 10.6 %collective-permute-start.10 = (f32[16,8,1,128]{3,2,1,0:T(1,128)S(1)}, f32[16,8,1,128]{3,2,1,0:T(1,128)S(1)}, u32[]{:S(2)}, u32[]{:S(2)}) collective-permute-start(f32[16,8,1,128]{3,2,1,0:T(1,128)S(1)} %get-tuple-element.18), channel_id=1, source_target_pairs={{1,0},{2,1},{3,2},{5,4},{6,5},{7,6},{9,8},{10,9},{11,10},{13,12},{... | collective-permute-start | bytes 196616 | tf_op jit(solution)/shard_map/ppermute | solution.py:19
  56.7 9.3 %collective-permute-start.11 = (f32[16,8,1,128]{3,2,1,0:T(1,128)S(1)}, f32[16,8,1,128]{3,2,1,0:T(1,128)S(1)}, u32[]{:S(2)}, u32[]{:S(2)}) collective-permute-start(f32[16,8,1,128]{3,2,1,0:T(1,128)S(1)} %get-tuple-element.19), channel_id=1, source_target_pairs={{0,1},{1,2},{2,3},{4,5},{5,6},{6,7},{8,9},{9,10},{10,11},{12,13},{... | collective-permute-start | bytes 196616 | tf_op jit(solution)/shard_map/ppermute | solution.py:18
  68.5 11.5 %collective-permute-start.12 = (f32[16,1,32,128]{3,2,1,0:T(8,128)S(1)}, f32[16,1,32,128]{3,2,1,0:T(8,128)S(1)}, u32[]{:S(2)}, u32[]{:S(2)}) collective-permute-start(f32[16,1,32,128]{3,2,1,0:T(8,128)S(1)} %get-tuple-element.17), channel_id=1, source_target_pairs={{4,0},{8,4},{12,8},{16,12},{20,16},{24,20},{28,24},{5,1},{9,5},{13... | collective-permute-start | bytes 786440 | tf_op jit(solution)/shard_map/ppermute | solution.py:19
  69.8 15.3 %collective-permute-start.13 = (f32[16,1,32,128]{3,2,1,0:T(8,128)S(1)}, f32[16,1,32,128]{3,2,1,0:T(8,128)S(1)}, u32[]{:S(2)}, u32[]{:S(2)}) collective-permute-start(f32[16,1,32,128]{3,2,1,0:T(8,128)S(1)} %get-tuple-element.16), channel_id=1, source_target_pairs={{0,4},{4,8},{8,12},{12,16},{16,20},{20,24},{24,28},{1,5},{5,9},{9,... | collective-permute-start | bytes 786440 | tf_op jit(solution)/shard_map/ppermute | solution.py:18
  74.8 10.7 %collective-permute-start.14 = (f32[16,8,1,128]{3,2,1,0:T(1,128)S(1)}, f32[16,8,1,128]{3,2,1,0:T(1,128)S(1)}, u32[]{:S(2)}, u32[]{:S(2)}) collective-permute-start(f32[16,8,1,128]{3,2,1,0:T(1,128)S(1)} %get-tuple-element.14), channel_id=1, source_target_pairs={{1,0},{2,1},{3,2},{5,4},{6,5},{7,6},{9,8},{10,9},{11,10},{13,12},{... | collective-permute-start | bytes 196616 | tf_op jit(solution)/shard_map/ppermute | solution.py:19
  76.1 9.4 %collective-permute-start.15 = (f32[16,8,1,128]{3,2,1,0:T(1,128)S(1)}, f32[16,8,1,128]{3,2,1,0:T(1,128)S(1)}, u32[]{:S(2)}, u32[]{:S(2)}) collective-permute-start(f32[16,8,1,128]{3,2,1,0:T(1,128)S(1)} %get-tuple-element.15), channel_id=1, source_target_pairs={{0,1},{1,2},{2,3},{4,5},{5,6},{6,7},{8,9},{9,10},{10,11},{12,13},{... | collective-permute-start | bytes 196616 | tf_op jit(solution)/shard_map/ppermute | solution.py:18
  91.2 4.2 %collective-permute-start.17 = (f32[16,8,1,128]{3,2,1,0:T(1,128)S(1)}, f32[16,8,1,128]{3,2,1,0:T(1,128)S(1)}, u32[]{:S(2)}, u32[]{:S(2)}) collective-permute-start(f32[16,8,1,128]{3,2,1,0:T(1,128)S(1)} %get-tuple-element.12), channel_id=1, source_target_pairs={{1,0},{2,1},{3,2},{5,4},{6,5},{7,6},{9,8},{10,9},{11,10},{13,12},{... | collective-permute-start | bytes 196616 | tf_op jit(solution)/shard_map/ppermute | solution.py:19
  108.4 4.1 %collective-permute-start.20 = (f32[16,16]{0,1:T(8,128)S(1)}, f32[16,16]{0,1:T(8,128)S(1)}, u32[]{:S(2)}, u32[]{:S(2)}) collective-permute-start(f32[16,16]{0,1:T(8,128)S(1)} %add.156), channel_id=1, source_target_pairs={{0,4},{4,0},{8,12},{12,8},{16,20},{20,16},{24,28},{28,24},{1,5},{5... | collective-permute-start | bytes 3080 | tf_op jit(solution)/shard_map/ppermute | solution.py:68
  116.1 9.3 %collective-permute-start.22 = (f32[16,16]{0,1:T(8,128)S(1)}, f32[16,16]{0,1:T(8,128)S(1)}, u32[]{:S(2)}, u32[]{:S(2)}) collective-permute-start(f32[16,16]{0,1:T(8,128)S(1)} %add.158), channel_id=1, source_target_pairs={{0,16},{4,20},{8,24},{12,28},{16,0},{20,4},{24,8},{28,12},{1,17},{... | collective-permute-start | bytes 3080 | tf_op jit(solution)/shard_map/ppermute | solution.py:68
  119.5 8.5 %collective-permute-start.23 = (f32[16,1,32,128]{3,2,1,0:T(8,128)}, f32[16,1,32,128]{3,2,1,0:T(8,128)S(1)}, u32[]{:S(2)}, u32[]{:S(2)}) collective-permute-start(f32[16,1,32,128]{3,2,1,0:T(8,128)} %get-tuple-element.11), channel_id=1, source_target_pairs={{4,0},{8,4},{12,8},{16,12},{20,16},{24,20},{28,24},{5,1},{9,5},{13... | collective-permute-start | bytes 786440 | tf_op jit(solution)/shard_map/ppermute | solution.py:19
  120.8 11.8 %collective-permute-start.24 = (f32[16,1,32,128]{3,2,1,0:T(8,128)}, f32[16,1,32,128]{3,2,1,0:T(8,128)S(1)}, u32[]{:S(2)}, u32[]{:S(2)}) collective-permute-start(f32[16,1,32,128]{3,2,1,0:T(8,128)} %get-tuple-element.10), channel_id=1, source_target_pairs={{0,4},{4,8},{8,12},{12,16},{16,20},{20,24},{24,28},{1,5},{5,9},{9,... | collective-permute-start | bytes 786440 | tf_op jit(solution)/shard_map/ppermute | solution.py:18
  145.9 4.0 %collective-permute-start.27 = (f32[16,16]{0,1:T(8,128)S(1)}, f32[16,16]{0,1:T(8,128)S(1)}, u32[]{:S(2)}, u32[]{:S(2)}) collective-permute-start(f32[16,16]{0,1:T(8,128)S(1)} %add.165), channel_id=1, source_target_pairs={{0,4},{4,0},{8,12},{12,8},{16,20},{20,16},{24,28},{28,24},{1,5},{5... | collective-permute-start | bytes 3080 | tf_op jit(solution)/shard_map/ppermute | solution.py:68
  149.9 5.9 %collective-permute-start.28 = (f32[16,16]{0,1:T(8,128)S(1)}, f32[16,16]{0,1:T(8,128)S(1)}, u32[]{:S(2)}, u32[]{:S(2)}) collective-permute-start(f32[16,16]{0,1:T(8,128)S(1)} %add.166), channel_id=1, source_target_pairs={{0,8},{4,12},{8,0},{12,4},{16,24},{20,28},{24,16},{28,20},{1,9},{5... | collective-permute-start | bytes 3080 | tf_op jit(solution)/shard_map/ppermute | solution.py:68
  155.8 4.6 %collective-permute-start.29 = (f32[16,16]{0,1:T(8,128)S(1)}, f32[16,16]{0,1:T(8,128)S(1)}, u32[]{:S(2)}, u32[]{:S(2)}) collective-permute-start(f32[16,16]{0,1:T(8,128)S(1)} %add.167), channel_id=1, source_target_pairs={{0,16},{4,20},{8,24},{12,28},{16,0},{20,4},{24,8},{28,12},{1,17},{... | collective-permute-start | bytes 3080 | tf_op jit(solution)/shard_map/ppermute | solution.py:68
  (19 other events, 59.0 us)

commit v4 on v0

--- a/solution.py
+++ b/solution.py
@@ -71,11 +71,11 @@
 
 
 def inner_products(left, right):
-    return jnp.einsum("kc,lc->kl", left, right, precision=lax.Precision.HIGHEST)
+    return jnp.einsum("kxyz,lxyz->kl", left, right, precision=lax.Precision.HIGHEST)
 
 
 def combine(matrix, rows):
-    return jnp.einsum("kl,lc->kc", matrix, rows, precision=lax.Precision.HIGHEST)
+    return jnp.einsum("kl,lxyz->kxyz", matrix, rows, precision=lax.Precision.HIGHEST)
 
 
 def triangle_inverse(gram_sum, vectors):
@@ -131,17 +131,17 @@
         field = (
             2.0 * (operate(middle, fields_one) - FILTER_CENTRE * middle) / FILTER_HALF - field
         ) / FILTER_NORM
-    flattened = field.reshape(vectors, -1)
+    flattened = field
     gram_sum = reduce_all(inner_products(flattened, flattened)) / cell_total
     inverse = triangle_inverse(gram_sum, vectors)
     basis_rows = combine(inverse, flattened)
-    raw_images = operate(field, fields_one).reshape(vectors, -1)
+    raw_images = operate(field, fields_one)
     mixed_sum = reduce_all(inner_products(flattened, raw_images)) / cell_total
     projected = jnp.einsum(
         "ka,ab,lb->kl", inverse, mixed_sum, inverse, precision=lax.Precision.HIGHEST
     )
     residual = combine(inverse, raw_images) - combine(projected, basis_rows)
-    return (basis_rows.reshape(field.shape), residual.reshape(field.shape))
+    return (basis_rows, residual)
 
 
 def solution(mesh):

time: 154 us -> 156 us (1.013)
  waiting for transfers between devices: 31.8 us -> 34.4 us
    ppermute x10, waiting for transfers between devices: 6.75 us -> 9.38 us  [reduce_all(): value = value + lax.ppermute(value, axis, pairs)]
  transfers between devices with their start and end apart: 30 -> 30, of which waited for: 13 -> 12; matrix products, arithmetic and copies ran while one was open for 12% -> 10% of each run, Pallas kernels for 0% -> 0%
where the time goes in v4:
time: 156 us
  starting transfers between devices  67.6 us (43%)
  waiting for transfers between devices  34.4 us (22%)
  other arithmetic  27.6 us (18%)
  matrix products  16.5 us (11%)
  local copies, waits for them, and re-layouts  8.06 us (5%)
    ppermute x8, starting transfers between devices, halo_pair(): lax.ppermute(lax.slice_in_dim(block, block.shape[dim] - 1, None, axis=dim...  32 us
    ppermute x8, waiting for transfers between devices, halo_pair(): lax.ppermute(lax.slice_in_dim(block, block.shape[dim] - 1, None, axis=dim...  16.4 us
    ppermute x10, starting transfers between devices, reduce_all(): value = value + lax.ppermute(value, axis, pairs)  14.8 us
    ppermute x8, starting transfers between devices, halo_pair(): high = lax.ppermute(lax.slice_in_dim(block, 0, 1, axis=dim), axis, backward)  10.3 us
    ppermute x10, waiting for transfers between devices, reduce_all(): value = value + lax.ppermute(value, axis, pairs)  9.38 us
    ppermute x2, waiting for transfers between devices, on_device(): lax.ppermute(to_high, axis, forward)  8.63 us
    dot_general x2, matrix products, inner_products(): jnp.einsum('kxyz,lxyz->kl', left, right, precision=lax.Precision.HIGHEST)  8.14 us
    ppermute x2, starting transfers between devices, on_device(): lax.ppermute(to_high, axis, forward)  7.93 us
  transfers between devices with their start and end apart: 30, of which 12 were waited for; matrix products, arithmetic and copies ran while one was open for 10% of the time, Pallas kernels for 0%

profile of v4, /device:TPU:0, one launch (start us, length us, event | category | flops | bytes accessed | tf_op | source)
XLA Modules:
  0.0 155.7 jit_solution(5062307811281525865)
XLA Ops:
  4.7 4.9 %collective-permute-start.1 = (f32[21,1,32,128]{3,2,1,0:T(8,128)S(1)}, f32[21,1,32,128]{3,2,1,0:T(8,128)S(1)}, u32[]{:S(2)}, u32[]{:S(2)}) collective-permute-start(f32[21,1,32,128]{3,2,1,0:T(8,128)S(1)} %pad_maximum_fusion.20), channel_id=1, source_target_pairs={{0,4},{4,8},{8,12},{12,16},{16,20},{20,24},{24,28},{1,5},{5,9},{9,... | collective-permute-start | bytes 1032200 | tf_op jit(solution)/shard_map/ppermute | solution.py:113
  12.5 3.0 %collective-permute-start = (f32[21,8,1,128]{3,2,1,0:T(1,128)S(1)}, f32[21,8,1,128]{3,2,1,0:T(1,128)S(1)}, u32[]{:S(2)}, u32[]{:S(2)}) collective-permute-start(f32[21,8,1,128]{3,2,1,0:T(1,128)S(1)} %pad_maximum_fusion.22), channel_id=1, source_target_pairs={{0,1},{1,2},{2,3},{4,5},{5,6},{6,7},{8,9},{9,10},{10,11},{12,13},{... | collective-permute-start | bytes 258056 | tf_op jit(solution)/shard_map/ppermute | solution.py:113
  16.5 7.8 %collective-permute-done.1 = f32[21,1,32,128]{3,2,1,0:T(8,128)S(1)} collective-permute-done((f32[21,1,32,128]{3,2,1,0:T(8,128)S(1)}, f32[21,1,32,128]{3,2,1,0:T(8,128)S(1)}, u32[]{:S(2)}, u32[]{:S(2)}) %collective-permute-start.1) | collective-permute-done | bytes 344096 | tf_op jit(solution)/shard_map/ppermute | solution.py:113
  30.8 5.0 %collective-permute-start.5 = (f32[16,1,32,128]{3,2,1,0:T(8,128)S(1)}, f32[16,1,32,128]{3,2,1,0:T(8,128)S(1)}, u32[]{:S(2)}, u32[]{:S(2)}) collective-permute-start(f32[16,1,32,128]{3,2,1,0:T(8,128)S(1)} %get-tuple-element.26), channel_id=1, source_target_pairs={{0,4},{4,8},{8,12},{12,16},{16,20},{20,24},{24,28},{1,5},{5,9},{9,... | collective-permute-start | bytes 786440 | tf_op jit(solution)/shard_map/ppermute | solution.py:18
  37.1 3.0 %collective-permute-start.7 = (f32[16,8,1,128]{3,2,1,0:T(1,128)S(1)}, f32[16,8,1,128]{3,2,1,0:T(1,128)S(1)}, u32[]{:S(2)}, u32[]{:S(2)}) collective-permute-start(f32[16,8,1,128]{3,2,1,0:T(1,128)S(1)} %get-tuple-element.25), channel_id=1, source_target_pairs={{0,1},{1,2},{2,3},{4,5},{5,6},{6,7},{8,9},{9,10},{10,11},{12,13},{... | collective-permute-start | bytes 196616 | tf_op jit(solution)/shard_map/ppermute | solution.py:18
  40.8 5.1 %collective-permute-done.5 = f32[16,1,32,128]{3,2,1,0:T(8,128)S(1)} collective-permute-done((f32[16,1,32,128]{3,2,1,0:T(8,128)S(1)}, f32[16,1,32,128]{3,2,1,0:T(8,128)S(1)}, u32[]{:S(2)}, u32[]{:S(2)}) %collective-permute-start.5) | collective-permute-done | bytes 262176 | tf_op jit(solution)/shard_map/ppermute | solution.py:18
  50.4 5.0 %collective-permute-start.9 = (f32[16,1,32,128]{3,2,1,0:T(8,128)S(1)}, f32[16,1,32,128]{3,2,1,0:T(8,128)S(1)}, u32[]{:S(2)}, u32[]{:S(2)}) collective-permute-start(f32[16,1,32,128]{3,2,1,0:T(8,128)S(1)} %get-tuple-element.22), channel_id=1, source_target_pairs={{0,4},{4,8},{8,12},{12,16},{16,20},{20,24},{24,28},{1,5},{5,9},{9,... | collective-permute-start | bytes 786440 | tf_op jit(solution)/shard_map/ppermute | solution.py:18
  56.7 3.0 %collective-permute-start.11 = (f32[16,8,1,128]{3,2,1,0:T(1,128)S(1)}, f32[16,8,1,128]{3,2,1,0:T(1,128)S(1)}, u32[]{:S(2)}, u32[]{:S(2)}) collective-permute-start(f32[16,8,1,128]{3,2,1,0:T(1,128)S(1)} %get-tuple-element.21), channel_id=1, source_target_pairs={{0,1},{1,2},{2,3},{4,5},{5,6},{6,7},{8,9},{9,10},{10,11},{12,13},{... | collective-permute-start | bytes 196616 | tf_op jit(solution)/shard_map/ppermute | solution.py:18
  60.4 5.3 %collective-permute-done.9 = f32[16,1,32,128]{3,2,1,0:T(8,128)S(1)} collective-permute-done((f32[16,1,32,128]{3,2,1,0:T(8,128)S(1)}, f32[16,1,32,128]{3,2,1,0:T(8,128)S(1)}, u32[]{:S(2)}, u32[]{:S(2)}) %collective-permute-start.9) | collective-permute-done | bytes 262176 | tf_op jit(solution)/shard_map/ppermute | solution.py:18
  69.8 5.0 %collective-permute-start.13 = (f32[16,1,32,128]{3,2,1,0:T(8,128)S(1)}, f32[16,1,32,128]{3,2,1,0:T(8,128)S(1)}, u32[]{:S(2)}, u32[]{:S(2)}) collective-permute-start(f32[16,1,32,128]{3,2,1,0:T(8,128)S(1)} %get-tuple-element.18), channel_id=1, source_target_pairs={{0,4},{4,8},{8,12},{12,16},{16,20},{20,24},{24,28},{1,5},{5,9},{9,... | collective-permute-start | bytes 786440 | tf_op jit(solution)/shard_map/ppermute | solution.py:18
  76.1 3.2 %collective-permute-start.15 = (f32[16,8,1,128]{3,2,1,0:T(1,128)S(1)}, f32[16,8,1,128]{3,2,1,0:T(1,128)S(1)}, u32[]{:S(2)}, u32[]{:S(2)}) collective-permute-start(f32[16,8,1,128]{3,2,1,0:T(1,128)S(1)} %get-tuple-element.17), channel_id=1, source_target_pairs={{0,1},{1,2},{2,3},{4,5},{5,6},{6,7},{8,9},{9,10},{10,11},{12,13},{... | collective-permute-start | bytes 196616 | tf_op jit(solution)/shard_map/ppermute | solution.py:18
  80.0 5.2 %collective-permute-done.13 = f32[16,1,32,128]{3,2,1,0:T(8,128)S(1)} collective-permute-done((f32[16,1,32,128]{3,2,1,0:T(8,128)S(1)}, f32[16,1,32,128]{3,2,1,0:T(8,128)S(1)}, u32[]{:S(2)}, u32[]{:S(2)}) %collective-permute-start.13) | collective-permute-done | bytes 262176 | tf_op jit(solution)/shard_map/ppermute | solution.py:18
  86.4 2.7 %broadcast_multiply_fusion = (f32[16,8,32,128]{3,2,1,0:T(8,128)S(1)}, f32[16,8,32,128]{3,2,1,0:T(8,128)}) fusion(f32[16,8,32,128]{3,2,1,0:T(8,128)S(1)} %get-tuple-element.9, f32[16,8,32,128]{3,2,1,0:T(8,128)S(1)} %get-tuple-element.7, f32[16,8,32,127]{3,2,1,0:T(8,128)S(1)} %fusion.30, f32[16,8,33,128]{3,2,1,0:T(8,128)S(1)} %fusion.6, ...), kind=kLoop, calls=%fused_computation.123 | loop fusion | flops 7340032 | bytes 19120128 | tf_op jit(solution)/shard_map/div | solution.py:131
  89.2 3.6 %fusion.70 = f32[16,16]{0,1:T(8,128)S(1)} fusion(f32[16,8,32,128]{3,2,1,0:T(8,128)S(1)} %get-tuple-element.4), kind=kOutput, calls=%fused_computation.120 | convolution fusion | flops 100663296 | bytes 2098176 | tf_op jit(solution)/shard_map/kxyz,lxyz->kl/dot_general | solution.py:74
  95.4 2.2 %collective-permute-done.17 = f32[16,16]{0,1:T(8,128)S(1)} collective-permute-done((f32[16,16]{0,1:T(8,128)S(1)}, f32[16,16]{0,1:T(8,128)S(1)}, u32[]{:S(2)}, u32[]{:S(2)}) %collective-permute-start.17) | collective-permute-done | bytes 1056 | tf_op jit(solution)/shard_map/ppermute | solution.py:68
  97.6 2.5 %collective-permute-start.18 = (f32[16,16]{0,1:T(8,128)S(1)}, f32[16,16]{0,1:T(8,128)S(1)}, u32[]{:S(2)}, u32[]{:S(2)}) collective-permute-start(f32[16,16]{0,1:T(8,128)S(1)} %add.143), channel_id=1, source_target_pairs={{0,4},{4,0},{8,12},{12,8},{16,20},{20,16},{24,28},{28,24},{1,5},{5... | collective-permute-start | bytes 3080 | tf_op jit(solution)/shard_map/ppermute | solution.py:68
  105.7 2.6 %collective-permute-start.20 = (f32[16,16]{0,1:T(8,128)S(1)}, f32[16,16]{0,1:T(8,128)S(1)}, u32[]{:S(2)}, u32[]{:S(2)}) collective-permute-start(f32[16,16]{0,1:T(8,128)S(1)} %add.145), channel_id=1, source_target_pairs={{0,16},{4,20},{8,24},{12,28},{16,0},{20,4},{24,8},{28,12},{1,17},{... | collective-permute-start | bytes 3080 | tf_op jit(solution)/shard_map/ppermute | solution.py:68
  109.7 4.6 %collective-permute-start.22 = (f32[16,1,32,128]{3,2,1,0:T(8,128)}, f32[16,1,32,128]{3,2,1,0:T(8,128)S(1)}, u32[]{:S(2)}, u32[]{:S(2)}) collective-permute-start(f32[16,1,32,128]{3,2,1,0:T(8,128)} %get-tuple-element.14), channel_id=1, source_target_pairs={{0,4},{4,8},{8,12},{12,16},{16,20},{20,24},{24,28},{1,5},{5,9},{9,... | collective-permute-start | bytes 786440 | tf_op jit(solution)/shard_map/ppermute | solution.py:18
  115.5 3.0 %collective-permute-start.24 = (f32[16,8,1,128]{3,2,1,0:T(1,128)S(1)}, f32[16,8,1,128]{3,2,1,0:T(1,128)S(1)}, u32[]{:S(2)}, u32[]{:S(2)}) collective-permute-start(f32[16,8,1,128]{3,2,1,0:T(1,128)S(1)} %get-tuple-element.13), channel_id=1, source_target_pairs={{0,1},{1,2},{2,3},{4,5},{5,6},{6,7},{8,9},{9,10},{10,11},{12,13},{... | collective-permute-start | bytes 196616 | tf_op jit(solution)/shard_map/ppermute | solution.py:18
  124.8 4.5 %fusion.73 = f32[16,16]{0,1:T(8,128)S(1)} fusion(f32[16,8,32,128]{3,2,1,0:T(8,128)S(1)} %fusion.28, f32[16,8,32,128]{3,2,1,0:T(8,128)S(1)} %get-tuple-element.4), kind=kOutput, calls=%fused_computation.121 | convolution fusion | flops 100663296 | bytes 4195328 | tf_op jit(solution)/shard_map/kxyz,lxyz->kl/dot_general | solution.py:74
  134.2 2.6 %collective-permute-start.27 = (f32[16,16]{0,1:T(8,128)S(1)}, f32[16,16]{0,1:T(8,128)S(1)}, u32[]{:S(2)}, u32[]{:S(2)}) collective-permute-start(f32[16,16]{0,1:T(8,128)S(1)} %add.152), channel_id=1, source_target_pairs={{0,4},{4,0},{8,12},{12,8},{16,20},{20,16},{24,28},{28,24},{1,5},{5... | collective-permute-start | bytes 3080 | tf_op jit(solution)/shard_map/ppermute | solution.py:68
  139.9 2.4 %collective-permute-done.28 = f32[16,16]{0,1:T(8,128)S(1)} collective-permute-done((f32[16,16]{0,1:T(8,128)S(1)}, f32[16,16]{0,1:T(8,128)S(1)}, u32[]{:S(2)}, u32[]{:S(2)}) %collective-permute-start.28) | collective-permute-done | bytes 1056 | tf_op jit(solution)/shard_map/ppermute | solution.py:68
  143.5 2.8 %fusion.63 = f32[16,8,32,128]{3,0,2,1:T(8,128)S(1)} fusion(f32[16,8,32,128]{3,2,1,0:T(8,128)S(1)} %get-tuple-element.4, f32[16,16]{1,0:T(8,128)S(1)} %fusion.81), kind=kOutput, calls=%fused_computation.115 | convolution fusion | flops 100663296 | bytes 4195328 | tf_op jit(solution)/shard_map/kl,lxyz->kxyz/dot_general | solution.py:78
  150.6 3.1 %fusion.67 = f32[16,8,32,128]{3,0,2,1:T(8,128)S(1)} fusion(f32[16,8,32,128]{3,0,2,1:T(8,128)S(1)} %fusion.105, f32[16,8,32,128]{3,2,1,0:T(8,128)S(1)} %copy-done.1, f32[16,16]{1,0:T(8,128)S(1)} %fusion.81), kind=kOutput, calls=%fused_computation.119 | convolution fusion | flops 101187584 | bytes 6292480 | tf_op jit(solution)/shard_map/kl,lxyz->kxyz/dot_general | solution.py:78
  (144 shorter events, 61.9 us)
Async XLA Ops:
  4.7 19.6 %collective-permute-start.1 = (f32[21,1,32,128]{3,2,1,0:T(8,128)S(1)}, f32[21,1,32,128]{3,2,1,0:T(8,128)S(1)}, u32[]{:S(2)}, u32[]{:S(2)}) collective-permute-start(f32[21,1,32,128]{3,2,1,0:T(8,128)S(1)} %pad_maximum_fusion.20), channel_id=1, source_target_pairs={{0,4},{4,8},{8,12},{12,16},{16,20},{20,24},{24,28},{1,5},{5,9},{9,... | collective-permute-start | bytes 1032200 | tf_op jit(solution)/shard_map/ppermute | solution.py:113
  9.6 14.6 %collective-permute-start.2 = (f32[21,1,32,128]{3,2,1,0:T(8,128)S(1)}, f32[21,1,32,128]{3,2,1,0:T(8,128)S(1)}, u32[]{:S(2)}, u32[]{:S(2)}) collective-permute-start(f32[21,1,32,128]{3,2,1,0:T(8,128)S(1)} %pad_maximum_fusion.21), channel_id=1, source_target_pairs={{4,0},{8,4},{12,8},{16,12},{20,16},{24,20},{28,24},{5,1},{9,5},{13... | collective-permute-start | bytes 1032200 | tf_op jit(solution)/shard_map/ppermute | solution.py:113
  11.1 4.4 %collective-permute-start.3 = (f32[21,8,1,128]{3,2,1,0:T(1,128)S(1)}, f32[21,8,1,128]{3,2,1,0:T(1,128)S(1)}, u32[]{:S(2)}, u32[]{:S(2)}) collective-permute-start(f32[21,8,1,128]{3,2,1,0:T(1,128)S(1)} %pad_maximum_fusion.23), channel_id=1, source_target_pairs={{1,0},{2,1},{3,2},{5,4},{6,5},{7,6},{9,8},{10,9},{11,10},{13,12},{... | collective-permute-start | bytes 258056 | tf_op jit(solution)/shard_map/ppermute | solution.py:113
  12.5 3.9 %collective-permute-start = (f32[21,8,1,128]{3,2,1,0:T(1,128)S(1)}, f32[21,8,1,128]{3,2,1,0:T(1,128)S(1)}, u32[]{:S(2)}, u32[]{:S(2)}) collective-permute-start(f32[21,8,1,128]{3,2,1,0:T(1,128)S(1)} %pad_maximum_fusion.22), channel_id=1, source_target_pairs={{0,1},{1,2},{2,3},{4,5},{5,6},{6,7},{8,9},{9,10},{10,11},{12,13},{... | collective-permute-start | bytes 258056 | tf_op jit(solution)/shard_map/ppermute | solution.py:113
  29.5 11.3 %collective-permute-start.4 = (f32[16,1,32,128]{3,2,1,0:T(8,128)S(1)}, f32[16,1,32,128]{3,2,1,0:T(8,128)S(1)}, u32[]{:S(2)}, u32[]{:S(2)}) collective-permute-start(f32[16,1,32,128]{3,2,1,0:T(8,128)S(1)} %get-tuple-element.27), channel_id=1, source_target_pairs={{4,0},{8,4},{12,8},{16,12},{20,16},{24,20},{28,24},{5,1},{9,5},{13... | collective-permute-start | bytes 786440 | tf_op jit(solution)/shard_map/ppermute | solution.py:19
  30.8 15.1 %collective-permute-start.5 = (f32[16,1,32,128]{3,2,1,0:T(8,128)S(1)}, f32[16,1,32,128]{3,2,1,0:T(8,128)S(1)}, u32[]{:S(2)}, u32[]{:S(2)}) collective-permute-start(f32[16,1,32,128]{3,2,1,0:T(8,128)S(1)} %get-tuple-element.26), channel_id=1, source_target_pairs={{0,4},{4,8},{8,12},{12,16},{16,20},{20,24},{24,28},{1,5},{5,9},{9,... | collective-permute-start | bytes 786440 | tf_op jit(solution)/shard_map/ppermute | solution.py:18
  35.8 10.4 %collective-permute-start.6 = (f32[16,8,1,128]{3,2,1,0:T(1,128)S(1)}, f32[16,8,1,128]{3,2,1,0:T(1,128)S(1)}, u32[]{:S(2)}, u32[]{:S(2)}) collective-permute-start(f32[16,8,1,128]{3,2,1,0:T(1,128)S(1)} %get-tuple-element.24), channel_id=1, source_target_pairs={{1,0},{2,1},{3,2},{5,4},{6,5},{7,6},{9,8},{10,9},{11,10},{13,12},{... | collective-permute-start | bytes 196616 | tf_op jit(solution)/shard_map/ppermute | solution.py:19
  37.1 9.1 %collective-permute-start.7 = (f32[16,8,1,128]{3,2,1,0:T(1,128)S(1)}, f32[16,8,1,128]{3,2,1,0:T(1,128)S(1)}, u32[]{:S(2)}, u32[]{:S(2)}) collective-permute-start(f32[16,8,1,128]{3,2,1,0:T(1,128)S(1)} %get-tuple-element.25), channel_id=1, source_target_pairs={{0,1},{1,2},{2,3},{4,5},{5,6},{6,7},{8,9},{9,10},{10,11},{12,13},{... | collective-permute-start | bytes 196616 | tf_op jit(solution)/shard_map/ppermute | solution.py:18
  49.1 11.3 %collective-permute-start.8 = (f32[16,1,32,128]{3,2,1,0:T(8,128)S(1)}, f32[16,1,32,128]{3,2,1,0:T(8,128)S(1)}, u32[]{:S(2)}, u32[]{:S(2)}) collective-permute-start(f32[16,1,32,128]{3,2,1,0:T(8,128)S(1)} %get-tuple-element.23), channel_id=1, source_target_pairs={{4,0},{8,4},{12,8},{16,12},{20,16},{24,20},{28,24},{5,1},{9,5},{13... | collective-permute-start | bytes 786440 | tf_op jit(solution)/shard_map/ppermute | solution.py:19
  50.4 15.3 %collective-permute-start.9 = (f32[16,1,32,128]{3,2,1,0:T(8,128)S(1)}, f32[16,1,32,128]{3,2,1,0:T(8,128)S(1)}, u32[]{:S(2)}, u32[]{:S(2)}) collective-permute-start(f32[16,1,32,128]{3,2,1,0:T(8,128)S(1)} %get-tuple-element.22), channel_id=1, source_target_pairs={{0,4},{4,8},{8,12},{12,16},{16,20},{20,24},{24,28},{1,5},{5,9},{9,... | collective-permute-start | bytes 786440 | tf_op jit(solution)/shard_map/ppermute | solution.py:18
  55.4 10.6 %collective-permute-start.10 = (f32[16,8,1,128]{3,2,1,0:T(1,128)S(1)}, f32[16,8,1,128]{3,2,1,0:T(1,128)S(1)}, u32[]{:S(2)}, u32[]{:S(2)}) collective-permute-start(f32[16,8,1,128]{3,2,1,0:T(1,128)S(1)} %get-tuple-element.20), channel_id=1, source_target_pairs={{1,0},{2,1},{3,2},{5,4},{6,5},{7,6},{9,8},{10,9},{11,10},{13,12},{... | collective-permute-start | bytes 196616 | tf_op jit(solution)/shard_map/ppermute | solution.py:19
  56.7 9.3 %collective-permute-start.11 = (f32[16,8,1,128]{3,2,1,0:T(1,128)S(1)}, f32[16,8,1,128]{3,2,1,0:T(1,128)S(1)}, u32[]{:S(2)}, u32[]{:S(2)}) collective-permute-start(f32[16,8,1,128]{3,2,1,0:T(1,128)S(1)} %get-tuple-element.21), channel_id=1, source_target_pairs={{0,1},{1,2},{2,3},{4,5},{5,6},{6,7},{8,9},{9,10},{10,11},{12,13},{... | collective-permute-start | bytes 196616 | tf_op jit(solution)/shard_map/ppermute | solution.py:18
  68.5 11.5 %collective-permute-start.12 = (f32[16,1,32,128]{3,2,1,0:T(8,128)S(1)}, f32[16,1,32,128]{3,2,1,0:T(8,128)S(1)}, u32[]{:S(2)}, u32[]{:S(2)}) collective-permute-start(f32[16,1,32,128]{3,2,1,0:T(8,128)S(1)} %get-tuple-element.19), channel_id=1, source_target_pairs={{4,0},{8,4},{12,8},{16,12},{20,16},{24,20},{28,24},{5,1},{9,5},{13... | collective-permute-start | bytes 786440 | tf_op jit(solution)/shard_map/ppermute | solution.py:19
  69.8 15.3 %collective-permute-start.13 = (f32[16,1,32,128]{3,2,1,0:T(8,128)S(1)}, f32[16,1,32,128]{3,2,1,0:T(8,128)S(1)}, u32[]{:S(2)}, u32[]{:S(2)}) collective-permute-start(f32[16,1,32,128]{3,2,1,0:T(8,128)S(1)} %get-tuple-element.18), channel_id=1, source_target_pairs={{0,4},{4,8},{8,12},{12,16},{16,20},{20,24},{24,28},{1,5},{5,9},{9,... | collective-permute-start | bytes 786440 | tf_op jit(solution)/shard_map/ppermute | solution.py:18
  74.8 10.7 %collective-permute-start.14 = (f32[16,8,1,128]{3,2,1,0:T(1,128)S(1)}, f32[16,8,1,128]{3,2,1,0:T(1,128)S(1)}, u32[]{:S(2)}, u32[]{:S(2)}) collective-permute-start(f32[16,8,1,128]{3,2,1,0:T(1,128)S(1)} %get-tuple-element.16), channel_id=1, source_target_pairs={{1,0},{2,1},{3,2},{5,4},{6,5},{7,6},{9,8},{10,9},{11,10},{13,12},{... | collective-permute-start | bytes 196616 | tf_op jit(solution)/shard_map/ppermute | solution.py:19
  76.1 9.4 %collective-permute-start.15 = (f32[16,8,1,128]{3,2,1,0:T(1,128)S(1)}, f32[16,8,1,128]{3,2,1,0:T(1,128)S(1)}, u32[]{:S(2)}, u32[]{:S(2)}) collective-permute-start(f32[16,8,1,128]{3,2,1,0:T(1,128)S(1)} %get-tuple-element.17), channel_id=1, source_target_pairs={{0,1},{1,2},{2,3},{4,5},{5,6},{6,7},{8,9},{9,10},{10,11},{12,13},{... | collective-permute-start | bytes 196616 | tf_op jit(solution)/shard_map/ppermute | solution.py:18
  97.6 4.4 %collective-permute-start.18 = (f32[16,16]{0,1:T(8,128)S(1)}, f32[16,16]{0,1:T(8,128)S(1)}, u32[]{:S(2)}, u32[]{:S(2)}) collective-permute-start(f32[16,16]{0,1:T(8,128)S(1)} %add.143), channel_id=1, source_target_pairs={{0,4},{4,0},{8,12},{12,8},{16,20},{20,16},{24,28},{28,24},{1,5},{5... | collective-permute-start | bytes 3080 | tf_op jit(solution)/shard_map/ppermute | solution.py:68
  105.7 12.9 %collective-permute-start.20 = (f32[16,16]{0,1:T(8,128)S(1)}, f32[16,16]{0,1:T(8,128)S(1)}, u32[]{:S(2)}, u32[]{:S(2)}) collective-permute-start(f32[16,16]{0,1:T(8,128)S(1)} %add.145), channel_id=1, source_target_pairs={{0,16},{4,20},{8,24},{12,28},{16,0},{20,4},{24,8},{28,12},{1,17},{... | collective-permute-start | bytes 3080 | tf_op jit(solution)/shard_map/ppermute | solution.py:68
  108.4 11.8 %collective-permute-start.21 = (f32[16,1,32,128]{3,2,1,0:T(8,128)}, f32[16,1,32,128]{3,2,1,0:T(8,128)S(1)}, u32[]{:S(2)}, u32[]{:S(2)}) collective-permute-start(f32[16,1,32,128]{3,2,1,0:T(8,128)} %get-tuple-element.15), channel_id=1, source_target_pairs={{4,0},{8,4},{12,8},{16,12},{20,16},{24,20},{28,24},{5,1},{9,5},{13... | collective-permute-start | bytes 786440 | tf_op jit(solution)/shard_map/ppermute | solution.py:19
  109.7 11.3 %collective-permute-start.22 = (f32[16,1,32,128]{3,2,1,0:T(8,128)}, f32[16,1,32,128]{3,2,1,0:T(8,128)S(1)}, u32[]{:S(2)}, u32[]{:S(2)}) collective-permute-start(f32[16,1,32,128]{3,2,1,0:T(8,128)} %get-tuple-element.14), channel_id=1, source_target_pairs={{0,4},{4,8},{8,12},{12,16},{16,20},{20,24},{24,28},{1,5},{5,9},{9,... | collective-permute-start | bytes 786440 | tf_op jit(solution)/shard_map/ppermute | solution.py:18
  114.2 7.1 %collective-permute-start.23 = (f32[16,8,1,128]{3,2,1,0:T(1,128)S(1)}, f32[16,8,1,128]{3,2,1,0:T(1,128)S(1)}, u32[]{:S(2)}, u32[]{:S(2)}) collective-permute-start(f32[16,8,1,128]{3,2,1,0:T(1,128)S(1)} %get-tuple-element.12), channel_id=1, source_target_pairs={{1,0},{2,1},{3,2},{5,4},{6,5},{7,6},{9,8},{10,9},{11,10},{13,12},{... | collective-permute-start | bytes 196616 | tf_op jit(solution)/shard_map/ppermute | solution.py:19
  115.5 5.8 %collective-permute-start.24 = (f32[16,8,1,128]{3,2,1,0:T(1,128)S(1)}, f32[16,8,1,128]{3,2,1,0:T(1,128)S(1)}, u32[]{:S(2)}, u32[]{:S(2)}) collective-permute-start(f32[16,8,1,128]{3,2,1,0:T(1,128)S(1)} %get-tuple-element.13), channel_id=1, source_target_pairs={{0,1},{1,2},{2,3},{4,5},{5,6},{6,7},{8,9},{9,10},{10,11},{12,13},{... | collective-permute-start | bytes 196616 | tf_op jit(solution)/shard_map/ppermute | solution.py:18
  134.2 4.4 %collective-permute-start.27 = (f32[16,16]{0,1:T(8,128)S(1)}, f32[16,16]{0,1:T(8,128)S(1)}, u32[]{:S(2)}, u32[]{:S(2)}) collective-permute-start(f32[16,16]{0,1:T(8,128)S(1)} %add.152), channel_id=1, source_target_pairs={{0,4},{4,0},{8,12},{12,8},{16,20},{20,16},{24,28},{28,24},{1,5},{5... | collective-permute-start | bytes 3080 | tf_op jit(solution)/shard_map/ppermute | solution.py:68
  142.4 5.9 %collective-permute-start.29 = (f32[16,16]{0,1:T(8,128)S(1)}, f32[16,16]{0,1:T(8,128)S(1)}, u32[]{:S(2)}, u32[]{:S(2)}) collective-permute-start(f32[16,16]{0,1:T(8,128)S(1)} %add.154), channel_id=1, source_target_pairs={{0,16},{4,20},{8,24},{12,28},{16,0},{20,4},{24,8},{28,12},{1,17},{... | collective-permute-start | bytes 3080 | tf_op jit(solution)/shard_map/ppermute | solution.py:68
  (19 other events, 55.8 us)

commit v5 on v0

--- a/solution.py
+++ b/solution.py
@@ -98,13 +98,15 @@
     field = start_panel * ocean_cells[None]
     fields = jnp.stack([ocean_cells, conduct_x, conduct_y, conduct_z, diag_shift])
     rows, cols = field.shape[1], field.shape[2]
-    edges = [
-        jnp.concatenate([part[:, a:b] for part in (field, fields)])
-        for a, b in ((rows - 1, rows), (0, 1))
-    ] + [
-        jnp.concatenate([part[:, :, a:b] for part in (field, fields)])
-        for a, b in ((cols - 1, cols), (0, 1))
-    ]
+    sent = ((0, 1), (0,), (0, 2), (0,))
+    edges = []
+    for (dim, first), keep in zip(
+        ((0, rows - 1), (0, 0), (1, cols - 1), (1, 0)), sent
+    ):
+        cut = lambda a, lead: lax.slice_in_dim(a, first, first + 1, axis=dim + lead)
+        edges.append(
+            jnp.concatenate([cut(field, 1), *(cut(fields[i : i + 1], 1) for i in keep)])
+        )
     halos = []
     for axis, (to_high, to_low) in (("gx", edges[0:2]), ("gy", edges[2:4])):
         count = lax.axis_size(axis)
@@ -112,14 +114,19 @@
         backward = [(target, source) for source, target in forward]
         halos += [lax.ppermute(to_high, axis, forward), lax.ppermute(to_low, axis, backward)]
 
-    def assemble(block, part):
-        low_x, high_x, low_y, high_y = (halo[part] for halo in halos)
+    def widen(halo, keep):
+        parts = [jnp.zeros_like(halo[vectors : vectors + 1])] * fields.shape[0]
+        for place, index in enumerate(keep):
+            parts[index] = halo[vectors + place : vectors + place + 1]
+        return jnp.concatenate(parts)
+
+    def assemble(block, low_x, high_x, low_y, high_y):
         block = jnp.concatenate([low_x, block, high_x], axis=1)
         edge = ((0, 0), (1, 1), (0, 0), (0, 0))
         return jnp.concatenate([jnp.pad(low_y, edge), block, jnp.pad(high_y, edge)], axis=2)
 
-    fields_one = assemble(fields, slice(vectors, None))
-    together = assemble(field, slice(0, vectors))
+    fields_one = assemble(fields, *(widen(halo, keep) for halo, keep in zip(halos, sent)))
+    together = assemble(field, *(halo[:vectors] for halo in halos))
     first = True
     for repeat in range(FILTER_STEPS):
         if first:

time: 154 us -> 153 us (level)
  waiting for transfers between devices: 31.8 us -> 36.6 us
  starting transfers between devices: 67.9 us -> 63.5 us
    ppermute x2, waiting for transfers between devices: 0.01 us -> 7.9 us  [on_device(): lax.ppermute(to_low, axis, backward)]
    ppermute x2, waiting for transfers between devices: 8.63 us -> 1.53 us  [on_device(): lax.ppermute(to_high, axis, forward)]
    ppermute x10, starting transfers between devices: 15.1 us -> 12 us  [reduce_all(): value = value + lax.ppermute(value, axis, pairs)]
    ppermute x10, waiting for transfers between devices: 6.75 us -> 9.78 us  [reduce_all(): value = value + lax.ppermute(value, axis, pairs)]
    unnamed x27 -> x29, local copies, waits for them, and re-layouts: 5.45 us -> 5.45 us
  transfers between devices with their start and end apart: 30 -> 30, of which waited for: 13 -> 15; matrix products, arithmetic and copies ran while one was open for 12% -> 12% of each run, Pallas kernels for 0% -> 0%
where the time goes in v5:
time: 153 us
  starting transfers between devices  63.5 us (42%)
  waiting for transfers between devices  36.6 us (24%)
  other arithmetic  26.7 us (17%)
  matrix products  16.5 us (11%)
  local copies, waits for them, and re-layouts  7.73 us (5%)
    ppermute x8, starting transfers between devices, halo_pair(): lax.ppermute(lax.slice_in_dim(block, block.shape[dim] - 1, None, axis=dim...  31.9 us
    ppermute x8, waiting for transfers between devices, halo_pair(): lax.ppermute(lax.slice_in_dim(block, block.shape[dim] - 1, None, axis=dim...  17.2 us
    ppermute x10, starting transfers between devices, reduce_all(): value = value + lax.ppermute(value, axis, pairs)  12 us
    ppermute x8, starting transfers between devices, halo_pair(): high = lax.ppermute(lax.slice_in_dim(block, 0, 1, axis=dim), axis, backward)  10.3 us
    ppermute x10, waiting for transfers between devices, reduce_all(): value = value + lax.ppermute(value, axis, pairs)  9.78 us
    dot_general x2, matrix products, inner_products(): return jnp.einsum('kc,lc->kl', left, right, precision=lax.Precision.HIGHEST)  8.14 us
    ppermute x2, waiting for transfers between devices, on_device(): lax.ppermute(to_low, axis, backward)  7.9 us
    dot_general x3, matrix products, combine(): jnp.einsum('kl,lc->kc', matrix, rows, precision=lax.Precision.HIGHEST)  7.89 us
  transfers between devices with their start and end apart: 30, of which 15 were waited for; matrix products, arithmetic and copies ran while one was open for 12% of the time, Pallas kernels for 0%

profile of v5, /device:TPU:0, one launch (start us, length us, event | category | flops | bytes accessed | tf_op | source)
XLA Modules:
  0.0 152.6 jit_solution(5964940209435001674)
XLA Ops:
  3.7 2.4 %collective-permute-start = (f32[18,8,1,128]{3,2,1,0:T(1,128)S(1)}, f32[18,8,1,128]{3,2,1,0:T(1,128)S(1)}, u32[]{:S(2)}, u32[]{:S(2)}) collective-permute-start(f32[18,8,1,128]{3,2,1,0:T(1,128)S(1)} %pad_maximum_fusion.22), channel_id=1, source_target_pairs={{0,1},{1,2},{2,3},{4,5},{5,6},{6,7},{8,9},{9,10},{10,11},{12,13},{... | collective-permute-start | bytes 221192 | tf_op jit(solution)/shard_map/ppermute | solution.py:115
  6.2 4.3 %collective-permute-start.1 = (f32[18,1,32,128]{3,2,1,0:T(8,128)S(1)}, f32[18,1,32,128]{3,2,1,0:T(8,128)S(1)}, u32[]{:S(2)}, u32[]{:S(2)}) collective-permute-start(f32[18,1,32,128]{3,2,1,0:T(8,128)S(1)} %pad_maximum_fusion.20), channel_id=1, source_target_pairs={{0,4},{4,8},{8,12},{12,16},{16,20},{20,24},{24,28},{1,5},{5,9},{9,... | collective-permute-start | bytes 884744 | tf_op jit(solution)/shard_map/ppermute | solution.py:115
  13.5 2.6 %collective-permute-done.3 = f32[17,8,1,128]{3,2,1,0:T(1,128)S(1)} collective-permute-done((f32[17,8,1,128]{3,2,1,0:T(1,128)S(1)}, f32[17,8,1,128]{3,2,1,0:T(1,128)S(1)}, u32[]{:S(2)}, u32[]{:S(2)}) %collective-permute-start.3) | collective-permute-done | bytes 69664 | tf_op jit(solution)/shard_map/ppermute | solution.py:115
  16.1 5.3 %collective-permute-done.2 = f32[17,1,32,128]{3,2,1,0:T(8,128)S(1)} collective-permute-done((f32[17,1,32,128]{3,2,1,0:T(8,128)S(1)}, f32[17,1,32,128]{3,2,1,0:T(8,128)S(1)}, u32[]{:S(2)}, u32[]{:S(2)}) %collective-permute-start.2) | collective-permute-done | bytes 278560 | tf_op jit(solution)/shard_map/ppermute | solution.py:115
  29.5 5.0 %collective-permute-start.5 = (f32[16,1,32,128]{3,2,1,0:T(8,128)S(1)}, f32[16,1,32,128]{3,2,1,0:T(8,128)S(1)}, u32[]{:S(2)}, u32[]{:S(2)}) collective-permute-start(f32[16,1,32,128]{3,2,1,0:T(8,128)S(1)} %get-tuple-element.24), channel_id=1, source_target_pairs={{0,4},{4,8},{8,12},{12,16},{16,20},{20,24},{24,28},{1,5},{5,9},{9,... | collective-permute-start | bytes 786440 | tf_op jit(solution)/shard_map/ppermute | solution.py:18
  35.8 3.0 %collective-permute-start.7 = (f32[16,8,1,128]{3,2,1,0:T(1,128)S(1)}, f32[16,8,1,128]{3,2,1,0:T(1,128)S(1)}, u32[]{:S(2)}, u32[]{:S(2)}) collective-permute-start(f32[16,8,1,128]{3,2,1,0:T(1,128)S(1)} %get-tuple-element.23), channel_id=1, source_target_pairs={{0,1},{1,2},{2,3},{4,5},{5,6},{6,7},{8,9},{9,10},{10,11},{12,13},{... | collective-permute-start | bytes 196616 | tf_op jit(solution)/shard_map/ppermute | solution.py:18
  39.7 5.9 %collective-permute-done.5 = f32[16,1,32,128]{3,2,1,0:T(8,128)S(1)} collective-permute-done((f32[16,1,32,128]{3,2,1,0:T(8,128)S(1)}, f32[16,1,32,128]{3,2,1,0:T(8,128)S(1)}, u32[]{:S(2)}, u32[]{:S(2)}) %collective-permute-start.5) | collective-permute-done | bytes 262176 | tf_op jit(solution)/shard_map/ppermute | solution.py:18
  50.0 5.0 %collective-permute-start.9 = (f32[16,1,32,128]{3,2,1,0:T(8,128)S(1)}, f32[16,1,32,128]{3,2,1,0:T(8,128)S(1)}, u32[]{:S(2)}, u32[]{:S(2)}) collective-permute-start(f32[16,1,32,128]{3,2,1,0:T(8,128)S(1)} %get-tuple-element.20), channel_id=1, source_target_pairs={{0,4},{4,8},{8,12},{12,16},{16,20},{20,24},{24,28},{1,5},{5,9},{9,... | collective-permute-start | bytes 786440 | tf_op jit(solution)/shard_map/ppermute | solution.py:18
  56.3 3.0 %collective-permute-start.11 = (f32[16,8,1,128]{3,2,1,0:T(1,128)S(1)}, f32[16,8,1,128]{3,2,1,0:T(1,128)S(1)}, u32[]{:S(2)}, u32[]{:S(2)}) collective-permute-start(f32[16,8,1,128]{3,2,1,0:T(1,128)S(1)} %get-tuple-element.19), channel_id=1, source_target_pairs={{0,1},{1,2},{2,3},{4,5},{5,6},{6,7},{8,9},{9,10},{10,11},{12,13},{... | collective-permute-start | bytes 196616 | tf_op jit(solution)/shard_map/ppermute | solution.py:18
  60.0 5.4 %collective-permute-done.9 = f32[16,1,32,128]{3,2,1,0:T(8,128)S(1)} collective-permute-done((f32[16,1,32,128]{3,2,1,0:T(8,128)S(1)}, f32[16,1,32,128]{3,2,1,0:T(8,128)S(1)}, u32[]{:S(2)}, u32[]{:S(2)}) %collective-permute-start.9) | collective-permute-done | bytes 262176 | tf_op jit(solution)/shard_map/ppermute | solution.py:18
  69.5 5.0 %collective-permute-start.13 = (f32[16,1,32,128]{3,2,1,0:T(8,128)S(1)}, f32[16,1,32,128]{3,2,1,0:T(8,128)S(1)}, u32[]{:S(2)}, u32[]{:S(2)}) collective-permute-start(f32[16,1,32,128]{3,2,1,0:T(8,128)S(1)} %get-tuple-element.16), channel_id=1, source_target_pairs={{0,4},{4,8},{8,12},{12,16},{16,20},{20,24},{24,28},{1,5},{5,9},{9,... | collective-permute-start | bytes 786440 | tf_op jit(solution)/shard_map/ppermute | solution.py:18
  75.8 3.2 %collective-permute-start.15 = (f32[16,8,1,128]{3,2,1,0:T(1,128)S(1)}, f32[16,8,1,128]{3,2,1,0:T(1,128)S(1)}, u32[]{:S(2)}, u32[]{:S(2)}) collective-permute-start(f32[16,8,1,128]{3,2,1,0:T(1,128)S(1)} %get-tuple-element.15), channel_id=1, source_target_pairs={{0,1},{1,2},{2,3},{4,5},{5,6},{6,7},{8,9},{9,10},{10,11},{12,13},{... | collective-permute-start | bytes 196616 | tf_op jit(solution)/shard_map/ppermute | solution.py:18
  79.7 5.2 %collective-permute-done.13 = f32[16,1,32,128]{3,2,1,0:T(8,128)S(1)} collective-permute-done((f32[16,1,32,128]{3,2,1,0:T(8,128)S(1)}, f32[16,1,32,128]{3,2,1,0:T(8,128)S(1)}, u32[]{:S(2)}, u32[]{:S(2)}) %collective-permute-start.13) | collective-permute-done | bytes 262176 | tf_op jit(solution)/shard_map/ppermute | solution.py:18
  86.1 2.7 %broadcast_multiply_fusion = (f32[16,8,32,128]{3,2,1,0:T(8,128)S(1)}, f32[16,8,32,128]{3,2,1,0:T(8,128)}) fusion(f32[16,8,32,128]{3,2,1,0:T(8,128)S(1)} %get-tuple-element.7, f32[16,8,32,128]{3,2,1,0:T(8,128)S(1)} %get-tuple-element.5, f32[16,8,32,127]{3,2,1,0:T(8,128)S(1)} %fusion.36, f32[16,8,33,128]{3,2,1,0:T(8,128)S(1)} %fusion.6, ...), kind=kLoop, calls=%fused_computation.131 | loop fusion | flops 7340032 | bytes 19120128 | tf_op jit(solution)/shard_map/div | solution.py:138
  88.9 3.6 %fusion.74 = f32[16,16]{0,1:T(8,128)S(1)} fusion(f32[16,8,32,128]{3,2,1,0:T(8,128)S(1)} %get-tuple-element.2), kind=kOutput, calls=%fused_computation.129 | convolution fusion | flops 100663296 | bytes 2098176 | tf_op jit(solution)/shard_map/kc,lc->kl/dot_general | solution.py:74
  93.6 3.6 %collective-permute-done.17 = f32[16,16]{0,1:T(8,128)S(1)} collective-permute-done((f32[16,16]{0,1:T(8,128)S(1)}, f32[16,16]{0,1:T(8,128)S(1)}, u32[]{:S(2)}, u32[]{:S(2)}) %collective-permute-start.17) | collective-permute-done | bytes 1056 | tf_op jit(solution)/shard_map/ppermute | solution.py:68
  97.3 2.5 %collective-permute-start.18 = (f32[16,16]{0,1:T(8,128)S(1)}, f32[16,16]{0,1:T(8,128)S(1)}, u32[]{:S(2)}, u32[]{:S(2)}) collective-permute-start(f32[16,16]{0,1:T(8,128)S(1)} %add.149), channel_id=1, source_target_pairs={{0,4},{4,0},{8,12},{12,8},{16,20},{20,16},{24,28},{28,24},{1,5},{5... | collective-permute-start | bytes 3080 | tf_op jit(solution)/shard_map/ppermute | solution.py:68
  105.4 2.5 %collective-permute-start.20 = (f32[16,16]{0,1:T(8,128)S(1)}, f32[16,16]{0,1:T(8,128)S(1)}, u32[]{:S(2)}, u32[]{:S(2)}) collective-permute-start(f32[16,16]{0,1:T(8,128)S(1)} %add.151), channel_id=1, source_target_pairs={{0,16},{4,20},{8,24},{12,28},{16,0},{20,4},{24,8},{28,12},{1,17},{... | collective-permute-start | bytes 3080 | tf_op jit(solution)/shard_map/ppermute | solution.py:68
  109.3 4.6 %collective-permute-start.22 = (f32[16,1,32,128]{3,2,1,0:T(8,128)}, f32[16,1,32,128]{3,2,1,0:T(8,128)S(1)}, u32[]{:S(2)}, u32[]{:S(2)}) collective-permute-start(f32[16,1,32,128]{3,2,1,0:T(8,128)} %get-tuple-element.12), channel_id=1, source_target_pairs={{0,4},{4,8},{8,12},{12,16},{16,20},{20,24},{24,28},{1,5},{5,9},{9,... | collective-permute-start | bytes 786440 | tf_op jit(solution)/shard_map/ppermute | solution.py:18
  115.2 3.0 %collective-permute-start.24 = (f32[16,8,1,128]{3,2,1,0:T(1,128)S(1)}, f32[16,8,1,128]{3,2,1,0:T(1,128)S(1)}, u32[]{:S(2)}, u32[]{:S(2)}) collective-permute-start(f32[16,8,1,128]{3,2,1,0:T(1,128)S(1)} %get-tuple-element.11), channel_id=1, source_target_pairs={{0,1},{1,2},{2,3},{4,5},{5,6},{6,7},{8,9},{9,10},{10,11},{12,13},{... | collective-permute-start | bytes 196616 | tf_op jit(solution)/shard_map/ppermute | solution.py:18
  124.4 4.5 %fusion.77 = f32[16,16]{0,1:T(8,128)S(1)} fusion(f32[16,8,32,128]{3,2,1,0:T(8,128)S(1)} %fusion.34, f32[16,8,32,128]{3,2,1,0:T(8,128)S(1)} %get-tuple-element.2), kind=kOutput, calls=%fused_computation.130 | convolution fusion | flops 100663296 | bytes 4195328 | tf_op jit(solution)/shard_map/kc,lc->kl/dot_general | solution.py:74
  133.9 2.4 %collective-permute-start.27 = (f32[16,16]{0,1:T(8,128)S(1)}, f32[16,16]{0,1:T(8,128)S(1)}, u32[]{:S(2)}, u32[]{:S(2)}) collective-permute-start(f32[16,16]{0,1:T(8,128)S(1)} %add.158), channel_id=1, source_target_pairs={{0,4},{4,0},{8,12},{12,8},{16,20},{20,16},{24,28},{28,24},{1,5},{5... | collective-permute-start | bytes 3080 | tf_op jit(solution)/shard_map/ppermute | solution.py:68
  139.4 2.8 %fusion.28 = f32[16,32768]{1,0:T(8,128)S(1)} fusion(f32[16,16]{1,0:T(8,128)S(1)} %fusion.84, f32[2,8,256,128]{3,2,1,0:T(8,128)S(1)} %bitcast.63), kind=kOutput, calls=%fused_computation.66 | convolution fusion | flops 100663296 | bytes 4195328 | tf_op jit(solution)/shard_map/kl,lc->kc/dot_general | solution.py:78
  145.2 3.1 %fusion.25 = f32[16,32768]{1,0:T(8,128)S(1)} fusion(f32[16,16]{1,0:T(8,128)S(1)} %fusion.84, f32[2,8,256,128]{3,2,1,0:T(8,128)S(1)} %bitcast.64), kind=kOutput, calls=%fused_computation.63 | convolution fusion | flops 100663296 | bytes 4195328 | tf_op jit(solution)/shard_map/kl,lc->kc/dot_general | solution.py:78
  (152 shorter events, 60.3 us)
Async XLA Ops:
  3.7 12.3 %collective-permute-start = (f32[18,8,1,128]{3,2,1,0:T(1,128)S(1)}, f32[18,8,1,128]{3,2,1,0:T(1,128)S(1)}, u32[]{:S(2)}, u32[]{:S(2)}) collective-permute-start(f32[18,8,1,128]{3,2,1,0:T(1,128)S(1)} %pad_maximum_fusion.22), channel_id=1, source_target_pairs={{0,1},{1,2},{2,3},{4,5},{5,6},{6,7},{8,9},{9,10},{10,11},{12,13},{... | collective-permute-start | bytes 221192 | tf_op jit(solution)/shard_map/ppermute | solution.py:115
  6.2 16.8 %collective-permute-start.1 = (f32[18,1,32,128]{3,2,1,0:T(8,128)S(1)}, f32[18,1,32,128]{3,2,1,0:T(8,128)S(1)}, u32[]{:S(2)}, u32[]{:S(2)}) collective-permute-start(f32[18,1,32,128]{3,2,1,0:T(8,128)S(1)} %pad_maximum_fusion.20), channel_id=1, source_target_pairs={{0,4},{4,8},{8,12},{12,16},{16,20},{20,24},{24,28},{1,5},{5,9},{9,... | collective-permute-start | bytes 884744 | tf_op jit(solution)/shard_map/ppermute | solution.py:115
  10.5 11.0 %collective-permute-start.2 = (f32[17,1,32,128]{3,2,1,0:T(8,128)S(1)}, f32[17,1,32,128]{3,2,1,0:T(8,128)S(1)}, u32[]{:S(2)}, u32[]{:S(2)}) collective-permute-start(f32[17,1,32,128]{3,2,1,0:T(8,128)S(1)} %pad_maximum_fusion.21), channel_id=1, source_target_pairs={{4,0},{8,4},{12,8},{16,12},{20,16},{24,20},{28,24},{5,1},{9,5},{13... | collective-permute-start | bytes 835592 | tf_op jit(solution)/shard_map/ppermute | solution.py:115
  11.9 4.1 %collective-permute-start.3 = (f32[17,8,1,128]{3,2,1,0:T(1,128)S(1)}, f32[17,8,1,128]{3,2,1,0:T(1,128)S(1)}, u32[]{:S(2)}, u32[]{:S(2)}) collective-permute-start(f32[17,8,1,128]{3,2,1,0:T(1,128)S(1)} %pad_maximum_fusion.23), channel_id=1, source_target_pairs={{1,0},{2,1},{3,2},{5,4},{6,5},{7,6},{9,8},{10,9},{11,10},{13,12},{... | collective-permute-start | bytes 208904 | tf_op jit(solution)/shard_map/ppermute | solution.py:115
  28.2 11.5 %collective-permute-start.4 = (f32[16,1,32,128]{3,2,1,0:T(8,128)S(1)}, f32[16,1,32,128]{3,2,1,0:T(8,128)S(1)}, u32[]{:S(2)}, u32[]{:S(2)}) collective-permute-start(f32[16,1,32,128]{3,2,1,0:T(8,128)S(1)} %get-tuple-element.25), channel_id=1, source_target_pairs={{4,0},{8,4},{12,8},{16,12},{20,16},{24,20},{28,24},{5,1},{9,5},{13... | collective-permute-start | bytes 786440 | tf_op jit(solution)/shard_map/ppermute | solution.py:19
  29.5 16.0 %collective-permute-start.5 = (f32[16,1,32,128]{3,2,1,0:T(8,128)S(1)}, f32[16,1,32,128]{3,2,1,0:T(8,128)S(1)}, u32[]{:S(2)}, u32[]{:S(2)}) collective-permute-start(f32[16,1,32,128]{3,2,1,0:T(8,128)S(1)} %get-tuple-element.24), channel_id=1, source_target_pairs={{0,4},{4,8},{8,12},{12,16},{16,20},{20,24},{24,28},{1,5},{5,9},{9,... | collective-permute-start | bytes 786440 | tf_op jit(solution)/shard_map/ppermute | solution.py:18
  34.5 11.3 %collective-permute-start.6 = (f32[16,8,1,128]{3,2,1,0:T(1,128)S(1)}, f32[16,8,1,128]{3,2,1,0:T(1,128)S(1)}, u32[]{:S(2)}, u32[]{:S(2)}) collective-permute-start(f32[16,8,1,128]{3,2,1,0:T(1,128)S(1)} %get-tuple-element.22), channel_id=1, source_target_pairs={{1,0},{2,1},{3,2},{5,4},{6,5},{7,6},{9,8},{10,9},{11,10},{13,12},{... | collective-permute-start | bytes 196616 | tf_op jit(solution)/shard_map/ppermute | solution.py:19
  35.8 10.0 %collective-permute-start.7 = (f32[16,8,1,128]{3,2,1,0:T(1,128)S(1)}, f32[16,8,1,128]{3,2,1,0:T(1,128)S(1)}, u32[]{:S(2)}, u32[]{:S(2)}) collective-permute-start(f32[16,8,1,128]{3,2,1,0:T(1,128)S(1)} %get-tuple-element.23), channel_id=1, source_target_pairs={{0,1},{1,2},{2,3},{4,5},{5,6},{6,7},{8,9},{9,10},{10,11},{12,13},{... | collective-permute-start | bytes 196616 | tf_op jit(solution)/shard_map/ppermute | solution.py:18
  48.7 11.3 %collective-permute-start.8 = (f32[16,1,32,128]{3,2,1,0:T(8,128)S(1)}, f32[16,1,32,128]{3,2,1,0:T(8,128)S(1)}, u32[]{:S(2)}, u32[]{:S(2)}) collective-permute-start(f32[16,1,32,128]{3,2,1,0:T(8,128)S(1)} %get-tuple-element.21), channel_id=1, source_target_pairs={{4,0},{8,4},{12,8},{16,12},{20,16},{24,20},{28,24},{5,1},{9,5},{13... | collective-permute-start | bytes 786440 | tf_op jit(solution)/shard_map/ppermute | solution.py:19
  50.0 15.4 %collective-permute-start.9 = (f32[16,1,32,128]{3,2,1,0:T(8,128)S(1)}, f32[16,1,32,128]{3,2,1,0:T(8,128)S(1)}, u32[]{:S(2)}, u32[]{:S(2)}) collective-permute-start(f32[16,1,32,128]{3,2,1,0:T(8,128)S(1)} %get-tuple-element.20), channel_id=1, source_target_pairs={{0,4},{4,8},{8,12},{12,16},{16,20},{20,24},{24,28},{1,5},{5,9},{9,... | collective-permute-start | bytes 786440 | tf_op jit(solution)/shard_map/ppermute | solution.py:18
  55.0 10.7 %collective-permute-start.10 = (f32[16,8,1,128]{3,2,1,0:T(1,128)S(1)}, f32[16,8,1,128]{3,2,1,0:T(1,128)S(1)}, u32[]{:S(2)}, u32[]{:S(2)}) collective-permute-start(f32[16,8,1,128]{3,2,1,0:T(1,128)S(1)} %get-tuple-element.18), channel_id=1, source_target_pairs={{1,0},{2,1},{3,2},{5,4},{6,5},{7,6},{9,8},{10,9},{11,10},{13,12},{... | collective-permute-start | bytes 196616 | tf_op jit(solution)/shard_map/ppermute | solution.py:19
  56.3 9.4 %collective-permute-start.11 = (f32[16,8,1,128]{3,2,1,0:T(1,128)S(1)}, f32[16,8,1,128]{3,2,1,0:T(1,128)S(1)}, u32[]{:S(2)}, u32[]{:S(2)}) collective-permute-start(f32[16,8,1,128]{3,2,1,0:T(1,128)S(1)} %get-tuple-element.19), channel_id=1, source_target_pairs={{0,1},{1,2},{2,3},{4,5},{5,6},{6,7},{8,9},{9,10},{10,11},{12,13},{... | collective-permute-start | bytes 196616 | tf_op jit(solution)/shard_map/ppermute | solution.py:18
  68.2 11.5 %collective-permute-start.12 = (f32[16,1,32,128]{3,2,1,0:T(8,128)S(1)}, f32[16,1,32,128]{3,2,1,0:T(8,128)S(1)}, u32[]{:S(2)}, u32[]{:S(2)}) collective-permute-start(f32[16,1,32,128]{3,2,1,0:T(8,128)S(1)} %get-tuple-element.17), channel_id=1, source_target_pairs={{4,0},{8,4},{12,8},{16,12},{20,16},{24,20},{28,24},{5,1},{9,5},{13... | collective-permute-start | bytes 786440 | tf_op jit(solution)/shard_map/ppermute | solution.py:19
  69.5 15.3 %collective-permute-start.13 = (f32[16,1,32,128]{3,2,1,0:T(8,128)S(1)}, f32[16,1,32,128]{3,2,1,0:T(8,128)S(1)}, u32[]{:S(2)}, u32[]{:S(2)}) collective-permute-start(f32[16,1,32,128]{3,2,1,0:T(8,128)S(1)} %get-tuple-element.16), channel_id=1, source_target_pairs={{0,4},{4,8},{8,12},{12,16},{16,20},{20,24},{24,28},{1,5},{5,9},{9,... | collective-permute-start | bytes 786440 | tf_op jit(solution)/shard_map/ppermute | solution.py:18
  74.5 10.7 %collective-permute-start.14 = (f32[16,8,1,128]{3,2,1,0:T(1,128)S(1)}, f32[16,8,1,128]{3,2,1,0:T(1,128)S(1)}, u32[]{:S(2)}, u32[]{:S(2)}) collective-permute-start(f32[16,8,1,128]{3,2,1,0:T(1,128)S(1)} %get-tuple-element.14), channel_id=1, source_target_pairs={{1,0},{2,1},{3,2},{5,4},{6,5},{7,6},{9,8},{10,9},{11,10},{13,12},{... | collective-permute-start | bytes 196616 | tf_op jit(solution)/shard_map/ppermute | solution.py:19
  75.8 9.5 %collective-permute-start.15 = (f32[16,8,1,128]{3,2,1,0:T(1,128)S(1)}, f32[16,8,1,128]{3,2,1,0:T(1,128)S(1)}, u32[]{:S(2)}, u32[]{:S(2)}) collective-permute-start(f32[16,8,1,128]{3,2,1,0:T(1,128)S(1)} %get-tuple-element.15), channel_id=1, source_target_pairs={{0,1},{1,2},{2,3},{4,5},{5,6},{6,7},{8,9},{9,10},{10,11},{12,13},{... | collective-permute-start | bytes 196616 | tf_op jit(solution)/shard_map/ppermute | solution.py:18
  97.3 4.4 %collective-permute-start.18 = (f32[16,16]{0,1:T(8,128)S(1)}, f32[16,16]{0,1:T(8,128)S(1)}, u32[]{:S(2)}, u32[]{:S(2)}) collective-permute-start(f32[16,16]{0,1:T(8,128)S(1)} %add.149), channel_id=1, source_target_pairs={{0,4},{4,0},{8,12},{12,8},{16,20},{20,16},{24,28},{28,24},{1,5},{5... | collective-permute-start | bytes 3080 | tf_op jit(solution)/shard_map/ppermute | solution.py:68
  105.4 12.8 %collective-permute-start.20 = (f32[16,16]{0,1:T(8,128)S(1)}, f32[16,16]{0,1:T(8,128)S(1)}, u32[]{:S(2)}, u32[]{:S(2)}) collective-permute-start(f32[16,16]{0,1:T(8,128)S(1)} %add.151), channel_id=1, source_target_pairs={{0,16},{4,20},{8,24},{12,28},{16,0},{20,4},{24,8},{28,12},{1,17},{... | collective-permute-start | bytes 3080 | tf_op jit(solution)/shard_map/ppermute | solution.py:68
  108.0 11.8 %collective-permute-start.21 = (f32[16,1,32,128]{3,2,1,0:T(8,128)}, f32[16,1,32,128]{3,2,1,0:T(8,128)S(1)}, u32[]{:S(2)}, u32[]{:S(2)}) collective-permute-start(f32[16,1,32,128]{3,2,1,0:T(8,128)} %get-tuple-element.13), channel_id=1, source_target_pairs={{4,0},{8,4},{12,8},{16,12},{20,16},{24,20},{28,24},{5,1},{9,5},{13... | collective-permute-start | bytes 786440 | tf_op jit(solution)/shard_map/ppermute | solution.py:19
  109.3 11.3 %collective-permute-start.22 = (f32[16,1,32,128]{3,2,1,0:T(8,128)}, f32[16,1,32,128]{3,2,1,0:T(8,128)S(1)}, u32[]{:S(2)}, u32[]{:S(2)}) collective-permute-start(f32[16,1,32,128]{3,2,1,0:T(8,128)} %get-tuple-element.12), channel_id=1, source_target_pairs={{0,4},{4,8},{8,12},{12,16},{16,20},{20,24},{24,28},{1,5},{5,9},{9,... | collective-permute-start | bytes 786440 | tf_op jit(solution)/shard_map/ppermute | solution.py:18
  113.9 7.1 %collective-permute-start.23 = (f32[16,8,1,128]{3,2,1,0:T(1,128)S(1)}, f32[16,8,1,128]{3,2,1,0:T(1,128)S(1)}, u32[]{:S(2)}, u32[]{:S(2)}) collective-permute-start(f32[16,8,1,128]{3,2,1,0:T(1,128)S(1)} %get-tuple-element.10), channel_id=1, source_target_pairs={{1,0},{2,1},{3,2},{5,4},{6,5},{7,6},{9,8},{10,9},{11,10},{13,12},{... | collective-permute-start | bytes 196616 | tf_op jit(solution)/shard_map/ppermute | solution.py:19
  115.2 5.8 %collective-permute-start.24 = (f32[16,8,1,128]{3,2,1,0:T(1,128)S(1)}, f32[16,8,1,128]{3,2,1,0:T(1,128)S(1)}, u32[]{:S(2)}, u32[]{:S(2)}) collective-permute-start(f32[16,8,1,128]{3,2,1,0:T(1,128)S(1)} %get-tuple-element.11), channel_id=1, source_target_pairs={{0,1},{1,2},{2,3},{4,5},{5,6},{6,7},{8,9},{9,10},{10,11},{12,13},{... | collective-permute-start | bytes 196616 | tf_op jit(solution)/shard_map/ppermute | solution.py:18
  137.9 6.1 %collective-permute-start.28 = (f32[16,16]{0,1:T(8,128)S(1)}, f32[16,16]{0,1:T(8,128)S(1)}, u32[]{:S(2)}, u32[]{:S(2)}) collective-permute-start(f32[16,16]{0,1:T(8,128)S(1)} %add.159), channel_id=1, source_target_pairs={{0,8},{4,12},{8,0},{12,4},{16,24},{20,28},{24,16},{28,20},{1,9},{5... | collective-permute-start | bytes 3080 | tf_op jit(solution)/shard_map/ppermute | solution.py:68
  144.0 4.6 %collective-permute-start.29 = (f32[16,16]{0,1:T(8,128)S(1)}, f32[16,16]{0,1:T(8,128)S(1)}, u32[]{:S(2)}, u32[]{:S(2)}) collective-permute-start(f32[16,16]{0,1:T(8,128)S(1)} %add.160), channel_id=1, source_target_pairs={{0,16},{4,20},{8,24},{12,28},{16,0},{20,4},{24,8},{28,12},{1,17},{... | collective-permute-start | bytes 3080 | tf_op jit(solution)/shard_map/ppermute | solution.py:68
  (20 other events, 82.4 us)

commit v6 on v5

--- a/solution.py
+++ b/solution.py
@@ -11,13 +11,24 @@
 FILTER_NORM = 2.0 * (22.0 / 18.0) * (22.0 / 18.0) - 1.0
 
 
+def swap_halos(to_high, to_low, axis):
+    count = lax.axis_size(axis)
+    even = lax.axis_index(axis) % 2 == 0
+    first = [(i, i ^ 1) for i in range(count - count % 2)]
+    second = [(i, j) for i in range(1, count - 1) for j in (i + 1 if i % 2 else i - 1,)]
+    got_first = lax.ppermute(jnp.where(even, to_high, to_low), axis, first)
+    got_second = lax.ppermute(jnp.where(even, to_low, to_high), axis, second)
+    low = jnp.where(even, got_second, got_first)
+    high = jnp.where(even, got_first, got_second)
+    return low, high
+
+
 def halo_pair(block, axis, dim):
-    count = lax.axis_size(axis)
-    forward = [(i, i + 1) for i in range(count - 1)]
-    backward = [(target, source) for source, target in forward]
-    low = lax.ppermute(lax.slice_in_dim(block, block.shape[dim] - 1, None, axis=dim), axis, forward)
-    high = lax.ppermute(lax.slice_in_dim(block, 0, 1, axis=dim), axis, backward)
-    return low, high
+    return swap_halos(
+        lax.slice_in_dim(block, block.shape[dim] - 1, None, axis=dim),
+        lax.slice_in_dim(block, 0, 1, axis=dim),
+        axis,
+    )
 
 
 def padded_2(block, sides, width):
@@ -108,11 +119,14 @@
             jnp.concatenate([cut(field, 1), *(cut(fields[i : i + 1], 1) for i in keep)])
         )
     halos = []
-    for axis, (to_high, to_low) in (("gx", edges[0:2]), ("gy", edges[2:4])):
-        count = lax.axis_size(axis)
-        forward = [(i, i + 1) for i in range(count - 1)]
-        backward = [(target, source) for source, target in forward]
-        halos += [lax.ppermute(to_high, axis, forward), lax.ppermute(to_low, axis, backward)]
+    for axis, (to_high, to_low), (keep_high, keep_low) in (
+        ("gx", edges[0:2], sent[0:2]),
+        ("gy", edges[2:4], sent[2:4]),
+    ):
+        size = max(to_high.shape[0], to_low.shape[0])
+        grow = lambda a: jnp.pad(a, ((0, size - a.shape[0]),) + ((0, 0),) * (a.ndim - 1))
+        low, high = swap_halos(grow(to_high), grow(to_low), axis)
+        halos += [low[: to_high.shape[0]], high[: to_low.shape[0]]]
 
     def widen(halo, keep):
         parts = [jnp.zeros_like(halo[vectors : vectors + 1])] * fields.shape[0]

time: 153 us -> 149 us (0.974)
  starting transfers between devices: 63.5 us -> 38.7 us
  waiting for transfers between devices: 36.6 us -> 50.6 us
  other arithmetic: 26.7 us -> 33.9 us
    ppermute x20, starting transfers between devices: 51.5 us -> 25.8 us  [the longest x10 17.6 us: swap_halos(): got_first = lax.ppermute(jnp.where(even, to_high, to_low), axis, first)]
    ppermute x20, waiting for transfers between devices: 26.8 us -> 40 us  [the longest x10 40 us: swap_halos(): got_first = lax.ppermute(jnp.where(even, to_high, to_low), axis, first)]
    select_n x0 -> x21, other arithmetic: none -> 3.7 us  [the longest x6 2.18 us: swap_halos(): low = jnp.where(even, got_second, got_first)]
    div x2, other arithmetic: 2.85 us -> 5.17 us  [on_device(): middle = (applied - FILTER_CENTRE * field) / FILTER_HALF]
    unnamed x29 -> x23, local copies, waits for them, and re-layouts: 5.45 us -> 5.45 us
  transfers between devices with their start and end apart: 30 -> 30, of which waited for: 15 -> 12; matrix products, arithmetic and copies ran while one was open for 12% -> 12% of each run, Pallas kernels for 0% -> 0%
where the time goes in v6:
time: 149 us; the launch traced here: 148 us
  waiting for transfers between devices  50.6 us (34%)
  starting transfers between devices  38.7 us (26%)
  other arithmetic  33.9 us (23%)
  matrix products  16.5 us (11%)
  local copies, waits for them, and re-layouts  6.88 us (5%)
    ppermute x10, waiting for transfers between devices, swap_halos(): got_first = lax.ppermute(jnp.where(even, to_high, to_low), axis, first)  40 us
    ppermute x10, starting transfers between devices, swap_halos(): got_first = lax.ppermute(jnp.where(even, to_high, to_low), axis, first)  17.6 us
    ppermute x10, starting transfers between devices, reduce_all(): value = value + lax.ppermute(value, axis, pairs)  12.9 us
    ppermute x10, waiting for transfers between devices, reduce_all(): value = value + lax.ppermute(value, axis, pairs)  10.5 us
    ppermute x10, starting transfers between devices, swap_halos(): got_second = lax.ppermute(jnp.where(even, to_low, to_high), axis, second)  8.16 us
    dot_general x2, matrix products, inner_products(): return jnp.einsum('kc,lc->kl', left, right, precision=lax.Precision.HIGHEST)  8.14 us
    dot_general x3, matrix products, combine(): jnp.einsum('kl,lc->kc', matrix, rows, precision=lax.Precision.HIGHEST)  7.89 us
    mul x5, other arithmetic, stencil(): flow_z = face_z * (centre[..., 1:] - centre[..., :-1])  5.73 us
  transfers between devices with their start and end apart: 30, of which 12 were waited for; matrix products, arithmetic and copies ran while one was open for 12% of the time, Pallas kernels for 0%

profile of v6, /device:TPU:0, one launch (start us, length us, event | category | flops | bytes accessed | tf_op | source)
XLA Modules:
  0.0 148.1 jit_solution(14238447312472806983)
XLA Ops:
  1.6 2.0 %broadcast_multiply_fusion.4 = f32[16,8,32,128]{3,2,1,0:T(8,128)S(1)} fusion(f32[16,8,32,128]{3,2,1,0:T(8,128)} %param.6, f32[8,32,128]{2,1,0:T(8,128)S(1)} %get-tuple-element.67), kind=kLoop, calls=%fused_computation.135 | loop fusion | flops 524288 | bytes 4325376 | tf_op jit(solution)/shard_map/mul | solution.py:109
  6.0 3.7 %collective-permute-start.1 = (f32[18,8,1,128]{3,2,1,0:T(1,128)S(1)}, f32[18,8,1,128]{3,2,1,0:T(1,128)}, u32[]{:S(2)}, u32[]{:S(2)}) collective-permute-start(f32[18,8,1,128]{3,2,1,0:T(1,128)S(1)} %get-tuple-element.10), channel_id=1, source_target_pairs={{0,1},{1,0},{2,3},{3,2},{4,5},{5,4},{6,7},{7,6},{8,9},{9,8},{10,11... | collective-permute-start | bytes 221192 | tf_op jit(solution)/shard_map/ppermute | solution.py:19
  10.5 4.3 %collective-permute-start.3 = (f32[18,1,32,128]{3,2,1,0:T(8,128)S(1)}, f32[18,1,32,128]{3,2,1,0:T(8,128)S(1)}, u32[]{:S(2)}, u32[]{:S(2)}) collective-permute-start(f32[18,1,32,128]{3,2,1,0:T(8,128)S(1)} %get-tuple-element.40), channel_id=1, source_target_pairs={{0,4},{4,0},{8,12},{12,8},{16,20},{20,16},{24,28},{28,24},{1,5},{5... | collective-permute-start | bytes 884744 | tf_op jit(solution)/shard_map/ppermute | solution.py:19
  17.1 9.8 %collective-permute-done.3 = f32[18,1,32,128]{3,2,1,0:T(8,128)S(1)} collective-permute-done((f32[18,1,32,128]{3,2,1,0:T(8,128)S(1)}, f32[18,1,32,128]{3,2,1,0:T(8,128)S(1)}, u32[]{:S(2)}, u32[]{:S(2)}) %collective-permute-start.3) | collective-permute-done | bytes 294944 | tf_op jit(solution)/shard_map/ppermute | solution.py:19
  27.5 1.9 %fusion.58 = f32[16,8,32,127]{3,2,1,0:T(8,128)} fusion(f32[16,8,32,128]{3,2,1,0:T(8,128)S(1)} %broadcast_multiply_fusion.4, f32[8,32,127]{2,1,0:T(8,128)S(1)} %slice_multiply_fusion.4), kind=kLoop, calls=%fused_computation.109 | loop fusion | flops 1040384 | bytes 6372352 | tf_op jit(solution)/shard_map/mul | solution.py:59
  31.4 3.7 %broadcast_multiply_fusion.3 = (f32[16,8,32,128]{3,2,1,0:T(8,128)S(1)}, f32[16,8,32,128]{3,2,1,0:T(8,128)S(1)}) fusion(f32[16,8,32,127]{3,2,1,0:T(8,128)} %fusion.58, f32[16,8,33,128]{3,2,1,0:T(8,128)S(1)} %fusion.18, f32[16,9,32,128]{3,2,1,0:T(8,128)S(1)} %fusion.20, f32[8,32,128]{2,1,0:T(8,128)S(1)} %get-tuple-element.51, f32[8,32,128]{2,1,0:T(8,128)S(1)} %slice.494, ...), kind=kLoop, calls=%fused_computation.134 | loop fusion | flops 6291456 | bytes 17154048 | tf_op jit(solution)/shard_map/div | solution.py:151
  35.3 2.5 %collective-permute-start.4 = (f32[16,1,32,128]{3,2,1,0:T(8,128)S(1)}, f32[16,1,32,128]{3,2,1,0:T(8,128)S(1)}, u32[]{:S(2)}, u32[]{:S(2)}) collective-permute-start(f32[16,1,32,128]{3,2,1,0:T(8,128)S(1)} %get-tuple-element.25), channel_id=1, source_target_pairs={{0,4},{4,0},{8,12},{12,8},{16,20},{20,16},{24,28},{28,24},{1,5},{5... | collective-permute-start | bytes 786440 | tf_op jit(solution)/shard_map/ppermute | solution.py:19
  39.9 9.3 %collective-permute-done.4 = f32[16,1,32,128]{3,2,1,0:T(8,128)S(1)} collective-permute-done((f32[16,1,32,128]{3,2,1,0:T(8,128)S(1)}, f32[16,1,32,128]{3,2,1,0:T(8,128)S(1)}, u32[]{:S(2)}, u32[]{:S(2)}) %collective-permute-start.4) | collective-permute-done | bytes 262176 | tf_op jit(solution)/shard_map/ppermute | solution.py:19
  52.5 2.5 %collective-permute-start.8 = (f32[16,1,32,128]{3,2,1,0:T(8,128)S(1)}, f32[16,1,32,128]{3,2,1,0:T(8,128)S(1)}, u32[]{:S(2)}, u32[]{:S(2)}) collective-permute-start(f32[16,1,32,128]{3,2,1,0:T(8,128)S(1)} %get-tuple-element.21), channel_id=1, source_target_pairs={{0,4},{4,0},{8,12},{12,8},{16,20},{20,16},{24,28},{28,24},{1,5},{5... | collective-permute-start | bytes 786440 | tf_op jit(solution)/shard_map/ppermute | solution.py:19
  57.1 8.4 %collective-permute-done.8 = f32[16,1,32,128]{3,2,1,0:T(8,128)S(1)} collective-permute-done((f32[16,1,32,128]{3,2,1,0:T(8,128)S(1)}, f32[16,1,32,128]{3,2,1,0:T(8,128)S(1)}, u32[]{:S(2)}, u32[]{:S(2)}) %collective-permute-start.8) | collective-permute-done | bytes 262176 | tf_op jit(solution)/shard_map/ppermute | solution.py:19
  68.3 2.5 %collective-permute-start.12 = (f32[16,1,32,128]{3,2,1,0:T(8,128)S(1)}, f32[16,1,32,128]{3,2,1,0:T(8,128)S(1)}, u32[]{:S(2)}, u32[]{:S(2)}) collective-permute-start(f32[16,1,32,128]{3,2,1,0:T(8,128)S(1)} %get-tuple-element.17), channel_id=1, source_target_pairs={{0,4},{4,0},{8,12},{12,8},{16,20},{20,16},{24,28},{28,24},{1,5},{5... | collective-permute-start | bytes 786440 | tf_op jit(solution)/shard_map/ppermute | solution.py:19
  73.1 7.5 %collective-permute-done.12 = f32[16,1,32,128]{3,2,1,0:T(8,128)S(1)} collective-permute-done((f32[16,1,32,128]{3,2,1,0:T(8,128)S(1)}, f32[16,1,32,128]{3,2,1,0:T(8,128)S(1)}, u32[]{:S(2)}, u32[]{:S(2)}) %collective-permute-start.12) | collective-permute-done | bytes 262176 | tf_op jit(solution)/shard_map/ppermute | solution.py:19
  81.9 2.7 %broadcast_multiply_fusion = (f32[16,8,32,128]{3,2,1,0:T(8,128)S(1)}, f32[16,8,32,128]{3,2,1,0:T(8,128)}) fusion(f32[16,8,32,128]{3,2,1,0:T(8,128)S(1)} %get-tuple-element.7, f32[16,8,32,128]{3,2,1,0:T(8,128)S(1)} %get-tuple-element.5, f32[16,8,32,127]{3,2,1,0:T(8,128)S(1)} %fusion.36, f32[16,8,33,128]{3,2,1,0:T(8,128)S(1)} %fusion.6, ...), kind=kLoop, calls=%fused_computation.131 | loop fusion | flops 7340032 | bytes 19120128 | tf_op jit(solution)/shard_map/div | solution.py:152
  84.7 3.6 %fusion.74 = f32[16,16]{0,1:T(8,128)S(1)} fusion(f32[16,8,32,128]{3,2,1,0:T(8,128)S(1)} %get-tuple-element.2), kind=kOutput, calls=%fused_computation.129 | convolution fusion | flops 100663296 | bytes 2098176 | tf_op jit(solution)/shard_map/kc,lc->kl/dot_general | solution.py:85
  89.8 3.4 %collective-permute-done.17 = f32[16,16]{0,1:T(8,128)S(1)} collective-permute-done((f32[16,16]{0,1:T(8,128)S(1)}, f32[16,16]{0,1:T(8,128)S(1)}, u32[]{:S(2)}, u32[]{:S(2)}) %collective-permute-start.17) | collective-permute-done | bytes 1056 | tf_op jit(solution)/shard_map/ppermute | solution.py:79
  93.1 2.5 %collective-permute-start.18 = (f32[16,16]{0,1:T(8,128)S(1)}, f32[16,16]{0,1:T(8,128)S(1)}, u32[]{:S(2)}, u32[]{:S(2)}) collective-permute-start(f32[16,16]{0,1:T(8,128)S(1)} %add.170), channel_id=1, source_target_pairs={{0,4},{4,0},{8,12},{12,8},{16,20},{20,16},{24,28},{28,24},{1,5},{5... | collective-permute-start | bytes 3080 | tf_op jit(solution)/shard_map/ppermute | solution.py:79
  99.2 2.0 %collective-permute-done.19 = f32[16,16]{0,1:T(8,128)S(1)} collective-permute-done((f32[16,16]{0,1:T(8,128)S(1)}, f32[16,16]{0,1:T(8,128)S(1)}, u32[]{:S(2)}, u32[]{:S(2)}) %collective-permute-start.19) | collective-permute-done | bytes 1056 | tf_op jit(solution)/shard_map/ppermute | solution.py:79
  101.2 2.5 %collective-permute-start.20 = (f32[16,16]{0,1:T(8,128)S(1)}, f32[16,16]{0,1:T(8,128)S(1)}, u32[]{:S(2)}, u32[]{:S(2)}) collective-permute-start(f32[16,16]{0,1:T(8,128)S(1)} %add.172), channel_id=1, source_target_pairs={{0,16},{4,20},{8,24},{12,28},{16,0},{20,4},{24,8},{28,12},{1,17},{... | collective-permute-start | bytes 3080 | tf_op jit(solution)/shard_map/ppermute | solution.py:79
  109.2 5.0 %collective-permute-done.21 = f32[16,1,32,128]{3,2,1,0:T(8,128)} collective-permute-done((f32[16,1,32,128]{3,2,1,0:T(8,128)S(1)}, f32[16,1,32,128]{3,2,1,0:T(8,128)}, u32[]{:S(2)}, u32[]{:S(2)}) %collective-permute-start.21) | collective-permute-done | bytes 262176 | tf_op jit(solution)/shard_map/ppermute | solution.py:19
  119.1 4.5 %fusion.77 = f32[16,16]{0,1:T(8,128)S(1)} fusion(f32[16,8,32,128]{3,2,1,0:T(8,128)S(1)} %fusion.34, f32[16,8,32,128]{3,2,1,0:T(8,128)S(1)} %get-tuple-element.2), kind=kOutput, calls=%fused_computation.130 | convolution fusion | flops 100663296 | bytes 4195328 | tf_op jit(solution)/shard_map/kc,lc->kl/dot_general | solution.py:85
  128.5 2.6 %collective-permute-start.27 = (f32[16,16]{0,1:T(8,128)S(1)}, f32[16,16]{0,1:T(8,128)S(1)}, u32[]{:S(2)}, u32[]{:S(2)}) collective-permute-start(f32[16,16]{0,1:T(8,128)S(1)} %add.179), channel_id=1, source_target_pairs={{0,4},{4,0},{8,12},{12,8},{16,20},{20,16},{24,28},{28,24},{1,5},{5... | collective-permute-start | bytes 3080 | tf_op jit(solution)/shard_map/ppermute | solution.py:79
  132.7 2.2 %collective-permute-start.28 = (f32[16,16]{0,1:T(8,128)S(1)}, f32[16,16]{0,1:T(8,128)S(1)}, u32[]{:S(2)}, u32[]{:S(2)}) collective-permute-start(f32[16,16]{0,1:T(8,128)S(1)} %add.180), channel_id=1, source_target_pairs={{0,8},{4,12},{8,0},{12,4},{16,24},{20,28},{24,16},{28,20},{1,9},{5... | collective-permute-start | bytes 3080 | tf_op jit(solution)/shard_map/ppermute | solution.py:79
  134.9 2.8 %fusion.28 = f32[16,32768]{1,0:T(8,128)S(1)} fusion(f32[16,16]{1,0:T(8,128)S(1)} %fusion.87, f32[2,8,256,128]{3,2,1,0:T(8,128)S(1)} %bitcast.83), kind=kOutput, calls=%fused_computation.66 | convolution fusion | flops 100663296 | bytes 4195328 | tf_op jit(solution)/shard_map/kl,lc->kc/dot_general | solution.py:89
  140.3 3.1 %fusion.25 = f32[16,32768]{1,0:T(8,128)S(1)} fusion(f32[16,16]{1,0:T(8,128)S(1)} %fusion.87, f32[2,8,256,128]{3,2,1,0:T(8,128)S(1)} %bitcast.84), kind=kOutput, calls=%fused_computation.63 | convolution fusion | flops 100663296 | bytes 4195328 | tf_op jit(solution)/shard_map/kl,lc->kc/dot_general | solution.py:89
  (153 shorter events, 51.2 us)
Async XLA Ops:
  4.7 11.4 %collective-permute-start = (f32[18,8,1,128]{3,2,1,0:T(1,128)}, f32[18,8,1,128]{3,2,1,0:T(1,128)}, u32[]{:S(2)}, u32[]{:S(2)}) collective-permute-start(f32[18,8,1,128]{3,2,1,0:T(1,128)} %broadcast_select_fusion.5), channel_id=1, source_target_pairs={{1,2},{2,1},{5,6},{6,5},{9,10},{10,9},{13,14},{14,13},{17,18},{18,... | collective-permute-start | bytes 221192 | tf_op jit(solution)/shard_map/ppermute | solution.py:20
  6.0 10.1 %collective-permute-start.1 = (f32[18,8,1,128]{3,2,1,0:T(1,128)S(1)}, f32[18,8,1,128]{3,2,1,0:T(1,128)}, u32[]{:S(2)}, u32[]{:S(2)}) collective-permute-start(f32[18,8,1,128]{3,2,1,0:T(1,128)S(1)} %get-tuple-element.10), channel_id=1, source_target_pairs={{0,1},{1,0},{2,3},{3,2},{4,5},{5,4},{6,7},{7,6},{8,9},{9,8},{10,11... | collective-permute-start | bytes 221192 | tf_op jit(solution)/shard_map/ppermute | solution.py:19
  9.8 7.3 %collective-permute-start.2 = (f32[18,1,32,128]{3,2,1,0:T(8,128)S(1)}, f32[18,1,32,128]{3,2,1,0:T(8,128)S(1)}, u32[]{:S(2)}, u32[]{:S(2)}) collective-permute-start(f32[18,1,32,128]{3,2,1,0:T(8,128)S(1)} %get-tuple-element.39), channel_id=1, source_target_pairs={{4,8},{8,4},{12,16},{16,12},{20,24},{24,20},{5,9},{9,5},{13,17},{1... | collective-permute-start | bytes 884744 | tf_op jit(solution)/shard_map/ppermute | solution.py:20
  10.5 16.4 %collective-permute-start.3 = (f32[18,1,32,128]{3,2,1,0:T(8,128)S(1)}, f32[18,1,32,128]{3,2,1,0:T(8,128)S(1)}, u32[]{:S(2)}, u32[]{:S(2)}) collective-permute-start(f32[18,1,32,128]{3,2,1,0:T(8,128)S(1)} %get-tuple-element.40), channel_id=1, source_target_pairs={{0,4},{4,0},{8,12},{12,8},{16,20},{20,16},{24,28},{28,24},{1,5},{5... | collective-permute-start | bytes 884744 | tf_op jit(solution)/shard_map/ppermute | solution.py:19
  35.3 13.9 %collective-permute-start.4 = (f32[16,1,32,128]{3,2,1,0:T(8,128)S(1)}, f32[16,1,32,128]{3,2,1,0:T(8,128)S(1)}, u32[]{:S(2)}, u32[]{:S(2)}) collective-permute-start(f32[16,1,32,128]{3,2,1,0:T(8,128)S(1)} %get-tuple-element.25), channel_id=1, source_target_pairs={{0,4},{4,0},{8,12},{12,8},{16,20},{20,16},{24,28},{28,24},{1,5},{5... | collective-permute-start | bytes 786440 | tf_op jit(solution)/shard_map/ppermute | solution.py:19
  37.8 11.4 %collective-permute-start.5 = (f32[16,1,32,128]{3,2,1,0:T(8,128)S(1)}, f32[16,1,32,128]{3,2,1,0:T(8,128)S(1)}, u32[]{:S(2)}, u32[]{:S(2)}) collective-permute-start(f32[16,1,32,128]{3,2,1,0:T(8,128)S(1)} %get-tuple-element.24), channel_id=1, source_target_pairs={{4,8},{8,4},{12,16},{16,12},{20,24},{24,20},{5,9},{9,5},{13,17},{1... | collective-permute-start | bytes 786440 | tf_op jit(solution)/shard_map/ppermute | solution.py:20
  52.5 13.1 %collective-permute-start.8 = (f32[16,1,32,128]{3,2,1,0:T(8,128)S(1)}, f32[16,1,32,128]{3,2,1,0:T(8,128)S(1)}, u32[]{:S(2)}, u32[]{:S(2)}) collective-permute-start(f32[16,1,32,128]{3,2,1,0:T(8,128)S(1)} %get-tuple-element.21), channel_id=1, source_target_pairs={{0,4},{4,0},{8,12},{12,8},{16,20},{20,16},{24,28},{28,24},{1,5},{5... | collective-permute-start | bytes 786440 | tf_op jit(solution)/shard_map/ppermute | solution.py:19
  55.0 10.5 %collective-permute-start.9 = (f32[16,1,32,128]{3,2,1,0:T(8,128)S(1)}, f32[16,1,32,128]{3,2,1,0:T(8,128)S(1)}, u32[]{:S(2)}, u32[]{:S(2)}) collective-permute-start(f32[16,1,32,128]{3,2,1,0:T(8,128)S(1)} %get-tuple-element.20), channel_id=1, source_target_pairs={{4,8},{8,4},{12,16},{16,12},{20,24},{24,20},{5,9},{9,5},{13,17},{1... | collective-permute-start | bytes 786440 | tf_op jit(solution)/shard_map/ppermute | solution.py:20
  68.3 12.3 %collective-permute-start.12 = (f32[16,1,32,128]{3,2,1,0:T(8,128)S(1)}, f32[16,1,32,128]{3,2,1,0:T(8,128)S(1)}, u32[]{:S(2)}, u32[]{:S(2)}) collective-permute-start(f32[16,1,32,128]{3,2,1,0:T(8,128)S(1)} %get-tuple-element.17), channel_id=1, source_target_pairs={{0,4},{4,0},{8,12},{12,8},{16,20},{20,16},{24,28},{28,24},{1,5},{5... | collective-permute-start | bytes 786440 | tf_op jit(solution)/shard_map/ppermute | solution.py:19
  70.9 9.8 %collective-permute-start.13 = (f32[16,1,32,128]{3,2,1,0:T(8,128)S(1)}, f32[16,1,32,128]{3,2,1,0:T(8,128)S(1)}, u32[]{:S(2)}, u32[]{:S(2)}) collective-permute-start(f32[16,1,32,128]{3,2,1,0:T(8,128)S(1)} %get-tuple-element.16), channel_id=1, source_target_pairs={{4,8},{8,4},{12,16},{16,12},{20,24},{24,20},{5,9},{9,5},{13,17},{1... | collective-permute-start | bytes 786440 | tf_op jit(solution)/shard_map/ppermute | solution.py:20
  71.5 1.6 %collective-permute-start.14 = (f32[16,8,1,128]{3,2,1,0:T(1,128)S(1)}, f32[16,8,1,128]{3,2,1,0:T(1,128)S(1)}, u32[]{:S(2)}, u32[]{:S(2)}) collective-permute-start(f32[16,8,1,128]{3,2,1,0:T(1,128)S(1)} %get-tuple-element.18), channel_id=1, source_target_pairs={{0,1},{1,0},{2,3},{3,2},{4,5},{5,4},{6,7},{7,6},{8,9},{9,8},{10,11... | collective-permute-start | bytes 196616 | tf_op jit(solution)/shard_map/ppermute | solution.py:19
  71.6 1.5 %collective-permute-start.15 = (f32[16,8,1,128]{3,2,1,0:T(1,128)S(1)}, f32[16,8,1,128]{3,2,1,0:T(1,128)S(1)}, u32[]{:S(2)}, u32[]{:S(2)}) collective-permute-start(f32[16,8,1,128]{3,2,1,0:T(1,128)S(1)} %get-tuple-element.19), channel_id=1, source_target_pairs={{1,2},{2,1},{5,6},{6,5},{9,10},{10,9},{13,14},{14,13},{17,18},{18,... | collective-permute-start | bytes 196616 | tf_op jit(solution)/shard_map/ppermute | solution.py:20
  89.5 3.7 %collective-permute-start.17 = (f32[16,16]{0,1:T(8,128)S(1)}, f32[16,16]{0,1:T(8,128)S(1)}, u32[]{:S(2)}, u32[]{:S(2)}) collective-permute-start(f32[16,16]{0,1:T(8,128)S(1)} %add.169), channel_id=1, source_target_pairs={{0,2},{1,3},{2,0},{3,1},{4,6},{5,7},{6,4},{7,5},{8,10},{9,11},{10,... | collective-permute-start | bytes 3080 | tf_op jit(solution)/shard_map/ppermute | solution.py:79
  93.1 4.4 %collective-permute-start.18 = (f32[16,16]{0,1:T(8,128)S(1)}, f32[16,16]{0,1:T(8,128)S(1)}, u32[]{:S(2)}, u32[]{:S(2)}) collective-permute-start(f32[16,16]{0,1:T(8,128)S(1)} %add.170), channel_id=1, source_target_pairs={{0,4},{4,0},{8,12},{12,8},{16,20},{20,16},{24,28},{28,24},{1,5},{5... | collective-permute-start | bytes 3080 | tf_op jit(solution)/shard_map/ppermute | solution.py:79
  97.6 3.7 %collective-permute-start.19 = (f32[16,16]{0,1:T(8,128)S(1)}, f32[16,16]{0,1:T(8,128)S(1)}, u32[]{:S(2)}, u32[]{:S(2)}) collective-permute-start(f32[16,16]{0,1:T(8,128)S(1)} %add.171), channel_id=1, source_target_pairs={{0,8},{4,12},{8,0},{12,4},{16,24},{20,28},{24,16},{28,20},{1,9},{5... | collective-permute-start | bytes 3080 | tf_op jit(solution)/shard_map/ppermute | solution.py:79
  101.2 6.3 %collective-permute-start.20 = (f32[16,16]{0,1:T(8,128)S(1)}, f32[16,16]{0,1:T(8,128)S(1)}, u32[]{:S(2)}, u32[]{:S(2)}) collective-permute-start(f32[16,16]{0,1:T(8,128)S(1)} %add.172), channel_id=1, source_target_pairs={{0,16},{4,20},{8,24},{12,28},{16,0},{20,4},{24,8},{28,12},{1,17},{... | collective-permute-start | bytes 3080 | tf_op jit(solution)/shard_map/ppermute | solution.py:79
  103.8 10.3 %collective-permute-start.21 = (f32[16,1,32,128]{3,2,1,0:T(8,128)S(1)}, f32[16,1,32,128]{3,2,1,0:T(8,128)}, u32[]{:S(2)}, u32[]{:S(2)}) collective-permute-start(f32[16,1,32,128]{3,2,1,0:T(8,128)S(1)} %get-tuple-element.13), channel_id=1, source_target_pairs={{0,4},{4,0},{8,12},{12,8},{16,20},{20,16},{24,28},{28,24},{1,5},{5... | collective-permute-start | bytes 786440 | tf_op jit(solution)/shard_map/ppermute | solution.py:19
  105.5 8.7 %collective-permute-start.22 = (f32[16,1,32,128]{3,2,1,0:T(8,128)S(1)}, f32[16,1,32,128]{3,2,1,0:T(8,128)}, u32[]{:S(2)}, u32[]{:S(2)}) collective-permute-start(f32[16,1,32,128]{3,2,1,0:T(8,128)S(1)} %get-tuple-element.12), channel_id=1, source_target_pairs={{4,8},{8,4},{12,16},{16,12},{20,24},{24,20},{5,9},{9,5},{13,17},{1... | collective-permute-start | bytes 786440 | tf_op jit(solution)/shard_map/ppermute | solution.py:20
  106.9 2.3 %collective-permute-start.23 = (f32[16,8,1,128]{3,2,1,0:T(1,128)S(1)}, f32[16,8,1,128]{3,2,1,0:T(1,128)S(1)}, u32[]{:S(2)}, u32[]{:S(2)}) collective-permute-start(f32[16,8,1,128]{3,2,1,0:T(1,128)S(1)} %get-tuple-element.14), channel_id=1, source_target_pairs={{0,1},{1,0},{2,3},{3,2},{4,5},{5,4},{6,7},{7,6},{8,9},{9,8},{10,11... | collective-permute-start | bytes 196616 | tf_op jit(solution)/shard_map/ppermute | solution.py:19
  106.9 2.3 %collective-permute-start.24 = (f32[16,8,1,128]{3,2,1,0:T(1,128)S(1)}, f32[16,8,1,128]{3,2,1,0:T(1,128)S(1)}, u32[]{:S(2)}, u32[]{:S(2)}) collective-permute-start(f32[16,8,1,128]{3,2,1,0:T(1,128)S(1)} %get-tuple-element.15), channel_id=1, source_target_pairs={{1,2},{2,1},{5,6},{6,5},{9,10},{10,9},{13,14},{14,13},{17,18},{18,... | collective-permute-start | bytes 196616 | tf_op jit(solution)/shard_map/ppermute | solution.py:20
  124.9 3.7 %collective-permute-start.26 = (f32[16,16]{0,1:T(8,128)S(1)}, f32[16,16]{0,1:T(8,128)S(1)}, u32[]{:S(2)}, u32[]{:S(2)}) collective-permute-start(f32[16,16]{0,1:T(8,128)S(1)} %add.178), channel_id=1, source_target_pairs={{0,2},{1,3},{2,0},{3,1},{4,6},{5,7},{6,4},{7,5},{8,10},{9,11},{10,... | collective-permute-start | bytes 3080 | tf_op jit(solution)/shard_map/ppermute | solution.py:79
  128.5 4.2 %collective-permute-start.27 = (f32[16,16]{0,1:T(8,128)S(1)}, f32[16,16]{0,1:T(8,128)S(1)}, u32[]{:S(2)}, u32[]{:S(2)}) collective-permute-start(f32[16,16]{0,1:T(8,128)S(1)} %add.179), channel_id=1, source_target_pairs={{0,4},{4,0},{8,12},{12,8},{16,20},{20,16},{24,28},{28,24},{1,5},{5... | collective-permute-start | bytes 3080 | tf_op jit(solution)/shard_map/ppermute | solution.py:79
  132.7 6.7 %collective-permute-start.28 = (f32[16,16]{0,1:T(8,128)S(1)}, f32[16,16]{0,1:T(8,128)S(1)}, u32[]{:S(2)}, u32[]{:S(2)}) collective-permute-start(f32[16,16]{0,1:T(8,128)S(1)} %add.180), channel_id=1, source_target_pairs={{0,8},{4,12},{8,0},{12,4},{16,24},{20,28},{24,16},{28,20},{1,9},{5... | collective-permute-start | bytes 3080 | tf_op jit(solution)/shard_map/ppermute | solution.py:79
  139.5 4.6 %collective-permute-start.29 = (f32[16,16]{0,1:T(8,128)S(1)}, f32[16,16]{0,1:T(8,128)S(1)}, u32[]{:S(2)}, u32[]{:S(2)}) collective-permute-start(f32[16,16]{0,1:T(8,128)S(1)} %add.181), channel_id=1, source_target_pairs={{0,16},{4,20},{8,24},{12,28},{16,0},{20,4},{24,8},{28,12},{1,17},{... | collective-permute-start | bytes 3080 | tf_op jit(solution)/shard_map/ppermute | solution.py:79
  (15 other events, 53.1 us)

commit v7 on v6

--- a/solution.py
+++ b/solution.py
@@ -125,6 +125,9 @@
     ):
         size = max(to_high.shape[0], to_low.shape[0])
         grow = lambda a: jnp.pad(a, ((0, size - a.shape[0]),) + ((0, 0),) * (a.ndim - 1))
+        if halos:
+            tie = 0.0 * (halos[0][0, 0, 0, 0] + halos[1][0, 0, 0, 0])
+            to_high, to_low = to_high + tie, to_low + tie
         low, high = swap_halos(grow(to_high), grow(to_low), axis)
         halos += [low[: to_high.shape[0]], high[: to_low.shape[0]]]
 

time: 149 us -> 156 us (1.047)
  waiting for transfers between devices: 50.6 us -> 55.2 us
    ppermute x10, waiting for transfers between devices: 40 us -> 44.2 us  [swap_halos(): got_first = lax.ppermute(jnp.where(even, to_high, to_low), axis, first)]
  transfers between devices with their start and end apart: 30 -> 30, of which waited for: 12 -> 12; matrix products, arithmetic and copies ran while one was open for 12% -> 11% of each run, Pallas kernels for 0% -> 0%
where the time goes in v7:
time: 156 us
  waiting for transfers between devices  55.2 us (35%)
  starting transfers between devices  39 us (25%)
  other arithmetic  34.2 us (22%)
  matrix products  16.5 us (11%)
  local copies, waits for them, and re-layouts  7.9 us (5%)
  between operations  2.76 us (2%)
    ppermute x10, waiting for transfers between devices, swap_halos(): got_first = lax.ppermute(jnp.where(even, to_high, to_low), axis, first)  44.2 us
    ppermute x10, starting transfers between devices, swap_halos(): got_first = lax.ppermute(jnp.where(even, to_high, to_low), axis, first)  18 us
    ppermute x10, starting transfers between devices, reduce_all(): value = value + lax.ppermute(value, axis, pairs)  12.8 us
    ppermute x10, waiting for transfers between devices, reduce_all(): value = value + lax.ppermute(value, axis, pairs)  11 us
    ppermute x10, starting transfers between devices, swap_halos(): got_second = lax.ppermute(jnp.where(even, to_low, to_high), axis, second)  8.23 us
    dot_general x2, matrix products, inner_products(): return jnp.einsum('kc,lc->kl', left, right, precision=lax.Precision.HIGHEST)  8.14 us
    dot_general x3, matrix products, combine(): jnp.einsum('kl,lc->kc', matrix, rows, precision=lax.Precision.HIGHEST)  7.88 us
    mul x5, other arithmetic, stencil(): flow_z = face_z * (centre[..., 1:] - centre[..., :-1])  5.73 us
  transfers between devices with their start and end apart: 30, of which 12 were waited for; matrix products, arithmetic and copies ran while one was open for 11% of the time, Pallas kernels for 0%

profile of v7, /device:TPU:0, one launch (start us, length us, event | category | flops | bytes accessed | tf_op | source)
XLA Modules:
  0.0 155.6 jit_solution(7036050413736149226)
XLA Ops:
  1.6 2.0 %broadcast_multiply_fusion.4 = f32[16,8,32,128]{3,2,1,0:T(8,128)S(1)} fusion(f32[16,8,32,128]{3,2,1,0:T(8,128)} %param.6, f32[8,32,128]{2,1,0:T(8,128)S(1)} %get-tuple-element.67), kind=kLoop, calls=%fused_computation.135 | loop fusion | flops 524288 | bytes 4325376 | tf_op jit(solution)/shard_map/mul | solution.py:109
  6.0 5.1 %collective-permute-start.1 = (f32[18,1,32,128]{3,2,1,0:T(8,128)}, f32[18,1,32,128]{3,2,1,0:T(8,128)}, u32[]{:S(2)}, u32[]{:S(2)}) collective-permute-start(f32[18,1,32,128]{3,2,1,0:T(8,128)} %get-tuple-element.37), channel_id=1, source_target_pairs={{0,4},{4,0},{8,12},{12,8},{16,20},{20,16},{24,28},{28,24},{1,5},{5... | collective-permute-start | bytes 884744 | tf_op jit(solution)/shard_map/ppermute | solution.py:19
  11.3 11.9 %collective-permute-done.1 = f32[18,1,32,128]{3,2,1,0:T(8,128)} collective-permute-done((f32[18,1,32,128]{3,2,1,0:T(8,128)}, f32[18,1,32,128]{3,2,1,0:T(8,128)}, u32[]{:S(2)}, u32[]{:S(2)}) %collective-permute-start.1) | collective-permute-done | bytes 294944 | tf_op jit(solution)/shard_map/ppermute | solution.py:19
  27.6 2.9 %collective-permute-start.3 = (f32[18,8,1,128]{3,2,1,0:T(1,128)S(1)}, f32[18,8,1,128]{3,2,1,0:T(1,128)S(1)}, u32[]{:S(2)}, u32[]{:S(2)}) collective-permute-start(f32[18,8,1,128]{3,2,1,0:T(1,128)S(1)} %get-tuple-element.53), channel_id=1, source_target_pairs={{0,1},{1,0},{2,3},{3,2},{4,5},{5,4},{6,7},{7,6},{8,9},{9,8},{10,11... | collective-permute-start | bytes 221192 | tf_op jit(solution)/shard_map/ppermute | solution.py:19
  32.2 1.9 %fusion.58 = f32[16,8,32,127]{3,2,1,0:T(8,128)} fusion(f32[16,8,32,128]{3,2,1,0:T(8,128)S(1)} %broadcast_multiply_fusion.4, f32[8,32,127]{2,1,0:T(8,128)S(1)} %slice_multiply_fusion.4), kind=kLoop, calls=%fused_computation.109 | loop fusion | flops 1040384 | bytes 6372352 | tf_op jit(solution)/shard_map/mul | solution.py:59
  36.1 3.7 %broadcast_multiply_fusion.3 = (f32[16,8,32,128]{3,2,1,0:T(8,128)S(1)}, f32[16,8,32,128]{3,2,1,0:T(8,128)S(1)}) fusion(f32[16,8,32,127]{3,2,1,0:T(8,128)} %fusion.58, f32[16,8,33,128]{3,2,1,0:T(8,128)S(1)} %fusion.18, f32[16,9,32,128]{3,2,1,0:T(8,128)S(1)} %fusion.20, f32[8,32,128]{2,1,0:T(8,128)S(1)} %get-tuple-element.49, f32[8,32,128]{2,1,0:T(8,128)S(1)} %slice.505, ...), kind=kLoop, calls=%fused_computation.134 | loop fusion | flops 6291456 | bytes 17154048 | tf_op jit(solution)/shard_map/div | solution.py:154
  40.0 2.5 %collective-permute-start.4 = (f32[16,1,32,128]{3,2,1,0:T(8,128)S(1)}, f32[16,1,32,128]{3,2,1,0:T(8,128)S(1)}, u32[]{:S(2)}, u32[]{:S(2)}) collective-permute-start(f32[16,1,32,128]{3,2,1,0:T(8,128)S(1)} %get-tuple-element.23), channel_id=1, source_target_pairs={{0,4},{4,0},{8,12},{12,8},{16,20},{20,16},{24,28},{28,24},{1,5},{5... | collective-permute-start | bytes 786440 | tf_op jit(solution)/shard_map/ppermute | solution.py:19
  45.3 9.6 %collective-permute-done.4 = f32[16,1,32,128]{3,2,1,0:T(8,128)S(1)} collective-permute-done((f32[16,1,32,128]{3,2,1,0:T(8,128)S(1)}, f32[16,1,32,128]{3,2,1,0:T(8,128)S(1)}, u32[]{:S(2)}, u32[]{:S(2)}) %collective-permute-start.4) | collective-permute-done | bytes 262176 | tf_op jit(solution)/shard_map/ppermute | solution.py:19
  58.1 2.5 %collective-permute-start.8 = (f32[16,1,32,128]{3,2,1,0:T(8,128)S(1)}, f32[16,1,32,128]{3,2,1,0:T(8,128)S(1)}, u32[]{:S(2)}, u32[]{:S(2)}) collective-permute-start(f32[16,1,32,128]{3,2,1,0:T(8,128)S(1)} %get-tuple-element.19), channel_id=1, source_target_pairs={{0,4},{4,0},{8,12},{12,8},{16,20},{20,16},{24,28},{28,24},{1,5},{5... | collective-permute-start | bytes 786440 | tf_op jit(solution)/shard_map/ppermute | solution.py:19
  62.7 9.3 %collective-permute-done.8 = f32[16,1,32,128]{3,2,1,0:T(8,128)S(1)} collective-permute-done((f32[16,1,32,128]{3,2,1,0:T(8,128)S(1)}, f32[16,1,32,128]{3,2,1,0:T(8,128)S(1)}, u32[]{:S(2)}, u32[]{:S(2)}) %collective-permute-start.8) | collective-permute-done | bytes 262176 | tf_op jit(solution)/shard_map/ppermute | solution.py:19
  74.9 2.5 %collective-permute-start.12 = (f32[16,1,32,128]{3,2,1,0:T(8,128)S(1)}, f32[16,1,32,128]{3,2,1,0:T(8,128)S(1)}, u32[]{:S(2)}, u32[]{:S(2)}) collective-permute-start(f32[16,1,32,128]{3,2,1,0:T(8,128)S(1)} %get-tuple-element.15), channel_id=1, source_target_pairs={{0,4},{4,0},{8,12},{12,8},{16,20},{20,16},{24,28},{28,24},{1,5},{5... | collective-permute-start | bytes 786440 | tf_op jit(solution)/shard_map/ppermute | solution.py:19
  79.7 8.3 %collective-permute-done.12 = f32[16,1,32,128]{3,2,1,0:T(8,128)S(1)} collective-permute-done((f32[16,1,32,128]{3,2,1,0:T(8,128)S(1)}, f32[16,1,32,128]{3,2,1,0:T(8,128)S(1)}, u32[]{:S(2)}, u32[]{:S(2)}) %collective-permute-start.12) | collective-permute-done | bytes 262176 | tf_op jit(solution)/shard_map/ppermute | solution.py:19
  89.3 2.7 %broadcast_multiply_fusion = (f32[16,8,32,128]{3,2,1,0:T(8,128)S(1)}, f32[16,8,32,128]{3,2,1,0:T(8,128)}) fusion(f32[16,8,32,128]{3,2,1,0:T(8,128)S(1)} %get-tuple-element.7, f32[16,8,32,128]{3,2,1,0:T(8,128)S(1)} %get-tuple-element.5, f32[16,8,32,127]{3,2,1,0:T(8,128)S(1)} %fusion.36, f32[16,8,33,128]{3,2,1,0:T(8,128)S(1)} %fusion.6, ...), kind=kLoop, calls=%fused_computation.131 | loop fusion | flops 7340032 | bytes 19120128 | tf_op jit(solution)/shard_map/div | solution.py:155
  92.1 3.6 %fusion.74 = f32[16,16]{0,1:T(8,128)S(1)} fusion(f32[16,8,32,128]{3,2,1,0:T(8,128)S(1)} %get-tuple-element.2), kind=kOutput, calls=%fused_computation.129 | convolution fusion | flops 100663296 | bytes 2098176 | tf_op jit(solution)/shard_map/kc,lc->kl/dot_general | solution.py:85
  96.9 3.6 %collective-permute-done.17 = f32[16,16]{0,1:T(8,128)S(1)} collective-permute-done((f32[16,16]{0,1:T(8,128)S(1)}, f32[16,16]{0,1:T(8,128)S(1)}, u32[]{:S(2)}, u32[]{:S(2)}) %collective-permute-start.17) | collective-permute-done | bytes 1056 | tf_op jit(solution)/shard_map/ppermute | solution.py:79
  100.5 2.5 %collective-permute-start.18 = (f32[16,16]{0,1:T(8,128)S(1)}, f32[16,16]{0,1:T(8,128)S(1)}, u32[]{:S(2)}, u32[]{:S(2)}) collective-permute-start(f32[16,16]{0,1:T(8,128)S(1)} %add.207), channel_id=1, source_target_pairs={{0,4},{4,0},{8,12},{12,8},{16,20},{20,16},{24,28},{28,24},{1,5},{5... | collective-permute-start | bytes 3080 | tf_op jit(solution)/shard_map/ppermute | solution.py:79
  103.0 1.9 %fusion.31 = f32[16,8,32,127]{3,2,1,0:T(8,128)} fusion(f32[16,8,32,128]{3,2,1,0:T(8,128)S(1)} %get-tuple-element.2, f32[8,32,127]{2,1,0:T(8,128)S(1)} %slice_multiply_fusion.4), kind=kLoop, calls=%fused_computation.70 | loop fusion | flops 1040384 | bytes 6372352 | tf_op jit(solution)/shard_map/mul | solution.py:59
  108.6 2.8 %collective-permute-start.20 = (f32[16,16]{0,1:T(8,128)S(1)}, f32[16,16]{0,1:T(8,128)S(1)}, u32[]{:S(2)}, u32[]{:S(2)}) collective-permute-start(f32[16,16]{0,1:T(8,128)S(1)} %add.209), channel_id=1, source_target_pairs={{0,16},{4,20},{8,24},{12,28},{16,0},{20,4},{24,8},{28,12},{1,17},{... | collective-permute-start | bytes 3080 | tf_op jit(solution)/shard_map/ppermute | solution.py:79
  116.7 5.0 %collective-permute-done.21 = f32[16,1,32,128]{3,2,1,0:T(8,128)} collective-permute-done((f32[16,1,32,128]{3,2,1,0:T(8,128)S(1)}, f32[16,1,32,128]{3,2,1,0:T(8,128)}, u32[]{:S(2)}, u32[]{:S(2)}) %collective-permute-start.21) | collective-permute-done | bytes 262176 | tf_op jit(solution)/shard_map/ppermute | solution.py:19
  126.7 4.5 %fusion.77 = f32[16,16]{0,1:T(8,128)S(1)} fusion(f32[16,8,32,128]{3,2,1,0:T(8,128)S(1)} %fusion.34, f32[16,8,32,128]{3,2,1,0:T(8,128)S(1)} %get-tuple-element.2), kind=kOutput, calls=%fused_computation.130 | convolution fusion | flops 100663296 | bytes 4195328 | tf_op jit(solution)/shard_map/kc,lc->kl/dot_general | solution.py:85
  136.1 2.6 %collective-permute-start.27 = (f32[16,16]{0,1:T(8,128)S(1)}, f32[16,16]{0,1:T(8,128)S(1)}, u32[]{:S(2)}, u32[]{:S(2)}) collective-permute-start(f32[16,16]{0,1:T(8,128)S(1)} %add.216), channel_id=1, source_target_pairs={{0,4},{4,0},{8,12},{12,8},{16,20},{20,16},{24,28},{28,24},{1,5},{5... | collective-permute-start | bytes 3080 | tf_op jit(solution)/shard_map/ppermute | solution.py:79
  140.3 2.2 %collective-permute-start.28 = (f32[16,16]{0,1:T(8,128)S(1)}, f32[16,16]{0,1:T(8,128)S(1)}, u32[]{:S(2)}, u32[]{:S(2)}) collective-permute-start(f32[16,16]{0,1:T(8,128)S(1)} %add.217), channel_id=1, source_target_pairs={{0,8},{4,12},{8,0},{12,4},{16,24},{20,28},{24,16},{28,20},{1,9},{5... | collective-permute-start | bytes 3080 | tf_op jit(solution)/shard_map/ppermute | solution.py:79
  142.5 2.8 %fusion.28 = f32[16,32768]{1,0:T(8,128)S(1)} fusion(f32[16,16]{1,0:T(8,128)S(1)} %fusion.86, f32[2,8,256,128]{3,2,1,0:T(8,128)S(1)} %bitcast.84), kind=kOutput, calls=%fused_computation.66 | convolution fusion | flops 100663296 | bytes 4195328 | tf_op jit(solution)/shard_map/kl,lc->kc/dot_general | solution.py:89
  147.6 3.1 %fusion.25 = f32[16,32768]{1,0:T(8,128)S(1)} fusion(f32[16,16]{1,0:T(8,128)S(1)} %fusion.86, f32[2,8,256,128]{3,2,1,0:T(8,128)S(1)} %bitcast.85), kind=kOutput, calls=%fused_computation.63 | convolution fusion | flops 100663296 | bytes 4195328 | tf_op jit(solution)/shard_map/kl,lc->kc/dot_general | solution.py:89
  (155 shorter events, 52.9 us)
Async XLA Ops:
  4.6 6.7 %collective-permute-start = (f32[18,1,32,128]{3,2,1,0:T(8,128)}, f32[18,1,32,128]{3,2,1,0:T(8,128)}, u32[]{:S(2)}, u32[]{:S(2)}) collective-permute-start(f32[18,1,32,128]{3,2,1,0:T(8,128)} %get-tuple-element.38), channel_id=1, source_target_pairs={{4,8},{8,4},{12,16},{16,12},{20,24},{24,20},{5,9},{9,5},{13,17},{1... | collective-permute-start | bytes 884744 | tf_op jit(solution)/shard_map/ppermute | solution.py:20
  6.0 17.3 %collective-permute-start.1 = (f32[18,1,32,128]{3,2,1,0:T(8,128)}, f32[18,1,32,128]{3,2,1,0:T(8,128)}, u32[]{:S(2)}, u32[]{:S(2)}) collective-permute-start(f32[18,1,32,128]{3,2,1,0:T(8,128)} %get-tuple-element.37), channel_id=1, source_target_pairs={{0,4},{4,0},{8,12},{12,8},{16,20},{20,16},{24,28},{28,24},{1,5},{5... | collective-permute-start | bytes 884744 | tf_op jit(solution)/shard_map/ppermute | solution.py:19
  26.9 4.7 %collective-permute-start.2 = (f32[18,8,1,128]{3,2,1,0:T(1,128)S(1)}, f32[18,8,1,128]{3,2,1,0:T(1,128)S(1)}, u32[]{:S(2)}, u32[]{:S(2)}) collective-permute-start(f32[18,8,1,128]{3,2,1,0:T(1,128)S(1)} %get-tuple-element.52), channel_id=1, source_target_pairs={{1,2},{2,1},{5,6},{6,5},{9,10},{10,9},{13,14},{14,13},{17,18},{18,... | collective-permute-start | bytes 221192 | tf_op jit(solution)/shard_map/ppermute | solution.py:20
  27.6 4.1 %collective-permute-start.3 = (f32[18,8,1,128]{3,2,1,0:T(1,128)S(1)}, f32[18,8,1,128]{3,2,1,0:T(1,128)S(1)}, u32[]{:S(2)}, u32[]{:S(2)}) collective-permute-start(f32[18,8,1,128]{3,2,1,0:T(1,128)S(1)} %get-tuple-element.53), channel_id=1, source_target_pairs={{0,1},{1,0},{2,3},{3,2},{4,5},{5,4},{6,7},{7,6},{8,9},{9,8},{10,11... | collective-permute-start | bytes 221192 | tf_op jit(solution)/shard_map/ppermute | solution.py:19
  40.0 14.9 %collective-permute-start.4 = (f32[16,1,32,128]{3,2,1,0:T(8,128)S(1)}, f32[16,1,32,128]{3,2,1,0:T(8,128)S(1)}, u32[]{:S(2)}, u32[]{:S(2)}) collective-permute-start(f32[16,1,32,128]{3,2,1,0:T(8,128)S(1)} %get-tuple-element.23), channel_id=1, source_target_pairs={{0,4},{4,0},{8,12},{12,8},{16,20},{20,16},{24,28},{28,24},{1,5},{5... | collective-permute-start | bytes 786440 | tf_op jit(solution)/shard_map/ppermute | solution.py:19
  42.6 12.3 %collective-permute-start.5 = (f32[16,1,32,128]{3,2,1,0:T(8,128)S(1)}, f32[16,1,32,128]{3,2,1,0:T(8,128)S(1)}, u32[]{:S(2)}, u32[]{:S(2)}) collective-permute-start(f32[16,1,32,128]{3,2,1,0:T(8,128)S(1)} %get-tuple-element.22), channel_id=1, source_target_pairs={{4,8},{8,4},{12,16},{16,12},{20,24},{24,20},{5,9},{9,5},{13,17},{1... | collective-permute-start | bytes 786440 | tf_op jit(solution)/shard_map/ppermute | solution.py:20
  43.2 2.0 %collective-permute-start.6 = (f32[16,8,1,128]{3,2,1,0:T(1,128)S(1)}, f32[16,8,1,128]{3,2,1,0:T(1,128)S(1)}, u32[]{:S(2)}, u32[]{:S(2)}) collective-permute-start(f32[16,8,1,128]{3,2,1,0:T(1,128)S(1)} %get-tuple-element.24), channel_id=1, source_target_pairs={{0,1},{1,0},{2,3},{3,2},{4,5},{5,4},{6,7},{7,6},{8,9},{9,8},{10,11... | collective-permute-start | bytes 196616 | tf_op jit(solution)/shard_map/ppermute | solution.py:19
  58.1 14.0 %collective-permute-start.8 = (f32[16,1,32,128]{3,2,1,0:T(8,128)S(1)}, f32[16,1,32,128]{3,2,1,0:T(8,128)S(1)}, u32[]{:S(2)}, u32[]{:S(2)}) collective-permute-start(f32[16,1,32,128]{3,2,1,0:T(8,128)S(1)} %get-tuple-element.19), channel_id=1, source_target_pairs={{0,4},{4,0},{8,12},{12,8},{16,20},{20,16},{24,28},{28,24},{1,5},{5... | collective-permute-start | bytes 786440 | tf_op jit(solution)/shard_map/ppermute | solution.py:19
  60.6 11.4 %collective-permute-start.9 = (f32[16,1,32,128]{3,2,1,0:T(8,128)S(1)}, f32[16,1,32,128]{3,2,1,0:T(8,128)S(1)}, u32[]{:S(2)}, u32[]{:S(2)}) collective-permute-start(f32[16,1,32,128]{3,2,1,0:T(8,128)S(1)} %get-tuple-element.18), channel_id=1, source_target_pairs={{4,8},{8,4},{12,16},{16,12},{20,24},{24,20},{5,9},{9,5},{13,17},{1... | collective-permute-start | bytes 786440 | tf_op jit(solution)/shard_map/ppermute | solution.py:20
  74.9 13.1 %collective-permute-start.12 = (f32[16,1,32,128]{3,2,1,0:T(8,128)S(1)}, f32[16,1,32,128]{3,2,1,0:T(8,128)S(1)}, u32[]{:S(2)}, u32[]{:S(2)}) collective-permute-start(f32[16,1,32,128]{3,2,1,0:T(8,128)S(1)} %get-tuple-element.15), channel_id=1, source_target_pairs={{0,4},{4,0},{8,12},{12,8},{16,20},{20,16},{24,28},{28,24},{1,5},{5... | collective-permute-start | bytes 786440 | tf_op jit(solution)/shard_map/ppermute | solution.py:19
  77.4 10.6 %collective-permute-start.13 = (f32[16,1,32,128]{3,2,1,0:T(8,128)S(1)}, f32[16,1,32,128]{3,2,1,0:T(8,128)S(1)}, u32[]{:S(2)}, u32[]{:S(2)}) collective-permute-start(f32[16,1,32,128]{3,2,1,0:T(8,128)S(1)} %get-tuple-element.14), channel_id=1, source_target_pairs={{4,8},{8,4},{12,16},{16,12},{20,24},{24,20},{5,9},{9,5},{13,17},{1... | collective-permute-start | bytes 786440 | tf_op jit(solution)/shard_map/ppermute | solution.py:20
  78.1 1.6 %collective-permute-start.14 = (f32[16,8,1,128]{3,2,1,0:T(1,128)S(1)}, f32[16,8,1,128]{3,2,1,0:T(1,128)S(1)}, u32[]{:S(2)}, u32[]{:S(2)}) collective-permute-start(f32[16,8,1,128]{3,2,1,0:T(1,128)S(1)} %get-tuple-element.16), channel_id=1, source_target_pairs={{0,1},{1,0},{2,3},{3,2},{4,5},{5,4},{6,7},{7,6},{8,9},{9,8},{10,11... | collective-permute-start | bytes 196616 | tf_op jit(solution)/shard_map/ppermute | solution.py:19
  96.9 3.7 %collective-permute-start.17 = (f32[16,16]{0,1:T(8,128)S(1)}, f32[16,16]{0,1:T(8,128)S(1)}, u32[]{:S(2)}, u32[]{:S(2)}) collective-permute-start(f32[16,16]{0,1:T(8,128)S(1)} %add.206), channel_id=1, source_target_pairs={{0,2},{1,3},{2,0},{3,1},{4,6},{5,7},{6,4},{7,5},{8,10},{9,11},{10,... | collective-permute-start | bytes 3080 | tf_op jit(solution)/shard_map/ppermute | solution.py:79
  100.5 4.4 %collective-permute-start.18 = (f32[16,16]{0,1:T(8,128)S(1)}, f32[16,16]{0,1:T(8,128)S(1)}, u32[]{:S(2)}, u32[]{:S(2)}) collective-permute-start(f32[16,16]{0,1:T(8,128)S(1)} %add.207), channel_id=1, source_target_pairs={{0,4},{4,0},{8,12},{12,8},{16,20},{20,16},{24,28},{28,24},{1,5},{5... | collective-permute-start | bytes 3080 | tf_op jit(solution)/shard_map/ppermute | solution.py:79
  104.9 3.7 %collective-permute-start.19 = (f32[16,16]{0,1:T(8,128)S(1)}, f32[16,16]{0,1:T(8,128)S(1)}, u32[]{:S(2)}, u32[]{:S(2)}) collective-permute-start(f32[16,16]{0,1:T(8,128)S(1)} %add.208), channel_id=1, source_target_pairs={{0,8},{4,12},{8,0},{12,4},{16,24},{20,28},{24,16},{28,20},{1,9},{5... | collective-permute-start | bytes 3080 | tf_op jit(solution)/shard_map/ppermute | solution.py:79
  108.6 6.5 %collective-permute-start.20 = (f32[16,16]{0,1:T(8,128)S(1)}, f32[16,16]{0,1:T(8,128)S(1)}, u32[]{:S(2)}, u32[]{:S(2)}) collective-permute-start(f32[16,16]{0,1:T(8,128)S(1)} %add.209), channel_id=1, source_target_pairs={{0,16},{4,20},{8,24},{12,28},{16,0},{20,4},{24,8},{28,12},{1,17},{... | collective-permute-start | bytes 3080 | tf_op jit(solution)/shard_map/ppermute | solution.py:79
  111.5 10.2 %collective-permute-start.21 = (f32[16,1,32,128]{3,2,1,0:T(8,128)S(1)}, f32[16,1,32,128]{3,2,1,0:T(8,128)}, u32[]{:S(2)}, u32[]{:S(2)}) collective-permute-start(f32[16,1,32,128]{3,2,1,0:T(8,128)S(1)} %get-tuple-element.11), channel_id=1, source_target_pairs={{0,4},{4,0},{8,12},{12,8},{16,20},{20,16},{24,28},{28,24},{1,5},{5... | collective-permute-start | bytes 786440 | tf_op jit(solution)/shard_map/ppermute | solution.py:19
  113.1 8.7 %collective-permute-start.22 = (f32[16,1,32,128]{3,2,1,0:T(8,128)S(1)}, f32[16,1,32,128]{3,2,1,0:T(8,128)}, u32[]{:S(2)}, u32[]{:S(2)}) collective-permute-start(f32[16,1,32,128]{3,2,1,0:T(8,128)S(1)} %get-tuple-element.10), channel_id=1, source_target_pairs={{4,8},{8,4},{12,16},{16,12},{20,24},{24,20},{5,9},{9,5},{13,17},{1... | collective-permute-start | bytes 786440 | tf_op jit(solution)/shard_map/ppermute | solution.py:20
  114.4 2.3 %collective-permute-start.23 = (f32[16,8,1,128]{3,2,1,0:T(1,128)S(1)}, f32[16,8,1,128]{3,2,1,0:T(1,128)S(1)}, u32[]{:S(2)}, u32[]{:S(2)}) collective-permute-start(f32[16,8,1,128]{3,2,1,0:T(1,128)S(1)} %get-tuple-element.12), channel_id=1, source_target_pairs={{0,1},{1,0},{2,3},{3,2},{4,5},{5,4},{6,7},{7,6},{8,9},{9,8},{10,11... | collective-permute-start | bytes 196616 | tf_op jit(solution)/shard_map/ppermute | solution.py:19
  114.4 2.3 %collective-permute-start.24 = (f32[16,8,1,128]{3,2,1,0:T(1,128)S(1)}, f32[16,8,1,128]{3,2,1,0:T(1,128)S(1)}, u32[]{:S(2)}, u32[]{:S(2)}) collective-permute-start(f32[16,8,1,128]{3,2,1,0:T(1,128)S(1)} %get-tuple-element.13), channel_id=1, source_target_pairs={{1,2},{2,1},{5,6},{6,5},{9,10},{10,9},{13,14},{14,13},{17,18},{18,... | collective-permute-start | bytes 196616 | tf_op jit(solution)/shard_map/ppermute | solution.py:20
  132.4 3.7 %collective-permute-start.26 = (f32[16,16]{0,1:T(8,128)S(1)}, f32[16,16]{0,1:T(8,128)S(1)}, u32[]{:S(2)}, u32[]{:S(2)}) collective-permute-start(f32[16,16]{0,1:T(8,128)S(1)} %add.215), channel_id=1, source_target_pairs={{0,2},{1,3},{2,0},{3,1},{4,6},{5,7},{6,4},{7,5},{8,10},{9,11},{10,... | collective-permute-start | bytes 3080 | tf_op jit(solution)/shard_map/ppermute | solution.py:79
  136.1 4.2 %collective-permute-start.27 = (f32[16,16]{0,1:T(8,128)S(1)}, f32[16,16]{0,1:T(8,128)S(1)}, u32[]{:S(2)}, u32[]{:S(2)}) collective-permute-start(f32[16,16]{0,1:T(8,128)S(1)} %add.216), channel_id=1, source_target_pairs={{0,4},{4,0},{8,12},{12,8},{16,20},{20,16},{24,28},{28,24},{1,5},{5... | collective-permute-start | bytes 3080 | tf_op jit(solution)/shard_map/ppermute | solution.py:79
  140.3 6.7 %collective-permute-start.28 = (f32[16,16]{0,1:T(8,128)S(1)}, f32[16,16]{0,1:T(8,128)S(1)}, u32[]{:S(2)}, u32[]{:S(2)}) collective-permute-start(f32[16,16]{0,1:T(8,128)S(1)} %add.217), channel_id=1, source_target_pairs={{0,8},{4,12},{8,0},{12,4},{16,24},{20,28},{24,16},{28,20},{1,9},{5... | collective-permute-start | bytes 3080 | tf_op jit(solution)/shard_map/ppermute | solution.py:79
  147.1 4.6 %collective-permute-start.29 = (f32[16,16]{0,1:T(8,128)S(1)}, f32[16,16]{0,1:T(8,128)S(1)}, u32[]{:S(2)}, u32[]{:S(2)}) collective-permute-start(f32[16,16]{0,1:T(8,128)S(1)} %add.218), channel_id=1, source_target_pairs={{0,16},{4,20},{8,24},{12,28},{16,0},{20,4},{24,8},{28,12},{1,17},{... | collective-permute-start | bytes 3080 | tf_op jit(solution)/shard_map/ppermute | solution.py:79
  (15 other events, 44.7 us)

commit v8 on v6

--- a/solution.py
+++ b/solution.py
@@ -4,6 +4,7 @@
 from jax.sharding import PartitionSpec as P
 
 FILTER_STEPS = 2
+CHAINS = 2
 
 
 FILTER_CENTRE = 22.0
@@ -141,17 +142,23 @@
 
     fields_one = assemble(fields, *(widen(halo, keep) for halo, keep in zip(halos, sent)))
     together = assemble(field, *(halo[:vectors] for halo in halos))
-    first = True
-    for repeat in range(FILTER_STEPS):
-        if first:
-            applied = stencil(together, fields_one)
-            first = False
-        else:
-            applied = operate(field, fields_one)
-        middle = (applied - FILTER_CENTRE * field) / FILTER_HALF
-        field = (
-            2.0 * (operate(middle, fields_one) - FILTER_CENTRE * middle) / FILTER_HALF - field
-        ) / FILTER_NORM
+    applied = stencil(together, fields_one)
+    share = vectors // CHAINS
+    finished = []
+    for chain in range(CHAINS):
+        part = slice(chain * share, (chain + 1) * share)
+        field_part = field[part]
+        applied_part = applied[part]
+        for repeat in range(FILTER_STEPS):
+            if repeat:
+                applied_part = operate(field_part, fields_one)
+            middle = (applied_part - FILTER_CENTRE * field_part) / FILTER_HALF
+            field_part = (
+                2.0 * (operate(middle, fields_one) - FILTER_CENTRE * middle) / FILTER_HALF
+                - field_part
+            ) / FILTER_NORM
+        finished.append(field_part)
+    field = jnp.concatenate(finished)
     flattened = field.reshape(vectors, -1)
     gram_sum = reduce_all(inner_products(flattened, flattened)) / cell_total
     inverse = triangle_inverse(gram_sum, vectors)

time: 149 us -> 182 us (1.22)
  starting transfers between devices: 38.7 us -> 72.5 us
  local copies, waits for them, and re-layouts: 6.88 us -> 12.8 us
  waiting for transfers between devices: 50.6 us -> 47.8 us
  matrix products: 16.5 us -> 13.9 us
    ppermute x10 -> x16, starting transfers between devices: 17.6 us -> 47.3 us  [swap_halos(): got_first = lax.ppermute(jnp.where(even, to_high, to_low), axis, first)]
    ppermute x10 -> x16, starting transfers between devices: 8.16 us -> 12.7 us  [swap_halos(): got_second = lax.ppermute(jnp.where(even, to_low, to_high), axis, second)]
    mul x2 -> x3, other arithmetic: 1.3 us -> 5.43 us  [stencil(): return inner_wet * (diag_term[1:-1, 1:-1] * centre + net_x + net_y + net_z)]
    ppermute x10, waiting for transfers between devices: 10.5 us -> 6.99 us  [reduce_all(): value = value + lax.ppermute(value, axis, pairs)]
    div x2, other arithmetic: 5.17 us -> 1.76 us  [on_device(): middle = (applied_part - FILTER_CENTRE * field_part) / FILTER_HALF]
    mul x5, other arithmetic: 4.31 us -> 1.55 us  [stencil(): flow_y = face_y * (values[..., 1:-1, 1:, :] - values[..., 1:-1, :-1, :])]
    dot_general x2, matrix products: 8.14 us -> 5.78 us  [inner_products(): return jnp.einsum('kc,lc->kl', left, right, precision=lax.Precision.HIGHEST)]
    concatenate x0 -> x1, local copies, waits for them, and re-layouts: none -> 2.28 us  [on_device(): field = jnp.concatenate(finished)]
  transfers between devices with their start and end apart: 30 -> 42, of which waited for: 12 -> 14; matrix products, arithmetic and copies ran while one was open for 12% -> 13% of each run, Pallas kernels for 0% -> 0%
where the time goes in v8:
time: 182 us; the launch traced here: 181 us
  starting transfers between devices  72.5 us (40%)
  waiting for transfers between devices  47.8 us (26%)
  other arithmetic  32.8 us (18%)
  matrix products  13.9 us (8%)
  local copies, waits for them, and re-layouts  12.8 us (7%)
    ppermute x16, starting transfers between devices, swap_halos(): got_first = lax.ppermute(jnp.where(even, to_high, to_low), axis, first)  47.3 us
    ppermute x16, waiting for transfers between devices, swap_halos(): got_first = lax.ppermute(jnp.where(even, to_high, to_low), axis, first)  40.8 us
    ppermute x16, starting transfers between devices, swap_halos(): got_second = lax.ppermute(jnp.where(even, to_low, to_high), axis, second)  12.7 us
    ppermute x10, starting transfers between devices, reduce_all(): value = value + lax.ppermute(value, axis, pairs)  12.5 us
    dot_general x3, matrix products, combine(): jnp.einsum('kl,lc->kc', matrix, rows, precision=lax.Precision.HIGHEST)  7.6 us
    ppermute x10, waiting for transfers between devices, reduce_all(): value = value + lax.ppermute(value, axis, pairs)  6.99 us
    unnamed x16, local copies, waits for them, and re-layouts  5.79 us
    dot_general x2, matrix products, inner_products(): return jnp.einsum('kc,lc->kl', left, right, precision=lax.Precision.HIGHEST)  5.78 us
  transfers between devices with their start and end apart: 42, of which 14 were waited for; matrix products, arithmetic and copies ran while one was open for 13% of the time, Pallas kernels for 0%

profile of v8, /device:TPU:0, one launch (start us, length us, event | category | flops | bytes accessed | tf_op | source)
XLA Modules:
  0.0 181.4 jit_solution(1759824323509888339)
XLA Ops:
  2.3 2.9 %copy_multiply_fusion = f32[16,8,32,128]{3,0,2,1:T(8,128)S(1)} fusion(f32[16,8,32,128]{3,2,1,0:T(8,128)} %param.6, f32[8,32,128]{2,1,0:T(8,128)S(1)} %convert_element_type.49), kind=kLoop, calls=%fused_computation.66 | loop fusion | flops 524288 | bytes 4325376 | tf_op jit(solution)/shard_map/mul | solution.py:110
  10.1 4.6 %collective-permute-start.3 = (f32[18,1,32,128]{3,0,2,1:T(8,128)}, f32[18,1,32,128]{3,0,2,1:T(8,128)}, u32[]{:S(2)}, u32[]{:S(2)}) collective-permute-start(f32[18,1,32,128]{3,0,2,1:T(8,128)} %get-tuple-element.57), channel_id=1, source_target_pairs={{0,4},{4,0},{8,12},{12,8},{16,20},{20,16},{24,28},{28,24},{1,5},{5... | collective-permute-start | bytes 884744 | tf_op jit(solution)/shard_map/ppermute | solution.py:20
  18.3 13.9 %collective-permute-done.3 = f32[18,1,32,128]{3,0,2,1:T(8,128)} collective-permute-done((f32[18,1,32,128]{3,0,2,1:T(8,128)}, f32[18,1,32,128]{3,0,2,1:T(8,128)}, u32[]{:S(2)}, u32[]{:S(2)}) %collective-permute-start.3) | collective-permute-done | bytes 294944 | tf_op jit(solution)/shard_map/ppermute | solution.py:20
  37.1 2.9 %fusion.27 = f32[16,8,32,128]{3,0,2,1:T(8,128)S(1)} fusion(f32[16,8,33,128]{3,0,2,1:T(8,128)S(1)} %fusion.8, f32[16,9,32,128]{3,0,2,1:T(8,128)S(1)} %fusion, f32[16,8,32,127]{3,0,2,1:T(8,128)S(1)} %fusion.24, f32[8,32,128]{2,1,0:T(8,128)S(1)} %get-tuple-element.78, f32[8,32,128]{2,1,0:T(8,128)S(1)} %slice.720, f32[8,32,128]{2,1,0:T(8,128)S(1)} %convert_element_type.49, ...), kind=kLoop, calls=%fused_computation.63 | loop fusion | flops 4718592 | bytes 15056896 | tf_op jit(solution)/shard_map/mul | solution.py:65
  45.7 5.3 %collective-permute-start.4 = (f32[8,1,32,128]{3,0,2,1:T(8,128)S(1)}, f32[8,1,32,128]{3,0,2,1:T(8,128)S(1)}, u32[]{:S(2)}, u32[]{:S(2)}) collective-permute-start(f32[8,1,32,128]{3,0,2,1:T(8,128)S(1)} %get-tuple-element.39), channel_id=1, source_target_pairs={{0,4},{4,0},{8,12},{12,8},{16,20},{20,16},{24,28},{28,24},{1,5},{5... | collective-permute-start | bytes 393224 | tf_op jit(solution)/shard_map/ppermute | solution.py:20
  51.7 4.3 %collective-permute-start.16 = (f32[8,1,32,128]{3,0,2,1:T(8,128)S(1)}, f32[8,1,32,128]{3,0,2,1:T(8,128)S(1)}, u32[]{:S(2)}, u32[]{:S(2)}) collective-permute-start(f32[8,1,32,128]{3,0,2,1:T(8,128)S(1)} %get-tuple-element.51), channel_id=1, source_target_pairs={{0,4},{4,0},{8,12},{12,8},{16,20},{20,16},{24,28},{28,24},{1,5},{5... | collective-permute-start | bytes 393224 | tf_op jit(solution)/shard_map/ppermute | solution.py:20
  56.0 3.6 %collective-permute-done.4 = f32[8,1,32,128]{3,0,2,1:T(8,128)S(1)} collective-permute-done((f32[8,1,32,128]{3,0,2,1:T(8,128)S(1)}, f32[8,1,32,128]{3,0,2,1:T(8,128)S(1)}, u32[]{:S(2)}, u32[]{:S(2)}) %collective-permute-start.4) | collective-permute-done | bytes 131104 | tf_op jit(solution)/shard_map/ppermute | solution.py:20
  59.7 2.8 %collective-permute-done.16 = f32[8,1,32,128]{3,0,2,1:T(8,128)S(1)} collective-permute-done((f32[8,1,32,128]{3,0,2,1:T(8,128)S(1)}, f32[8,1,32,128]{3,0,2,1:T(8,128)S(1)}, u32[]{:S(2)}, u32[]{:S(2)}) %collective-permute-start.16) | collective-permute-done | bytes 131104 | tf_op jit(solution)/shard_map/ppermute | solution.py:20
  69.4 5.3 %collective-permute-start.8 = (f32[8,1,32,128]{3,0,2,1:T(8,128)S(1)}, f32[8,1,32,128]{3,0,2,1:T(8,128)S(1)}, u32[]{:S(2)}, u32[]{:S(2)}) collective-permute-start(f32[8,1,32,128]{3,0,2,1:T(8,128)S(1)} %get-tuple-element.35), channel_id=1, source_target_pairs={{0,4},{4,0},{8,12},{12,8},{16,20},{20,16},{24,28},{28,24},{1,5},{5... | collective-permute-start | bytes 393224 | tf_op jit(solution)/shard_map/ppermute | solution.py:20
  75.6 4.3 %collective-permute-start.20 = (f32[8,1,32,128]{3,0,2,1:T(8,128)S(1)}, f32[8,1,32,128]{3,0,2,1:T(8,128)S(1)}, u32[]{:S(2)}, u32[]{:S(2)}) collective-permute-start(f32[8,1,32,128]{3,0,2,1:T(8,128)S(1)} %get-tuple-element.47), channel_id=1, source_target_pairs={{0,4},{4,0},{8,12},{12,8},{16,20},{20,16},{24,28},{28,24},{1,5},{5... | collective-permute-start | bytes 393224 | tf_op jit(solution)/shard_map/ppermute | solution.py:20
  80.0 2.9 %collective-permute-done.8 = f32[8,1,32,128]{3,0,2,1:T(8,128)S(1)} collective-permute-done((f32[8,1,32,128]{3,0,2,1:T(8,128)S(1)}, f32[8,1,32,128]{3,0,2,1:T(8,128)S(1)}, u32[]{:S(2)}, u32[]{:S(2)}) %collective-permute-start.8) | collective-permute-done | bytes 131104 | tf_op jit(solution)/shard_map/ppermute | solution.py:20
  83.0 2.8 %collective-permute-done.20 = f32[8,1,32,128]{3,0,2,1:T(8,128)S(1)} collective-permute-done((f32[8,1,32,128]{3,0,2,1:T(8,128)S(1)}, f32[8,1,32,128]{3,0,2,1:T(8,128)S(1)}, u32[]{:S(2)}, u32[]{:S(2)}) %collective-permute-start.20) | collective-permute-done | bytes 131104 | tf_op jit(solution)/shard_map/ppermute | solution.py:20
  93.7 5.3 %collective-permute-start.12 = (f32[8,1,32,128]{3,0,2,1:T(8,128)S(1)}, f32[8,1,32,128]{3,0,2,1:T(8,128)S(1)}, u32[]{:S(2)}, u32[]{:S(2)}) collective-permute-start(f32[8,1,32,128]{3,0,2,1:T(8,128)S(1)} %get-tuple-element.31), channel_id=1, source_target_pairs={{0,4},{4,0},{8,12},{12,8},{16,20},{20,16},{24,28},{28,24},{1,5},{5... | collective-permute-start | bytes 393224 | tf_op jit(solution)/shard_map/ppermute | solution.py:20
  99.7 4.3 %collective-permute-start.24 = (f32[8,1,32,128]{3,0,2,1:T(8,128)S(1)}, f32[8,1,32,128]{3,0,2,1:T(8,128)S(1)}, u32[]{:S(2)}, u32[]{:S(2)}) collective-permute-start(f32[8,1,32,128]{3,0,2,1:T(8,128)S(1)} %get-tuple-element.43), channel_id=1, source_target_pairs={{0,4},{4,0},{8,12},{12,8},{16,20},{20,16},{24,28},{28,24},{1,5},{5... | collective-permute-start | bytes 393224 | tf_op jit(solution)/shard_map/ppermute | solution.py:20
  104.1 3.7 %collective-permute-done.12 = f32[8,1,32,128]{3,0,2,1:T(8,128)S(1)} collective-permute-done((f32[8,1,32,128]{3,0,2,1:T(8,128)S(1)}, f32[8,1,32,128]{3,0,2,1:T(8,128)S(1)}, u32[]{:S(2)}, u32[]{:S(2)}) %collective-permute-start.12) | collective-permute-done | bytes 131104 | tf_op jit(solution)/shard_map/ppermute | solution.py:20
  107.7 2.8 %collective-permute-done.24 = f32[8,1,32,128]{3,0,2,1:T(8,128)S(1)} collective-permute-done((f32[8,1,32,128]{3,0,2,1:T(8,128)S(1)}, f32[8,1,32,128]{3,0,2,1:T(8,128)S(1)}, u32[]{:S(2)}, u32[]{:S(2)}) %collective-permute-start.24) | collective-permute-done | bytes 131104 | tf_op jit(solution)/shard_map/ppermute | solution.py:20
  112.9 2.9 %convolution_bitcast_fusion.1 = f32[16,16]{0,1:T(8,128)S(1)} fusion(f32[8,8,32,128]{3,0,2,1:T(8,128)S(1)} %get-tuple-element.61, f32[8,8,32,128]{3,0,2,1:T(8,128)S(1)} %get-tuple-element.60), kind=kOutput, calls=%fused_computation.95 | convolution fusion | flops 101187584 | bytes 2098176 | tf_op jit(solution)/shard_map/kc,lc->kl/dot_general | solution.py:86
  120.6 2.5 %collective-permute-start.30 = (f32[16,16]{0,1:T(8,128)S(1)}, f32[16,16]{0,1:T(8,128)S(1)}, u32[]{:S(2)}, u32[]{:S(2)}) collective-permute-start(f32[16,16]{0,1:T(8,128)S(1)} %add.236), channel_id=1, source_target_pairs={{0,4},{4,0},{8,12},{12,8},{16,20},{20,16},{24,28},{28,24},{1,5},{5... | collective-permute-start | bytes 3080 | tf_op jit(solution)/shard_map/ppermute | solution.py:80
  128.4 3.0 %collective-permute-start.32 = (f32[16,16]{0,1:T(8,128)S(1)}, f32[16,16]{0,1:T(8,128)S(1)}, u32[]{:S(2)}, u32[]{:S(2)}) collective-permute-start(f32[16,16]{0,1:T(8,128)S(1)} %add.238), channel_id=1, source_target_pairs={{0,16},{4,20},{8,24},{12,28},{16,0},{20,4},{24,8},{28,12},{1,17},{... | collective-permute-start | bytes 3080 | tf_op jit(solution)/shard_map/ppermute | solution.py:80
  135.3 4.3 %collective-permute-start.33 = (f32[16,1,32,128]{3,0,2,1:T(8,128)S(1)}, f32[16,1,32,128]{3,0,2,1:T(8,128)S(1)}, u32[]{:S(2)}, u32[]{:S(2)}) collective-permute-start(f32[16,1,32,128]{3,0,2,1:T(8,128)S(1)} %get-tuple-element.20), channel_id=1, source_target_pairs={{0,4},{4,0},{8,12},{12,8},{16,20},{20,16},{24,28},{28,24},{1,5},{5... | collective-permute-start | bytes 786440 | tf_op jit(solution)/shard_map/ppermute | solution.py:20
  142.1 8.4 %collective-permute-done.33 = f32[16,1,32,128]{3,0,2,1:T(8,128)S(1)} collective-permute-done((f32[16,1,32,128]{3,0,2,1:T(8,128)S(1)}, f32[16,1,32,128]{3,0,2,1:T(8,128)S(1)}, u32[]{:S(2)}, u32[]{:S(2)}) %collective-permute-start.33) | collective-permute-done | bytes 262176 | tf_op jit(solution)/shard_map/ppermute | solution.py:20
  154.9 2.9 %convolution_bitcast_fusion = f32[16,16]{0,1:T(8,128)S(1)} fusion(f32[16,8,32,128]{3,0,2,1:T(8,128)S(1)} %get-tuple-element.17, f32[8,8,32,128]{3,0,2,1:T(8,128)S(1)} %get-tuple-element.61, f32[8,8,32,128]{3,0,2,1:T(8,128)S(1)} %get-tuple-element.60), kind=kOutput, calls=%fused_computation.94 | convolution fusion | flops 101187584 | bytes 4195328 | tf_op jit(solution)/shard_map/kc,lc->kl/dot_general | solution.py:86
  168.9 2.8 %fusion.17 = f32[16,32768]{1,0:T(8,128)S(1)} fusion(f32[16,16]{1,0:T(8,128)S(1)} %fusion.120, f32[2,8,256,128]{3,2,1,0:T(8,128)S(1)} %bitcast.60), kind=kOutput, calls=%fused_computation.49 | convolution fusion | flops 100663296 | bytes 4195328 | tf_op jit(solution)/shard_map/kl,lc->kc/dot_general | solution.py:90
  172.8 2.8 %fusion.14 = f32[16,32768]{1,0:T(8,128)S(1)} fusion(f32[16,16]{1,0:T(8,128)S(1)} %fusion.120, f32[2,8,256,128]{3,2,1,0:T(8,128)S(1)} %bitcast.61), kind=kOutput, calls=%fused_computation.46 | convolution fusion | flops 100663296 | bytes 4195328 | tf_op jit(solution)/shard_map/kl,lc->kc/dot_general | solution.py:90
  (185 shorter events, 78.4 us)
Async XLA Ops:
  5.9 11.2 %collective-permute-start.1 = (f32[18,8,1,128]{3,0,2,1:T(8,128)}, f32[18,8,1,128]{3,0,2,1:T(8,128)}, u32[]{:S(2)}, u32[]{:S(2)}) collective-permute-start(f32[18,8,1,128]{3,0,2,1:T(8,128)} %get-tuple-element.93), channel_id=1, source_target_pairs={{0,1},{1,0},{2,3},{3,2},{4,5},{5,4},{6,7},{7,6},{8,9},{9,8},{10,11... | collective-permute-start | bytes 221192 | tf_op jit(solution)/shard_map/ppermute | solution.py:20
  6.4 10.8 %collective-permute-start = (f32[18,8,1,128]{3,0,2,1:T(8,128)}, f32[18,8,1,128]{3,0,2,1:T(8,128)}, u32[]{:S(2)}, u32[]{:S(2)}) collective-permute-start(f32[18,8,1,128]{3,0,2,1:T(8,128)} %get-tuple-element.94), channel_id=1, source_target_pairs={{1,2},{2,1},{5,6},{6,5},{9,10},{10,9},{13,14},{14,13},{17,18},{18,... | collective-permute-start | bytes 221192 | tf_op jit(solution)/shard_map/ppermute | solution.py:21
  8.7 9.6 %collective-permute-start.2 = (f32[18,1,32,128]{3,0,2,1:T(8,128)}, f32[18,1,32,128]{3,0,2,1:T(8,128)}, u32[]{:S(2)}, u32[]{:S(2)}) collective-permute-start(f32[18,1,32,128]{3,0,2,1:T(8,128)} %get-tuple-element.56), channel_id=1, source_target_pairs={{4,8},{8,4},{12,16},{16,12},{20,24},{24,20},{5,9},{9,5},{13,17},{1... | collective-permute-start | bytes 884744 | tf_op jit(solution)/shard_map/ppermute | solution.py:21
  10.1 22.0 %collective-permute-start.3 = (f32[18,1,32,128]{3,0,2,1:T(8,128)}, f32[18,1,32,128]{3,0,2,1:T(8,128)}, u32[]{:S(2)}, u32[]{:S(2)}) collective-permute-start(f32[18,1,32,128]{3,0,2,1:T(8,128)} %get-tuple-element.57), channel_id=1, source_target_pairs={{0,4},{4,0},{8,12},{12,8},{16,20},{20,16},{24,28},{28,24},{1,5},{5... | collective-permute-start | bytes 884744 | tf_op jit(solution)/shard_map/ppermute | solution.py:20
  41.3 9.7 %collective-permute-start.7 = (f32[8,8,1,128]{3,0,2,1:T(8,128)S(1)}, f32[8,8,1,128]{3,0,2,1:T(8,128)S(1)}, u32[]{:S(2)}, u32[]{:S(2)}) collective-permute-start(f32[8,8,1,128]{3,0,2,1:T(8,128)S(1)} %get-tuple-element.41), channel_id=1, source_target_pairs={{1,2},{2,1},{5,6},{6,5},{9,10},{10,9},{13,14},{14,13},{17,18},{18,... | collective-permute-start | bytes 98312 | tf_op jit(solution)/shard_map/ppermute | solution.py:21
  42.0 9.7 %collective-permute-start.18 = (f32[8,8,1,128]{3,0,2,1:T(8,128)S(1)}, f32[8,8,1,128]{3,0,2,1:T(8,128)S(1)}, u32[]{:S(2)}, u32[]{:S(2)}) collective-permute-start(f32[8,8,1,128]{3,0,2,1:T(8,128)S(1)} %get-tuple-element.52), channel_id=1, source_target_pairs={{0,1},{1,0},{2,3},{3,2},{4,5},{5,4},{6,7},{7,6},{8,9},{9,8},{10,11... | collective-permute-start | bytes 98312 | tf_op jit(solution)/shard_map/ppermute | solution.py:20
  44.3 11.7 %collective-permute-start.19 = (f32[8,8,1,128]{3,0,2,1:T(8,128)S(1)}, f32[8,8,1,128]{3,0,2,1:T(8,128)S(1)}, u32[]{:S(2)}, u32[]{:S(2)}) collective-permute-start(f32[8,8,1,128]{3,0,2,1:T(8,128)S(1)} %get-tuple-element.53), channel_id=1, source_target_pairs={{1,2},{2,1},{5,6},{6,5},{9,10},{10,9},{13,14},{14,13},{17,18},{18,... | collective-permute-start | bytes 98312 | tf_op jit(solution)/shard_map/ppermute | solution.py:21
  45.0 11.1 %collective-permute-start.5 = (f32[8,1,32,128]{3,0,2,1:T(8,128)S(1)}, f32[8,1,32,128]{3,0,2,1:T(8,128)S(1)}, u32[]{:S(2)}, u32[]{:S(2)}) collective-permute-start(f32[8,1,32,128]{3,0,2,1:T(8,128)S(1)} %get-tuple-element.38), channel_id=1, source_target_pairs={{4,8},{8,4},{12,16},{16,12},{20,24},{24,20},{5,9},{9,5},{13,17},{1... | collective-permute-start | bytes 393224 | tf_op jit(solution)/shard_map/ppermute | solution.py:21
  45.7 14.0 %collective-permute-start.4 = (f32[8,1,32,128]{3,0,2,1:T(8,128)S(1)}, f32[8,1,32,128]{3,0,2,1:T(8,128)S(1)}, u32[]{:S(2)}, u32[]{:S(2)}) collective-permute-start(f32[8,1,32,128]{3,0,2,1:T(8,128)S(1)} %get-tuple-element.39), channel_id=1, source_target_pairs={{0,4},{4,0},{8,12},{12,8},{16,20},{20,16},{24,28},{28,24},{1,5},{5... | collective-permute-start | bytes 393224 | tf_op jit(solution)/shard_map/ppermute | solution.py:20
  51.7 10.8 %collective-permute-start.16 = (f32[8,1,32,128]{3,0,2,1:T(8,128)S(1)}, f32[8,1,32,128]{3,0,2,1:T(8,128)S(1)}, u32[]{:S(2)}, u32[]{:S(2)}) collective-permute-start(f32[8,1,32,128]{3,0,2,1:T(8,128)S(1)} %get-tuple-element.51), channel_id=1, source_target_pairs={{0,4},{4,0},{8,12},{12,8},{16,20},{20,16},{24,28},{28,24},{1,5},{5... | collective-permute-start | bytes 393224 | tf_op jit(solution)/shard_map/ppermute | solution.py:20
  66.4 9.2 %collective-permute-start.22 = (f32[8,8,1,128]{3,0,2,1:T(8,128)S(1)}, f32[8,8,1,128]{3,0,2,1:T(8,128)S(1)}, u32[]{:S(2)}, u32[]{:S(2)}) collective-permute-start(f32[8,8,1,128]{3,0,2,1:T(8,128)S(1)} %get-tuple-element.48), channel_id=1, source_target_pairs={{0,1},{1,0},{2,3},{3,2},{4,5},{5,4},{6,7},{7,6},{8,9},{9,8},{10,11... | collective-permute-start | bytes 98312 | tf_op jit(solution)/shard_map/ppermute | solution.py:20
  68.1 11.9 %collective-permute-start.23 = (f32[8,8,1,128]{3,0,2,1:T(8,128)S(1)}, f32[8,8,1,128]{3,0,2,1:T(8,128)S(1)}, u32[]{:S(2)}, u32[]{:S(2)}) collective-permute-start(f32[8,8,1,128]{3,0,2,1:T(8,128)S(1)} %get-tuple-element.49), channel_id=1, source_target_pairs={{1,2},{2,1},{5,6},{6,5},{9,10},{10,9},{13,14},{14,13},{17,18},{18,... | collective-permute-start | bytes 98312 | tf_op jit(solution)/shard_map/ppermute | solution.py:21
  68.7 11.2 %collective-permute-start.9 = (f32[8,1,32,128]{3,0,2,1:T(8,128)S(1)}, f32[8,1,32,128]{3,0,2,1:T(8,128)S(1)}, u32[]{:S(2)}, u32[]{:S(2)}) collective-permute-start(f32[8,1,32,128]{3,0,2,1:T(8,128)S(1)} %get-tuple-element.34), channel_id=1, source_target_pairs={{4,8},{8,4},{12,16},{16,12},{20,24},{24,20},{5,9},{9,5},{13,17},{1... | collective-permute-start | bytes 393224 | tf_op jit(solution)/shard_map/ppermute | solution.py:21
  69.4 13.5 %collective-permute-start.8 = (f32[8,1,32,128]{3,0,2,1:T(8,128)S(1)}, f32[8,1,32,128]{3,0,2,1:T(8,128)S(1)}, u32[]{:S(2)}, u32[]{:S(2)}) collective-permute-start(f32[8,1,32,128]{3,0,2,1:T(8,128)S(1)} %get-tuple-element.35), channel_id=1, source_target_pairs={{0,4},{4,0},{8,12},{12,8},{16,20},{20,16},{24,28},{28,24},{1,5},{5... | collective-permute-start | bytes 393224 | tf_op jit(solution)/shard_map/ppermute | solution.py:20
  75.6 10.1 %collective-permute-start.20 = (f32[8,1,32,128]{3,0,2,1:T(8,128)S(1)}, f32[8,1,32,128]{3,0,2,1:T(8,128)S(1)}, u32[]{:S(2)}, u32[]{:S(2)}) collective-permute-start(f32[8,1,32,128]{3,0,2,1:T(8,128)S(1)} %get-tuple-element.47), channel_id=1, source_target_pairs={{0,4},{4,0},{8,12},{12,8},{16,20},{20,16},{24,28},{28,24},{1,5},{5... | collective-permute-start | bytes 393224 | tf_op jit(solution)/shard_map/ppermute | solution.py:20
  89.3 9.7 %collective-permute-start.15 = (f32[8,8,1,128]{3,0,2,1:T(8,128)S(1)}, f32[8,8,1,128]{3,0,2,1:T(8,128)S(1)}, u32[]{:S(2)}, u32[]{:S(2)}) collective-permute-start(f32[8,8,1,128]{3,0,2,1:T(8,128)S(1)} %get-tuple-element.33), channel_id=1, source_target_pairs={{1,2},{2,1},{5,6},{6,5},{9,10},{10,9},{13,14},{14,13},{17,18},{18,... | collective-permute-start | bytes 98312 | tf_op jit(solution)/shard_map/ppermute | solution.py:21
  90.0 9.7 %collective-permute-start.26 = (f32[8,8,1,128]{3,0,2,1:T(8,128)S(1)}, f32[8,8,1,128]{3,0,2,1:T(8,128)S(1)}, u32[]{:S(2)}, u32[]{:S(2)}) collective-permute-start(f32[8,8,1,128]{3,0,2,1:T(8,128)S(1)} %get-tuple-element.44), channel_id=1, source_target_pairs={{0,1},{1,0},{2,3},{3,2},{4,5},{5,4},{6,7},{7,6},{8,9},{9,8},{10,11... | collective-permute-start | bytes 98312 | tf_op jit(solution)/shard_map/ppermute | solution.py:20
  92.3 11.7 %collective-permute-start.27 = (f32[8,8,1,128]{3,0,2,1:T(8,128)S(1)}, f32[8,8,1,128]{3,0,2,1:T(8,128)S(1)}, u32[]{:S(2)}, u32[]{:S(2)}) collective-permute-start(f32[8,8,1,128]{3,0,2,1:T(8,128)S(1)} %get-tuple-element.45), channel_id=1, source_target_pairs={{1,2},{2,1},{5,6},{6,5},{9,10},{10,9},{13,14},{14,13},{17,18},{18,... | collective-permute-start | bytes 98312 | tf_op jit(solution)/shard_map/ppermute | solution.py:21
  93.0 11.1 %collective-permute-start.13 = (f32[8,1,32,128]{3,0,2,1:T(8,128)S(1)}, f32[8,1,32,128]{3,0,2,1:T(8,128)S(1)}, u32[]{:S(2)}, u32[]{:S(2)}) collective-permute-start(f32[8,1,32,128]{3,0,2,1:T(8,128)S(1)} %get-tuple-element.30), channel_id=1, source_target_pairs={{4,8},{8,4},{12,16},{16,12},{20,24},{24,20},{5,9},{9,5},{13,17},{1... | collective-permute-start | bytes 393224 | tf_op jit(solution)/shard_map/ppermute | solution.py:21
  93.7 14.0 %collective-permute-start.12 = (f32[8,1,32,128]{3,0,2,1:T(8,128)S(1)}, f32[8,1,32,128]{3,0,2,1:T(8,128)S(1)}, u32[]{:S(2)}, u32[]{:S(2)}) collective-permute-start(f32[8,1,32,128]{3,0,2,1:T(8,128)S(1)} %get-tuple-element.31), channel_id=1, source_target_pairs={{0,4},{4,0},{8,12},{12,8},{16,20},{20,16},{24,28},{28,24},{1,5},{5... | collective-permute-start | bytes 393224 | tf_op jit(solution)/shard_map/ppermute | solution.py:20
  99.7 10.8 %collective-permute-start.24 = (f32[8,1,32,128]{3,0,2,1:T(8,128)S(1)}, f32[8,1,32,128]{3,0,2,1:T(8,128)S(1)}, u32[]{:S(2)}, u32[]{:S(2)}) collective-permute-start(f32[8,1,32,128]{3,0,2,1:T(8,128)S(1)} %get-tuple-element.43), channel_id=1, source_target_pairs={{0,4},{4,0},{8,12},{12,8},{16,20},{20,16},{24,28},{28,24},{1,5},{5... | collective-permute-start | bytes 393224 | tf_op jit(solution)/shard_map/ppermute | solution.py:20
  128.4 11.2 %collective-permute-start.32 = (f32[16,16]{0,1:T(8,128)S(1)}, f32[16,16]{0,1:T(8,128)S(1)}, u32[]{:S(2)}, u32[]{:S(2)}) collective-permute-start(f32[16,16]{0,1:T(8,128)S(1)} %add.238), channel_id=1, source_target_pairs={{0,16},{4,20},{8,24},{12,28},{16,0},{20,4},{24,8},{28,12},{1,17},{... | collective-permute-start | bytes 3080 | tf_op jit(solution)/shard_map/ppermute | solution.py:80
  132.2 9.0 %collective-permute-start.36 = (f32[16,8,1,128]{3,0,2,1:T(8,128)}, f32[16,8,1,128]{3,0,2,1:T(8,128)}, u32[]{:S(2)}, u32[]{:S(2)}) collective-permute-start(f32[16,8,1,128]{3,0,2,1:T(8,128)} %broadcast_select_fusion.22), channel_id=1, source_target_pairs={{1,2},{2,1},{5,6},{6,5},{9,10},{10,9},{13,14},{14,13},{17,18},{18,... | collective-permute-start | bytes 196616 | tf_op jit(solution)/shard_map/ppermute | solution.py:21
  135.3 15.2 %collective-permute-start.33 = (f32[16,1,32,128]{3,0,2,1:T(8,128)S(1)}, f32[16,1,32,128]{3,0,2,1:T(8,128)S(1)}, u32[]{:S(2)}, u32[]{:S(2)}) collective-permute-start(f32[16,1,32,128]{3,0,2,1:T(8,128)S(1)} %get-tuple-element.20), channel_id=1, source_target_pairs={{0,4},{4,0},{8,12},{12,8},{16,20},{20,16},{24,28},{28,24},{1,5},{5... | collective-permute-start | bytes 786440 | tf_op jit(solution)/shard_map/ppermute | solution.py:20
  (24 other events, 117.1 us)

commit v9 on v6

--- a/solution.py
+++ b/solution.py
@@ -70,7 +70,7 @@
 
 
 def reduce_all(value):
-    for axis in ("gy", "gx"):
+    for axis in ("gx", "gy"):
         count = lax.axis_size(axis)
         assert count & (count - 1) == 0
         step = 1

time: 149 us -> 152 us (1.020)
  starting transfers between devices: 38.7 us -> 42.4 us
    ppermute x10, starting transfers between devices: 12.9 us -> 16.6 us  [reduce_all(): value = value + lax.ppermute(value, axis, pairs)]
    ppermute x10, waiting for transfers between devices: 10.5 us -> 7.29 us  [reduce_all(): value = value + lax.ppermute(value, axis, pairs)]
    ppermute x10, waiting for transfers between devices: 40 us -> 42.6 us  [swap_halos(): got_first = lax.ppermute(jnp.where(even, to_high, to_low), axis, first)]
  transfers between devices with their start and end apart: 30 -> 30, of which waited for: 12 -> 10; matrix products, arithmetic and copies ran while one was open for 12% -> 12% of each run, Pallas kernels for 0% -> 0%
where the time goes in v9:
time: 152 us; the launch traced here: 151 us
  waiting for transfers between devices  49.9 us (33%)
  starting transfers between devices  42.4 us (28%)
  other arithmetic  33.9 us (22%)
  matrix products  16.5 us (11%)
  local copies, waits for them, and re-layouts  6.88 us (5%)
    ppermute x10, waiting for transfers between devices, swap_halos(): got_first = lax.ppermute(jnp.where(even, to_high, to_low), axis, first)  42.6 us
    ppermute x10, starting transfers between devices, swap_halos(): got_first = lax.ppermute(jnp.where(even, to_high, to_low), axis, first)  17.6 us
    ppermute x10, starting transfers between devices, reduce_all(): value = value + lax.ppermute(value, axis, pairs)  16.6 us
    ppermute x10, starting transfers between devices, swap_halos(): got_second = lax.ppermute(jnp.where(even, to_low, to_high), axis, second)  8.16 us
    dot_general x2, matrix products, inner_products(): return jnp.einsum('kc,lc->kl', left, right, precision=lax.Precision.HIGHEST)  8.14 us
    dot_general x3, matrix products, combine(): jnp.einsum('kl,lc->kc', matrix, rows, precision=lax.Precision.HIGHEST)  7.88 us
    ppermute x10, waiting for transfers between devices, reduce_all(): value = value + lax.ppermute(value, axis, pairs)  7.29 us
    mul x5, other arithmetic, stencil(): flow_z = face_z * (centre[..., 1:] - centre[..., :-1])  5.73 us
  transfers between devices with their start and end apart: 30, of which 10 were waited for; matrix products, arithmetic and copies ran while one was open for 12% of the time, Pallas kernels for 0%

profile of v9, /device:TPU:0, one launch (start us, length us, event | category | flops | bytes accessed | tf_op | source)
XLA Modules:
  0.0 151.1 jit_solution(16279237585052329310)
XLA Ops:
  1.6 2.0 %broadcast_multiply_fusion.4 = f32[16,8,32,128]{3,2,1,0:T(8,128)S(1)} fusion(f32[16,8,32,128]{3,2,1,0:T(8,128)} %param.6, f32[8,32,128]{2,1,0:T(8,128)S(1)} %get-tuple-element.67), kind=kLoop, calls=%fused_computation.135 | loop fusion | flops 524288 | bytes 4325376 | tf_op jit(solution)/shard_map/mul | solution.py:109
  6.0 3.7 %collective-permute-start.1 = (f32[18,8,1,128]{3,2,1,0:T(1,128)S(1)}, f32[18,8,1,128]{3,2,1,0:T(1,128)}, u32[]{:S(2)}, u32[]{:S(2)}) collective-permute-start(f32[18,8,1,128]{3,2,1,0:T(1,128)S(1)} %get-tuple-element.10), channel_id=1, source_target_pairs={{0,1},{1,0},{2,3},{3,2},{4,5},{5,4},{6,7},{7,6},{8,9},{9,8},{10,11... | collective-permute-start | bytes 221192 | tf_op jit(solution)/shard_map/ppermute | solution.py:19
  10.5 4.3 %collective-permute-start.3 = (f32[18,1,32,128]{3,2,1,0:T(8,128)S(1)}, f32[18,1,32,128]{3,2,1,0:T(8,128)S(1)}, u32[]{:S(2)}, u32[]{:S(2)}) collective-permute-start(f32[18,1,32,128]{3,2,1,0:T(8,128)S(1)} %get-tuple-element.40), channel_id=1, source_target_pairs={{0,4},{4,0},{8,12},{12,8},{16,20},{20,16},{24,28},{28,24},{1,5},{5... | collective-permute-start | bytes 884744 | tf_op jit(solution)/shard_map/ppermute | solution.py:19
  17.1 9.8 %collective-permute-done.3 = f32[18,1,32,128]{3,2,1,0:T(8,128)S(1)} collective-permute-done((f32[18,1,32,128]{3,2,1,0:T(8,128)S(1)}, f32[18,1,32,128]{3,2,1,0:T(8,128)S(1)}, u32[]{:S(2)}, u32[]{:S(2)}) %collective-permute-start.3) | collective-permute-done | bytes 294944 | tf_op jit(solution)/shard_map/ppermute | solution.py:19
  27.5 1.9 %fusion.58 = f32[16,8,32,127]{3,2,1,0:T(8,128)} fusion(f32[16,8,32,128]{3,2,1,0:T(8,128)S(1)} %broadcast_multiply_fusion.4, f32[8,32,127]{2,1,0:T(8,128)S(1)} %slice_multiply_fusion.4), kind=kLoop, calls=%fused_computation.109 | loop fusion | flops 1040384 | bytes 6372352 | tf_op jit(solution)/shard_map/mul | solution.py:59
  31.4 3.7 %broadcast_multiply_fusion.3 = (f32[16,8,32,128]{3,2,1,0:T(8,128)S(1)}, f32[16,8,32,128]{3,2,1,0:T(8,128)S(1)}) fusion(f32[16,8,32,127]{3,2,1,0:T(8,128)} %fusion.58, f32[16,8,33,128]{3,2,1,0:T(8,128)S(1)} %fusion.18, f32[16,9,32,128]{3,2,1,0:T(8,128)S(1)} %fusion.20, f32[8,32,128]{2,1,0:T(8,128)S(1)} %get-tuple-element.51, f32[8,32,128]{2,1,0:T(8,128)S(1)} %slice.494, ...), kind=kLoop, calls=%fused_computation.134 | loop fusion | flops 6291456 | bytes 17154048 | tf_op jit(solution)/shard_map/div | solution.py:151
  35.3 2.5 %collective-permute-start.4 = (f32[16,1,32,128]{3,2,1,0:T(8,128)S(1)}, f32[16,1,32,128]{3,2,1,0:T(8,128)S(1)}, u32[]{:S(2)}, u32[]{:S(2)}) collective-permute-start(f32[16,1,32,128]{3,2,1,0:T(8,128)S(1)} %get-tuple-element.25), channel_id=1, source_target_pairs={{0,4},{4,0},{8,12},{12,8},{16,20},{20,16},{24,28},{28,24},{1,5},{5... | collective-permute-start | bytes 786440 | tf_op jit(solution)/shard_map/ppermute | solution.py:19
  39.9 9.3 %collective-permute-done.4 = f32[16,1,32,128]{3,2,1,0:T(8,128)S(1)} collective-permute-done((f32[16,1,32,128]{3,2,1,0:T(8,128)S(1)}, f32[16,1,32,128]{3,2,1,0:T(8,128)S(1)}, u32[]{:S(2)}, u32[]{:S(2)}) %collective-permute-start.4) | collective-permute-done | bytes 262176 | tf_op jit(solution)/shard_map/ppermute | solution.py:19
  52.5 2.5 %collective-permute-start.8 = (f32[16,1,32,128]{3,2,1,0:T(8,128)S(1)}, f32[16,1,32,128]{3,2,1,0:T(8,128)S(1)}, u32[]{:S(2)}, u32[]{:S(2)}) collective-permute-start(f32[16,1,32,128]{3,2,1,0:T(8,128)S(1)} %get-tuple-element.21), channel_id=1, source_target_pairs={{0,4},{4,0},{8,12},{12,8},{16,20},{20,16},{24,28},{28,24},{1,5},{5... | collective-permute-start | bytes 786440 | tf_op jit(solution)/shard_map/ppermute | solution.py:19
  57.1 8.4 %collective-permute-done.8 = f32[16,1,32,128]{3,2,1,0:T(8,128)S(1)} collective-permute-done((f32[16,1,32,128]{3,2,1,0:T(8,128)S(1)}, f32[16,1,32,128]{3,2,1,0:T(8,128)S(1)}, u32[]{:S(2)}, u32[]{:S(2)}) %collective-permute-start.8) | collective-permute-done | bytes 262176 | tf_op jit(solution)/shard_map/ppermute | solution.py:19
  68.3 2.5 %collective-permute-start.12 = (f32[16,1,32,128]{3,2,1,0:T(8,128)S(1)}, f32[16,1,32,128]{3,2,1,0:T(8,128)S(1)}, u32[]{:S(2)}, u32[]{:S(2)}) collective-permute-start(f32[16,1,32,128]{3,2,1,0:T(8,128)S(1)} %get-tuple-element.17), channel_id=1, source_target_pairs={{0,4},{4,0},{8,12},{12,8},{16,20},{20,16},{24,28},{28,24},{1,5},{5... | collective-permute-start | bytes 786440 | tf_op jit(solution)/shard_map/ppermute | solution.py:19
  73.1 7.5 %collective-permute-done.12 = f32[16,1,32,128]{3,2,1,0:T(8,128)S(1)} collective-permute-done((f32[16,1,32,128]{3,2,1,0:T(8,128)S(1)}, f32[16,1,32,128]{3,2,1,0:T(8,128)S(1)}, u32[]{:S(2)}, u32[]{:S(2)}) %collective-permute-start.12) | collective-permute-done | bytes 262176 | tf_op jit(solution)/shard_map/ppermute | solution.py:19
  81.9 2.7 %broadcast_multiply_fusion = (f32[16,8,32,128]{3,2,1,0:T(8,128)S(1)}, f32[16,8,32,128]{3,2,1,0:T(8,128)}) fusion(f32[16,8,32,128]{3,2,1,0:T(8,128)S(1)} %get-tuple-element.7, f32[16,8,32,128]{3,2,1,0:T(8,128)S(1)} %get-tuple-element.5, f32[16,8,32,127]{3,2,1,0:T(8,128)S(1)} %fusion.36, f32[16,8,33,128]{3,2,1,0:T(8,128)S(1)} %fusion.6, ...), kind=kLoop, calls=%fused_computation.131 | loop fusion | flops 7340032 | bytes 19120128 | tf_op jit(solution)/shard_map/div | solution.py:152
  84.7 3.6 %fusion.74 = f32[16,16]{0,1:T(8,128)S(1)} fusion(f32[16,8,32,128]{3,2,1,0:T(8,128)S(1)} %get-tuple-element.2), kind=kOutput, calls=%fused_computation.129 | convolution fusion | flops 100663296 | bytes 2098176 | tf_op jit(solution)/shard_map/kc,lc->kl/dot_general | solution.py:85
  88.3 2.5 %collective-permute-start.16 = (f32[16,16]{0,1:T(8,128)S(1)}, f32[16,16]{0,1:T(8,128)S(1)}, u32[]{:S(2)}, u32[]{:S(2)}) collective-permute-start(f32[16,16]{0,1:T(8,128)S(1)} %fusion.74), channel_id=1, source_target_pairs={{0,4},{4,0},{8,12},{12,8},{16,20},{20,16},{24,28},{28,24},{1,5},{5... | collective-permute-start | bytes 3080 | tf_op jit(solution)/shard_map/ppermute | solution.py:79
  96.1 2.8 %collective-permute-start.18 = (f32[16,16]{0,1:T(8,128)S(1)}, f32[16,16]{0,1:T(8,128)S(1)}, u32[]{:S(2)}, u32[]{:S(2)}) collective-permute-start(f32[16,16]{0,1:T(8,128)S(1)} %add.170), channel_id=1, source_target_pairs={{0,16},{4,20},{8,24},{12,28},{16,0},{20,4},{24,8},{28,12},{1,17},{... | collective-permute-start | bytes 3080 | tf_op jit(solution)/shard_map/ppermute | solution.py:79
  98.9 1.9 %fusion.31 = f32[16,8,32,127]{3,2,1,0:T(8,128)} fusion(f32[16,8,32,128]{3,2,1,0:T(8,128)S(1)} %get-tuple-element.2, f32[8,32,127]{2,1,0:T(8,128)S(1)} %slice_multiply_fusion.4), kind=kLoop, calls=%fused_computation.70 | loop fusion | flops 1040384 | bytes 6372352 | tf_op jit(solution)/shard_map/mul | solution.py:59
  107.9 7.6 %collective-permute-done.21 = f32[16,1,32,128]{3,2,1,0:T(8,128)} collective-permute-done((f32[16,1,32,128]{3,2,1,0:T(8,128)S(1)}, f32[16,1,32,128]{3,2,1,0:T(8,128)}, u32[]{:S(2)}, u32[]{:S(2)}) %collective-permute-start.21) | collective-permute-done | bytes 262176 | tf_op jit(solution)/shard_map/ppermute | solution.py:19
  120.4 4.5 %fusion.77 = f32[16,16]{0,1:T(8,128)S(1)} fusion(f32[16,8,32,128]{3,2,1,0:T(8,128)S(1)} %fusion.34, f32[16,8,32,128]{3,2,1,0:T(8,128)S(1)} %get-tuple-element.2), kind=kOutput, calls=%fused_computation.130 | convolution fusion | flops 100663296 | bytes 4195328 | tf_op jit(solution)/shard_map/kc,lc->kl/dot_general | solution.py:85
  125.0 2.6 %collective-permute-start.25 = (f32[16,16]{0,1:T(8,128)S(1)}, f32[16,16]{0,1:T(8,128)S(1)}, u32[]{:S(2)}, u32[]{:S(2)}) collective-permute-start(f32[16,16]{0,1:T(8,128)S(1)} %fusion.77), channel_id=1, source_target_pairs={{0,4},{4,0},{8,12},{12,8},{16,20},{20,16},{24,28},{28,24},{1,5},{5... | collective-permute-start | bytes 3080 | tf_op jit(solution)/shard_map/ppermute | solution.py:79
  129.3 2.1 %collective-permute-start.26 = (f32[16,16]{0,1:T(8,128)S(1)}, f32[16,16]{0,1:T(8,128)S(1)}, u32[]{:S(2)}, u32[]{:S(2)}) collective-permute-start(f32[16,16]{0,1:T(8,128)S(1)} %add.178), channel_id=1, source_target_pairs={{0,8},{4,12},{8,0},{12,4},{16,24},{20,28},{24,16},{28,20},{1,9},{5... | collective-permute-start | bytes 3080 | tf_op jit(solution)/shard_map/ppermute | solution.py:79
  133.2 2.7 %collective-permute-start.27 = (f32[16,16]{0,1:T(8,128)S(1)}, f32[16,16]{0,1:T(8,128)S(1)}, u32[]{:S(2)}, u32[]{:S(2)}) collective-permute-start(f32[16,16]{0,1:T(8,128)S(1)} %add.179), channel_id=1, source_target_pairs={{0,16},{4,20},{8,24},{12,28},{16,0},{20,4},{24,8},{28,12},{1,17},{... | collective-permute-start | bytes 3080 | tf_op jit(solution)/shard_map/ppermute | solution.py:79
  137.8 2.8 %fusion.28 = f32[16,32768]{1,0:T(8,128)S(1)} fusion(f32[16,16]{1,0:T(8,128)S(1)} %fusion.87, f32[2,8,256,128]{3,2,1,0:T(8,128)S(1)} %bitcast.83), kind=kOutput, calls=%fused_computation.66 | convolution fusion | flops 100663296 | bytes 4195328 | tf_op jit(solution)/shard_map/kl,lc->kc/dot_general | solution.py:89
  144.0 3.1 %fusion.25 = f32[16,32768]{1,0:T(8,128)S(1)} fusion(f32[16,16]{1,0:T(8,128)S(1)} %fusion.87, f32[2,8,256,128]{3,2,1,0:T(8,128)S(1)} %bitcast.84), kind=kOutput, calls=%fused_computation.63 | convolution fusion | flops 100663296 | bytes 4195328 | tf_op jit(solution)/shard_map/kl,lc->kc/dot_general | solution.py:89
  (153 shorter events, 52.1 us)
Async XLA Ops:
  4.7 11.4 %collective-permute-start = (f32[18,8,1,128]{3,2,1,0:T(1,128)}, f32[18,8,1,128]{3,2,1,0:T(1,128)}, u32[]{:S(2)}, u32[]{:S(2)}) collective-permute-start(f32[18,8,1,128]{3,2,1,0:T(1,128)} %broadcast_select_fusion.5), channel_id=1, source_target_pairs={{1,2},{2,1},{5,6},{6,5},{9,10},{10,9},{13,14},{14,13},{17,18},{18,... | collective-permute-start | bytes 221192 | tf_op jit(solution)/shard_map/ppermute | solution.py:20
  6.0 10.1 %collective-permute-start.1 = (f32[18,8,1,128]{3,2,1,0:T(1,128)S(1)}, f32[18,8,1,128]{3,2,1,0:T(1,128)}, u32[]{:S(2)}, u32[]{:S(2)}) collective-permute-start(f32[18,8,1,128]{3,2,1,0:T(1,128)S(1)} %get-tuple-element.10), channel_id=1, source_target_pairs={{0,1},{1,0},{2,3},{3,2},{4,5},{5,4},{6,7},{7,6},{8,9},{9,8},{10,11... | collective-permute-start | bytes 221192 | tf_op jit(solution)/shard_map/ppermute | solution.py:19
  9.8 7.3 %collective-permute-start.2 = (f32[18,1,32,128]{3,2,1,0:T(8,128)S(1)}, f32[18,1,32,128]{3,2,1,0:T(8,128)S(1)}, u32[]{:S(2)}, u32[]{:S(2)}) collective-permute-start(f32[18,1,32,128]{3,2,1,0:T(8,128)S(1)} %get-tuple-element.39), channel_id=1, source_target_pairs={{4,8},{8,4},{12,16},{16,12},{20,24},{24,20},{5,9},{9,5},{13,17},{1... | collective-permute-start | bytes 884744 | tf_op jit(solution)/shard_map/ppermute | solution.py:20
  10.5 16.4 %collective-permute-start.3 = (f32[18,1,32,128]{3,2,1,0:T(8,128)S(1)}, f32[18,1,32,128]{3,2,1,0:T(8,128)S(1)}, u32[]{:S(2)}, u32[]{:S(2)}) collective-permute-start(f32[18,1,32,128]{3,2,1,0:T(8,128)S(1)} %get-tuple-element.40), channel_id=1, source_target_pairs={{0,4},{4,0},{8,12},{12,8},{16,20},{20,16},{24,28},{28,24},{1,5},{5... | collective-permute-start | bytes 884744 | tf_op jit(solution)/shard_map/ppermute | solution.py:19
  35.3 13.9 %collective-permute-start.4 = (f32[16,1,32,128]{3,2,1,0:T(8,128)S(1)}, f32[16,1,32,128]{3,2,1,0:T(8,128)S(1)}, u32[]{:S(2)}, u32[]{:S(2)}) collective-permute-start(f32[16,1,32,128]{3,2,1,0:T(8,128)S(1)} %get-tuple-element.25), channel_id=1, source_target_pairs={{0,4},{4,0},{8,12},{12,8},{16,20},{20,16},{24,28},{28,24},{1,5},{5... | collective-permute-start | bytes 786440 | tf_op jit(solution)/shard_map/ppermute | solution.py:19
  37.8 11.4 %collective-permute-start.5 = (f32[16,1,32,128]{3,2,1,0:T(8,128)S(1)}, f32[16,1,32,128]{3,2,1,0:T(8,128)S(1)}, u32[]{:S(2)}, u32[]{:S(2)}) collective-permute-start(f32[16,1,32,128]{3,2,1,0:T(8,128)S(1)} %get-tuple-element.24), channel_id=1, source_target_pairs={{4,8},{8,4},{12,16},{16,12},{20,24},{24,20},{5,9},{9,5},{13,17},{1... | collective-permute-start | bytes 786440 | tf_op jit(solution)/shard_map/ppermute | solution.py:20
  52.5 13.1 %collective-permute-start.8 = (f32[16,1,32,128]{3,2,1,0:T(8,128)S(1)}, f32[16,1,32,128]{3,2,1,0:T(8,128)S(1)}, u32[]{:S(2)}, u32[]{:S(2)}) collective-permute-start(f32[16,1,32,128]{3,2,1,0:T(8,128)S(1)} %get-tuple-element.21), channel_id=1, source_target_pairs={{0,4},{4,0},{8,12},{12,8},{16,20},{20,16},{24,28},{28,24},{1,5},{5... | collective-permute-start | bytes 786440 | tf_op jit(solution)/shard_map/ppermute | solution.py:19
  55.0 10.5 %collective-permute-start.9 = (f32[16,1,32,128]{3,2,1,0:T(8,128)S(1)}, f32[16,1,32,128]{3,2,1,0:T(8,128)S(1)}, u32[]{:S(2)}, u32[]{:S(2)}) collective-permute-start(f32[16,1,32,128]{3,2,1,0:T(8,128)S(1)} %get-tuple-element.20), channel_id=1, source_target_pairs={{4,8},{8,4},{12,16},{16,12},{20,24},{24,20},{5,9},{9,5},{13,17},{1... | collective-permute-start | bytes 786440 | tf_op jit(solution)/shard_map/ppermute | solution.py:20
  68.3 12.3 %collective-permute-start.12 = (f32[16,1,32,128]{3,2,1,0:T(8,128)S(1)}, f32[16,1,32,128]{3,2,1,0:T(8,128)S(1)}, u32[]{:S(2)}, u32[]{:S(2)}) collective-permute-start(f32[16,1,32,128]{3,2,1,0:T(8,128)S(1)} %get-tuple-element.17), channel_id=1, source_target_pairs={{0,4},{4,0},{8,12},{12,8},{16,20},{20,16},{24,28},{28,24},{1,5},{5... | collective-permute-start | bytes 786440 | tf_op jit(solution)/shard_map/ppermute | solution.py:19
  70.9 9.8 %collective-permute-start.13 = (f32[16,1,32,128]{3,2,1,0:T(8,128)S(1)}, f32[16,1,32,128]{3,2,1,0:T(8,128)S(1)}, u32[]{:S(2)}, u32[]{:S(2)}) collective-permute-start(f32[16,1,32,128]{3,2,1,0:T(8,128)S(1)} %get-tuple-element.16), channel_id=1, source_target_pairs={{4,8},{8,4},{12,16},{16,12},{20,24},{24,20},{5,9},{9,5},{13,17},{1... | collective-permute-start | bytes 786440 | tf_op jit(solution)/shard_map/ppermute | solution.py:20
  71.5 1.6 %collective-permute-start.14 = (f32[16,8,1,128]{3,2,1,0:T(1,128)S(1)}, f32[16,8,1,128]{3,2,1,0:T(1,128)S(1)}, u32[]{:S(2)}, u32[]{:S(2)}) collective-permute-start(f32[16,8,1,128]{3,2,1,0:T(1,128)S(1)} %get-tuple-element.18), channel_id=1, source_target_pairs={{0,1},{1,0},{2,3},{3,2},{4,5},{5,4},{6,7},{7,6},{8,9},{9,8},{10,11... | collective-permute-start | bytes 196616 | tf_op jit(solution)/shard_map/ppermute | solution.py:19
  88.3 4.1 %collective-permute-start.16 = (f32[16,16]{0,1:T(8,128)S(1)}, f32[16,16]{0,1:T(8,128)S(1)}, u32[]{:S(2)}, u32[]{:S(2)}) collective-permute-start(f32[16,16]{0,1:T(8,128)S(1)} %fusion.74), channel_id=1, source_target_pairs={{0,4},{4,0},{8,12},{12,8},{16,20},{20,16},{24,28},{28,24},{1,5},{5... | collective-permute-start | bytes 3080 | tf_op jit(solution)/shard_map/ppermute | solution.py:79
  92.4 3.7 %collective-permute-start.17 = (f32[16,16]{0,1:T(8,128)S(1)}, f32[16,16]{0,1:T(8,128)S(1)}, u32[]{:S(2)}, u32[]{:S(2)}) collective-permute-start(f32[16,16]{0,1:T(8,128)S(1)} %add.169), channel_id=1, source_target_pairs={{0,8},{4,12},{8,0},{12,4},{16,24},{20,28},{24,16},{28,20},{1,9},{5... | collective-permute-start | bytes 3080 | tf_op jit(solution)/shard_map/ppermute | solution.py:79
  96.1 4.8 %collective-permute-start.18 = (f32[16,16]{0,1:T(8,128)S(1)}, f32[16,16]{0,1:T(8,128)S(1)}, u32[]{:S(2)}, u32[]{:S(2)}) collective-permute-start(f32[16,16]{0,1:T(8,128)S(1)} %add.170), channel_id=1, source_target_pairs={{0,16},{4,20},{8,24},{12,28},{16,0},{20,4},{24,8},{28,12},{1,17},{... | collective-permute-start | bytes 3080 | tf_op jit(solution)/shard_map/ppermute | solution.py:79
  102.0 4.3 %collective-permute-start.20 = (f32[16,16]{0,1:T(8,128)S(1)}, f32[16,16]{0,1:T(8,128)S(1)}, u32[]{:S(2)}, u32[]{:S(2)}) collective-permute-start(f32[16,16]{0,1:T(8,128)S(1)} %add.172), channel_id=1, source_target_pairs={{0,2},{1,3},{2,0},{3,1},{4,6},{5,7},{6,4},{7,5},{8,10},{9,11},{10,... | collective-permute-start | bytes 3080 | tf_op jit(solution)/shard_map/ppermute | solution.py:79
  102.6 13.0 %collective-permute-start.21 = (f32[16,1,32,128]{3,2,1,0:T(8,128)S(1)}, f32[16,1,32,128]{3,2,1,0:T(8,128)}, u32[]{:S(2)}, u32[]{:S(2)}) collective-permute-start(f32[16,1,32,128]{3,2,1,0:T(8,128)S(1)} %get-tuple-element.13), channel_id=1, source_target_pairs={{0,4},{4,0},{8,12},{12,8},{16,20},{20,16},{24,28},{28,24},{1,5},{5... | collective-permute-start | bytes 786440 | tf_op jit(solution)/shard_map/ppermute | solution.py:19
  104.3 11.2 %collective-permute-start.22 = (f32[16,1,32,128]{3,2,1,0:T(8,128)S(1)}, f32[16,1,32,128]{3,2,1,0:T(8,128)}, u32[]{:S(2)}, u32[]{:S(2)}) collective-permute-start(f32[16,1,32,128]{3,2,1,0:T(8,128)S(1)} %get-tuple-element.12), channel_id=1, source_target_pairs={{4,8},{8,4},{12,16},{16,12},{20,24},{24,20},{5,9},{9,5},{13,17},{1... | collective-permute-start | bytes 786440 | tf_op jit(solution)/shard_map/ppermute | solution.py:20
  105.7 2.3 %collective-permute-start.23 = (f32[16,8,1,128]{3,2,1,0:T(1,128)S(1)}, f32[16,8,1,128]{3,2,1,0:T(1,128)S(1)}, u32[]{:S(2)}, u32[]{:S(2)}) collective-permute-start(f32[16,8,1,128]{3,2,1,0:T(1,128)S(1)} %get-tuple-element.14), channel_id=1, source_target_pairs={{0,1},{1,0},{2,3},{3,2},{4,5},{5,4},{6,7},{7,6},{8,9},{9,8},{10,11... | collective-permute-start | bytes 196616 | tf_op jit(solution)/shard_map/ppermute | solution.py:19
  105.7 2.3 %collective-permute-start.24 = (f32[16,8,1,128]{3,2,1,0:T(1,128)S(1)}, f32[16,8,1,128]{3,2,1,0:T(1,128)S(1)}, u32[]{:S(2)}, u32[]{:S(2)}) collective-permute-start(f32[16,8,1,128]{3,2,1,0:T(1,128)S(1)} %get-tuple-element.15), channel_id=1, source_target_pairs={{1,2},{2,1},{5,6},{6,5},{9,10},{10,9},{13,14},{14,13},{17,18},{18,... | collective-permute-start | bytes 196616 | tf_op jit(solution)/shard_map/ppermute | solution.py:20
  125.0 4.3 %collective-permute-start.25 = (f32[16,16]{0,1:T(8,128)S(1)}, f32[16,16]{0,1:T(8,128)S(1)}, u32[]{:S(2)}, u32[]{:S(2)}) collective-permute-start(f32[16,16]{0,1:T(8,128)S(1)} %fusion.77), channel_id=1, source_target_pairs={{0,4},{4,0},{8,12},{12,8},{16,20},{20,16},{24,28},{28,24},{1,5},{5... | collective-permute-start | bytes 3080 | tf_op jit(solution)/shard_map/ppermute | solution.py:79
  129.3 3.9 %collective-permute-start.26 = (f32[16,16]{0,1:T(8,128)S(1)}, f32[16,16]{0,1:T(8,128)S(1)}, u32[]{:S(2)}, u32[]{:S(2)}) collective-permute-start(f32[16,16]{0,1:T(8,128)S(1)} %add.178), channel_id=1, source_target_pairs={{0,8},{4,12},{8,0},{12,4},{16,24},{20,28},{24,16},{28,20},{1,9},{5... | collective-permute-start | bytes 3080 | tf_op jit(solution)/shard_map/ppermute | solution.py:79
  133.2 4.6 %collective-permute-start.27 = (f32[16,16]{0,1:T(8,128)S(1)}, f32[16,16]{0,1:T(8,128)S(1)}, u32[]{:S(2)}, u32[]{:S(2)}) collective-permute-start(f32[16,16]{0,1:T(8,128)S(1)} %add.179), channel_id=1, source_target_pairs={{0,16},{4,20},{8,24},{12,28},{16,0},{20,4},{24,8},{28,12},{1,17},{... | collective-permute-start | bytes 3080 | tf_op jit(solution)/shard_map/ppermute | solution.py:79
  137.8 4.6 %collective-permute-start.28 = (f32[16,16]{0,1:T(8,128)S(1)}, f32[16,16]{0,1:T(8,128)S(1)}, u32[]{:S(2)}, u32[]{:S(2)}) collective-permute-start(f32[16,16]{0,1:T(8,128)S(1)} %add.180), channel_id=1, source_target_pairs={{0,1},{1,0},{2,3},{3,2},{4,5},{5,4},{6,7},{7,6},{8,9},{9,8},{10,11... | collective-permute-start | bytes 3080 | tf_op jit(solution)/shard_map/ppermute | solution.py:79
  142.4 4.7 %collective-permute-start.29 = (f32[16,16]{0,1:T(8,128)S(1)}, f32[16,16]{0,1:T(8,128)S(1)}, u32[]{:S(2)}, u32[]{:S(2)}) collective-permute-start(f32[16,16]{0,1:T(8,128)S(1)} %add.181), channel_id=1, source_target_pairs={{0,2},{1,3},{2,0},{3,1},{4,6},{5,7},{6,4},{7,5},{8,10},{9,11},{10,... | collective-permute-start | bytes 3080 | tf_op jit(solution)/shard_map/ppermute | solution.py:79
  (15 other events, 54.2 us)
